TPU v7x, 128 devices: a whole 4x4x4 slice. The times are simulated.
128 devices in a mesh: aux: 4 (over x), row: 32 (over z, y, core).
Axes of the slice: x: 4, y: 4, z: 4, core: 2. Of those that a mesh axis runs over, the one named last changes fastest.
Arguments:
- b_tiles: bfloat16 [4, 32768, 2048], P('aux', 'row'), may hold values from -0.125 to 0.125
- occ_coeff: bfloat16 [32768, 256], P('row'), may hold values from -3 to 3
- tile_blocks: int32 [256, 16], P('row'), may hold values from 0 to 255, as said below
- screen_mask: int32 [256, 16], P('row'), may hold values from 0 to 1, as said below
Outputs:
- exchange: bfloat16 [32768, 32, 4, 256], P('row', None, 'aux')
Inputs may be any that keep to these rules, and one draw needn't show every extreme that they name: `tile_blocks`: each entry names a basis block at most 8 blocks away from its own row's block; the first slot of every block names the block itself. `screen_mask`: in every basis block the kept slots come first; some block keeps all 16.
All inputs are finite; a program needn't handle non-finite values.
Results may differ from a plain program's by a relative error of at most 0.0057.
Values may be sent and summed in bfloat16 or wider, within the bound.
No kernel may reach another device: no remote copies, remote signals or barrier semaphores. Data moves between devices by JAX's collectives and lax.ppermute only.
A program may use at most 128 MiB of HBM per device.

v0:
```python
import jax
import jax.numpy as jnp
from jax import lax
from jax.sharding import PartitionSpec as P


def with_halo(block, sides, width):
    for axis, dim in sides:
        count = lax.axis_size(axis)
        forward = [(i, i + 1) for i in range(count - 1)]
        backward = [(target, source) for source, target in forward]
        low = lax.ppermute(
            lax.slice_in_dim(block, block.shape[dim] - width, None, axis=dim), axis, forward
        )
        high = lax.ppermute(lax.slice_in_dim(block, 0, width, axis=dim), axis, backward)
        block = jnp.concatenate([low, block, high], axis=dim)
    return block


def per_device(b_tiles, occ_coeff, tile_blocks, screen_mask):
    p_local, rows_local, stored = b_tiles.shape
    blocks_local, slot_count = tile_blocks.shape
    block_size = rows_local // blocks_local
    orbitals = occ_coeff.shape[1]
    row_count = lax.axis_size("row")
    aux_count = lax.axis_size("aux")
    extended = with_halo(occ_coeff, (("row", 0),), rows_local)
    coeff_blocks = extended.reshape(3 * blocks_local, block_size, orbitals)
    local_index = tile_blocks - (lax.axis_index("row") - 1) * blocks_local
    picked = jnp.take(coeff_blocks, local_index, axis=0)
    keep_mask = screen_mask.astype(jnp.bfloat16)
    tiles_five = b_tiles.reshape(p_local, blocks_local, block_size, slot_count, block_size)
    masked = picked * keep_mask[:, :, None, None]
    half_sum = jnp.einsum(
        "pbmsn,bsni->pbmi", tiles_five, masked, preferred_element_type=jnp.float32
    )
    half_local = half_sum.astype(jnp.bfloat16).reshape(p_local, rows_local, orbitals)
    slab_rows = lax.all_gather(half_local, "aux", axis=0, tiled=True)
    share = rows_local // aux_count
    all_rows = lax.all_gather(half_local, "row", axis=1, tiled=True)
    split_rows = all_rows.reshape(p_local, row_count, aux_count, share, orbitals)
    regrouped = lax.all_to_all(split_rows, "aux", split_axis=2, concat_axis=0, tiled=True)
    partner = regrouped.reshape(p_local * aux_count, row_count * share, orbitals)
    result = jnp.einsum("pmi,pli->ml", slab_rows, partner, preferred_element_type=jnp.float32)
    return result.astype(jnp.bfloat16).reshape(rows_local, row_count, 1, share)


def solution(mesh):
    in_specs = (P("aux", "row", None), P("row", None), P("row", None), P("row", None))
    out_specs = P("row", None, "aux", None)
    return jax.shard_map(
        per_device, mesh=mesh, in_specs=in_specs, out_specs=out_specs, check_vma=False
    )
```

profile of v0, /device:TPU:1, one launch (start us, length us, event | category | flops | bytes accessed | tf_op | source)
XLA Modules:
  0.0 382.9 jit_solution(15495398956538830125)
XLA Ops:
  7.4 0.0 copy-start
  7.4 0.0 copy-start.1
  7.4 0.0 all-gather.5.cloned.1.call-start
  7.4 4.7 %collective-permute-start = (bf16[1024,256]{1,0:T(8,128)(2,1)}, bf16[1024,256]{1,0:T(8,128)(2,1)S(1)}, u32[]{:S(2)}, u32[]{:S(2)}) collective-permute-start(bf16[1024,256]{1,0:T(8,128)(2,1)} %param.5), channel_id=1, source_target_pairs={{0,1},{1,2},{2,3},{3,4},{4,5},{5,6},{6,7},{7,8},{8,9},{9,10},{10,1... | collective-permute-start | bytes 1572872 | tf_op jit(solution)/shard_map/ppermute | solution.py:12
  12.1 1.9 collective-permute-start.1
  14.0 0.7 compare_and_fusion
  14.7 0.1 reshape.37
  14.8 5.6 %copy.12 = bf16[128,8,16,128]{3,2,1,0:T(8,128)(2,1)} copy(bf16[128,8,16,128]{3,1,2,0:T(8,128)(2,1)} %bitcast.36) | data formatting | bytes 8388608
  20.4 0.0 copy-done.1
  20.4 0.0 collective-permute-done
  20.4 2.4 collective-permute-done.1
  22.8 0.0 copy-done
  22.8 0.1 pad_maximum_fusion
  22.9 6.7 %gather_fusion = bf16[128,128,256]{2,1,0:T(8,128)(2,1)} fusion(bf16[24,128,256]{2,1,0:T(8,128)(2,1)S(1)} %bitcast.32, s32[1024]{0:T(1024)S(1)} %pad_clamp_fusion), kind=kCustom, calls=%fused_computation | custom fusion | bytes 16777728 | tf_op jit(solution)/shard_map/jit(_take)/gather | solution.py:30
  29.6 8.2 %fusion.12 = bf16[8,256,128]{1,2,0:T(8,128)(2,1)} fusion(bf16[8,16,128,256]{3,2,1,0:T(8,128)(2,1)} %bitcast.35, pred[8,16]{1,0:T(8,128)(4,1)S(1)} %get-tuple-element.5, bf16[8,16]{1,0:T(8,128)(2,1)S(1)} %convert_element_type.15, bf16[8,128,16,128]{3,2,1,0:T(8,128)(2,1)} %bitcast.37), kind=kOutput, calls=%fused_computation.11 | convolution fusion | flops 1094975488 | bytes 13107584 | tf_op jit(solution)/shard_map/pbmsn,bsni->pbmi/dot_general | solution.py:34
  37.8 0.0 all-gather.5.cloned.1.call-update
  37.8 76.5 %all-gather.5.cloned.1.call-done = bf16[1,32768,256]{2,1,0:T(8,128)(2,1)} async-done(((bf16[1,1024,256]{2,1,0:T(8,128)(2,1)}), bf16[1,32768,256]{2,1,0:T(8,128)(2,1)}) %all-gather.5.cloned.1.call-update) | async-done | bytes 16777232 | tf_op jit(solution)/shard_map/all_gather | solution.py:40
  114.4 14.0 %copy.9 = bf16[1,32,4,256,256]{4,3,1,0,2:T(8,128)(2,1)} copy(bf16[1,32,4,256,256]{4,3,2,1,0:T(8,128)(2,1)} %bitcast.33) | data formatting | bytes 33554432 | tf_op jit(solution)/shard_map/reshape | solution.py:41
  128.4 7.0 %all-to-all-start = ((bf16[1,32,4,256,256]{4,3,1,0,2:T(8,128)(2,1)}), bf16[1,32,4,256,256]{4,3,1,0,2:T(8,128)(2,1)}, u32[]{:S(2)}, u32[]{:S(2)}) async-start(bf16[1,32,4,256,256]{4,3,1,0,2:T(8,128)(2,1)} %copy.9), calls=%async_computation | async-start | bytes 33554432 | tf_op jit(solution)/shard_map/all_to_all | solution.py:42
  135.3 0.0 all-gather.3.cloned.1.call-start
  135.4 0.5 all-gather.3.cloned.1.call-update
  135.9 48.8 %all-gather.3.cloned.1.call-done = bf16[4,1024,256]{2,1,0:T(8,128)(2,1)} async-done(((bf16[1,1024,256]{2,1,0:T(8,128)(2,1)}), bf16[4,1024,256]{2,1,0:T(8,128)(2,1)}) %all-gather.3.cloned.1.call-update) | async-done | bytes 2097168 | tf_op jit(solution)/shard_map/all_gather | solution.py:38
  184.8 151.0 %all-to-all-done = bf16[1,32,4,256,256]{4,3,1,0,2:T(8,128)(2,1)} async-done(((bf16[1,32,4,256,256]{4,3,1,0,2:T(8,128)(2,1)}), bf16[1,32,4,256,256]{4,3,1,0,2:T(8,128)(2,1)}, u32[]{:S(2)}, u32[]{:S(2)}) %all-to-all-start) | async-done | bytes 16777248 | tf_op jit(solution)/shard_map/all_to_all | solution.py:42
  335.8 24.1 %bitcast_convert_fusion = bf16[1024,8192]{1,0:T(8,128)(2,1)} fusion(bf16[4,1024,256]{2,1,0:T(8,128)(2,1)} %all-gather.3.cloned.1.call-done, bf16[4,8192,256]{2,1,0:T(8,128)(2,1)} %bitcast.12), kind=kOutput, calls=%fused_computation.1 | convolution fusion | flops 17188257792 | bytes 35651584 | tf_op jit(solution)/shard_map/pmi,pli->ml/dot_general | solution.py:44
  359.9 15.6 %copy.13 = bf16[128,8,32,256]{3,2,1,0:T(8,128)(2,1)} copy(bf16[128,8,32,256]{3,1,2,0:T(8,128)(2,1)} %bitcast.34) | data formatting | bytes 33554432
  (2 shorter events, 0.0 us)
Async XLA Ops:
  7.4 15.4 %copy-start = (bf16[1024,256]{1,0:T(8,128)(2,1)S(1)}, bf16[1024,256]{1,0:T(8,128)(2,1)}, u32[]{:S(2)}) copy-start(bf16[1024,256]{1,0:T(8,128)(2,1)} %param.5) | copy-start | bytes 1572868
  7.4 13.0 %copy-start.1 = (s32[8,16]{1,0:T(8,128)S(1)}, s32[8,16]{1,0:T(8,128)}, u32[]{:S(2)}) copy-start(s32[8,16]{1,0:T(8,128)} %param.7) | copy-start | bytes 1540
  7.4 107.0 %all-gather.5.cloned.1.call-start = ((), (), s32[]{:S(2)}) async-start(), calls=%async_computation.2 | async-start | bytes 17301504 | tf_op jit(solution)/shard_map/all_gather | solution.py:40
  7.4 13.0 %collective-permute-start = (bf16[1024,256]{1,0:T(8,128)(2,1)}, bf16[1024,256]{1,0:T(8,128)(2,1)S(1)}, u32[]{:S(2)}, u32[]{:S(2)}) collective-permute-start(bf16[1024,256]{1,0:T(8,128)(2,1)} %param.5), channel_id=1, source_target_pairs={{0,1},{1,2},{2,3},{3,4},{4,5},{5,6},{6,7},{7,8},{8,9},{9,10},{10,1... | collective-permute-start | bytes 1572872 | tf_op jit(solution)/shard_map/ppermute | solution.py:12
  12.1 10.7 %collective-permute-start.1 = (bf16[1024,256]{1,0:T(8,128)(2,1)}, bf16[1024,256]{1,0:T(8,128)(2,1)S(1)}, u32[]{:S(2)}, u32[]{:S(2)}) collective-permute-start(bf16[1024,256]{1,0:T(8,128)(2,1)} %param.5), channel_id=1, source_target_pairs={{1,0},{2,1},{3,2},{4,3},{5,4},{6,5},{7,6},{8,7},{9,8},{10,9},{11,1... | collective-permute-start | bytes 1572872 | tf_op jit(solution)/shard_map/ppermute | solution.py:15
  128.4 207.4 %all-to-all-start = ((bf16[1,32,4,256,256]{4,3,1,0,2:T(8,128)(2,1)}), bf16[1,32,4,256,256]{4,3,1,0,2:T(8,128)(2,1)}, u32[]{:S(2)}, u32[]{:S(2)}) async-start(bf16[1,32,4,256,256]{4,3,1,0,2:T(8,128)(2,1)} %copy.9), calls=%async_computation | async-start | bytes 33554432 | tf_op jit(solution)/shard_map/all_to_all | solution.py:42
  135.3 49.4 %all-gather.3.cloned.1.call-start = ((), (), s32[]{:S(2)}) async-start(), calls=%async_computation.1 | async-start | bytes 2621440 | tf_op jit(solution)/shard_map/all_gather | solution.py:38
Sparse Core Ops, SparseCore 0:
  38.0 76.3 all-gather.4
Sparse Core Ops, SparseCore 1:
  137.5 47.2 all-gather.2
where the time goes:
time: 383 us
  waiting for transfers between devices  279 us (73%)
  local copies, waits for them, and re-layouts  42 us (11%)
  matrix products  32.2 us (8%)
  between operations  14.9 us (4%)
  starting transfers between devices  13.7 us (4%)
    all_to_all x1, waiting for transfers between devices, per_device(): lax.all_to_all(split_rows, 'aux', split_axis=2, concat_axis=0, tiled=True)  151 us
    all_gather x1, waiting for transfers between devices, per_device(): all_rows = lax.all_gather(half_local, 'row', axis=1, tiled=True)  76.5 us
    all_gather x1, waiting for transfers between devices, per_device(): slab_rows = lax.all_gather(half_local, 'aux', axis=0, tiled=True)  48.8 us
    dot_general x1, matrix products, per_device(): jnp.einsum('pmi,pli->ml', slab_rows, partner, preferred_element_type=jnp....  24.1 us
    unnamed x6, local copies, waits for them, and re-layouts  21.2 us
    reshape x1, local copies, waits for them, and re-layouts, per_device(): all_rows.reshape(p_local, row_count, aux_count, share, orbitals)  14 us
    dot_general x1, matrix products, per_device(): jnp.einsum('pbmsn,bsni->pbmi', tiles_five, masked, preferred_element_type...  8.17 us
  transfers between devices with their start and end apart: 5, of which 4 were waited for; matrix products, arithmetic and copies ran while one was open for 2% of the time, Pallas kernels for 0%

commit v1 on v0

v1 whole, which is shorter than its diff:
```python
import jax
import jax.numpy as jnp
from jax import lax
from jax.sharding import Mesh, PartitionSpec as P


def with_halo(block, sides, width):
    for axis, dim in sides:
        count = lax.axis_size(axis)
        forward = [(i, i + 1) for i in range(count - 1)]
        backward = [(target, source) for source, target in forward]
        low = lax.ppermute(
            lax.slice_in_dim(block, block.shape[dim] - width, None, axis=dim), axis, forward
        )
        high = lax.ppermute(lax.slice_in_dim(block, 0, width, axis=dim), axis, backward)
        block = jnp.concatenate([low, block, high], axis=dim)
    return block


ROW = ("rzy", "core")


def per_device(b_tiles, occ_coeff, tile_blocks, screen_mask):
    p_local, rows_local, stored = b_tiles.shape
    blocks_local, slot_count = tile_blocks.shape
    block_size = rows_local // blocks_local
    orbitals = occ_coeff.shape[1]
    aux_count = lax.axis_size("aux")
    row_index = lax.axis_index(ROW)
    extended = with_halo(occ_coeff, ((ROW, 0),), rows_local)
    coeff_blocks = extended.reshape(3 * blocks_local, block_size, orbitals)
    local_index = tile_blocks - (row_index - 1) * blocks_local
    picked = jnp.take(coeff_blocks, local_index, axis=0)
    keep_mask = screen_mask.astype(jnp.bfloat16)
    tiles_five = b_tiles.reshape(p_local, blocks_local, block_size, slot_count, block_size)
    masked = picked * keep_mask[:, :, None, None]
    half_sum = jnp.einsum(
        "pbmsn,bsni->pbmi", tiles_five, masked, preferred_element_type=jnp.float32
    )
    half_local = half_sum.astype(jnp.bfloat16).reshape(p_local, rows_local, orbitals)
    slab_rows = lax.all_gather(half_local, "aux", axis=0, tiled=True)
    share = rows_local // aux_count
    piece = lax.dynamic_slice_in_dim(slab_rows, lax.axis_index("aux") * share, share, axis=1)
    plane = lax.all_gather(piece, "rzy", axis=0)
    partner = lax.all_gather(plane, "core", axis=1)
    chips, cores = partner.shape[:2]
    partner = partner.reshape(chips * cores, *piece.shape)
    result = jnp.einsum("pmi,rpki->mrk", slab_rows, partner, preferred_element_type=jnp.float32)
    return result.astype(jnp.bfloat16).reshape(rows_local, chips * cores, 1, share)


def solution(mesh):
    aux_count, row_count = mesh.devices.shape
    devices = mesh.devices.reshape(aux_count, row_count // 2, 2)
    split_mesh = Mesh(devices, ("aux",) + ROW)
    in_specs = (P("aux", ROW, None), P(ROW, None), P(ROW, None), P(ROW, None))
    out_specs = P(ROW, None, "aux", None)
    return jax.shard_map(
        per_device, mesh=split_mesh, in_specs=in_specs, out_specs=out_specs, check_vma=False
    )
```

time: 383 us -> 228 us (0.60)
  waiting for transfers between devices: 279 us -> 142 us
  local copies, waits for them, and re-layouts: 42 us -> 32.3 us
  starting transfers between devices: 13.7 us -> 6.72 us
    all_to_all x1 -> x0, waiting for transfers between devices: 151 us -> none  [per_device(): lax.all_to_all(split_rows, 'aux', split_axis=2, concat_axis=0, tiled=True)]
    all_gather x1 -> x2, waiting for transfers between devices: 76.5 us -> 105 us  [the longest x1 71 us: per_device(): plane = lax.all_gather(piece, 'rzy', axis=0)]
    unnamed x6 -> x5, local copies, waits for them, and re-layouts: 21.2 us -> 5.56 us
    all_gather x1, waiting for transfers between devices: 48.8 us -> 34.2 us  [per_device(): slab_rows = lax.all_gather(half_local, 'aux', axis=0, tiled=True)]
    all_to_all x1 -> x0, starting transfers between devices: 6.99 us -> none  [per_device(): lax.all_to_all(split_rows, 'aux', split_axis=2, concat_axis=0, tiled=True)]
    reshape x1, local copies, waits for them, and re-layouts: 14 us -> 17.9 us  [per_device(): result.astype(jnp.bfloat16).reshape(rows_local, chips * cores, 1, share)]
  transfers between devices with their start and end apart: 5 -> 5, of which waited for: 4 -> 4; matrix products, arithmetic and copies ran while one was open for 2% -> 3% of each run, Pallas kernels for 0% -> 0%
where the time goes in v1:
time: 228 us; the launch traced here: 227 us
  waiting for transfers between devices  142 us (62%)
  local copies, waits for them, and re-layouts  32.3 us (14%)
  matrix products  32 us (14%)
  between operations  13.1 us (6%)
  starting transfers between devices  6.72 us (3%)
    all_gather x1, waiting for transfers between devices, per_device(): plane = lax.all_gather(piece, 'rzy', axis=0)  71 us
    all_gather x1, waiting for transfers between devices, per_device(): partner = lax.all_gather(plane, 'core', axis=1)  34.5 us
    all_gather x1, waiting for transfers between devices, per_device(): slab_rows = lax.all_gather(half_local, 'aux', axis=0, tiled=True)  34.2 us
    dot_general x1, matrix products, per_device(): jnp.einsum('pmi,rpki->mrk', slab_rows, partner, preferred_element_type=jn...  23.9 us
    reshape x1, local copies, waits for them, and re-layouts, per_device(): result.astype(jnp.bfloat16).reshape(rows_local, chips * cores, 1, share)  17.9 us
    dot_general x1, matrix products, per_device(): jnp.einsum('pbmsn,bsni->pbmi', tiles_five, masked, preferred_element_type...  8.14 us
    gather x1, local copies, waits for them, and re-layouts, per_device(): picked = jnp.take(coeff_blocks, local_index, axis=0)  6.75 us
    unnamed x5, local copies, waits for them, and re-layouts  5.56 us
  transfers between devices with their start and end apart: 5, of which 4 were waited for; matrix products, arithmetic and copies ran while one was open for 3% of the time, Pallas kernels for 0%

profile of v1, /device:TPU:1, one launch (start us, length us, event | category | flops | bytes accessed | tf_op | source)
XLA Modules:
  0.0 227.2 jit_solution(13417141563487165089)
XLA Ops:
  6.5 0.0 copy-start
  6.5 0.0 all-gather.6.cloned.1.call-start
  6.5 4.7 %collective-permute-start = (bf16[1024,256]{1,0:T(8,128)(2,1)}, bf16[1024,256]{1,0:T(8,128)(2,1)S(1)}, u32[]{:S(2)}, u32[]{:S(2)}) collective-permute-start(bf16[1024,256]{1,0:T(8,128)(2,1)} %param.5), channel_id=1, source_target_pairs={{0,1},{1,2},{2,3},{3,4},{4,5},{5,6},{6,7},{7,8},{8,9},{9,10},{10,1... | collective-permute-start | bytes 1572872 | tf_op jit(solution)/shard_map/ppermute | solution.py:12
  11.3 1.9 collective-permute-start.1
  13.2 0.7 convert_element_type.15
  13.9 0.7 compare_and_fusion
  14.6 0.1 reshape.32
  14.7 5.6 %copy.11 = bf16[128,8,16,128]{3,2,1,0:T(8,128)(2,1)} copy(bf16[128,8,16,128]{3,1,2,0:T(8,128)(2,1)} %bitcast.32) | data formatting | bytes 8388608
  20.2 0.0 collective-permute-done
  20.2 1.7 collective-permute-done.1
  22.0 0.0 copy-done
  22.0 0.1 pad_maximum_fusion
  22.1 6.7 %gather_fusion = bf16[128,128,256]{2,1,0:T(8,128)(2,1)} fusion(bf16[24,128,256]{2,1,0:T(8,128)(2,1)S(1)} %bitcast.29, s32[1024]{0:T(1024)S(1)} %pad_clamp_fusion), kind=kCustom, calls=%fused_computation | custom fusion | bytes 16777728 | tf_op jit(solution)/shard_map/jit(_take)/gather | solution.py:33
  28.8 8.1 %fusion.14 = bf16[8,256,128]{1,2,0:T(8,128)(2,1)} fusion(bf16[8,16,128,256]{3,2,1,0:T(8,128)(2,1)} %bitcast.30, pred[8,16]{1,0:T(8,128)(4,1)S(1)} %get-tuple-element.5, bf16[8,16]{1,0:T(8,128)(2,1)S(1)} %convert_element_type.15, bf16[8,128,16,128]{3,2,1,0:T(8,128)(2,1)} %bitcast.33), kind=kOutput, calls=%fused_computation.13 | convolution fusion | flops 1094975488 | bytes 13107584 | tf_op jit(solution)/shard_map/pbmsn,bsni->pbmi/dot_general | solution.py:37
  37.0 0.0 all-gather.6.cloned.1.call-update
  37.0 0.0 all-gather.8.cloned.1.call-start
  37.0 34.2 %all-gather.6.cloned.1.call-done = bf16[4,1024,256]{2,1,0:T(8,128)(2,1)} async-done(((bf16[1,1024,256]{2,1,0:T(8,128)(2,1)}), bf16[4,1024,256]{2,1,0:T(8,128)(2,1)}) %all-gather.6.cloned.1.call-update) | async-done | bytes 2097168 | tf_op jit(solution)/shard_map/all_gather | solution.py:41
  71.3 0.0 copy-start.1
  71.3 2.0 constant_dynamic-slice_fusion
  73.3 0.0 all-gather.8.cloned.1.call-update
  73.3 0.0 all-gather.10.cloned.1.call-start
  73.4 71.0 %all-gather.8.cloned.1.call-done = bf16[64,256,256]{2,1,0:T(8,128)(2,1)} async-done(((bf16[4,256,256]{2,1,0:T(8,128)(2,1)}), bf16[64,256,256]{2,1,0:T(8,128)(2,1)}) %all-gather.8.cloned.1.call-update) | async-done | bytes 8388624 | tf_op jit(solution)/shard_map/all_gather | solution.py:44
  144.4 0.0 all-gather.10.cloned.1.call-update
  144.4 34.5 %all-gather.10.cloned.1.call-done = bf16[16,8,256,256]{3,2,1,0:T(8,128)(2,1)} async-done(((bf16[16,4,256,256]{3,2,1,0:T(8,128)(2,1)}), bf16[16,8,256,256]{3,2,1,0:T(8,128)(2,1)}) %all-gather.10.cloned.1.call-update) | async-done | bytes 16777232 | tf_op jit(solution)/shard_map/all_gather | solution.py:45
  178.9 0.0 copy-done.1
  178.9 23.9 %fusion = bf16[1024,32,1,256]{3,0,1,2:T(8,128)(2,1)} fusion(bf16[32,4,256,256]{3,2,1,0:T(8,128)(2,1)} %bitcast.35, bf16[4,1024,256]{2,1,0:T(8,128)(2,1)S(1)} %copy-done.1), kind=kOutput, calls=%fused_computation.2 | convolution fusion | flops 17188257792 | bytes 35651584 | tf_op jit(solution)/shard_map/pmi,rpki->mrk/dot_general | solution.py:48
  202.8 17.9 %copy.8 = bf16[1024,32,1,256]{3,1,2,0:T(8,128)(2,1)} copy(bf16[1024,32,1,256]{3,0,1,2:T(8,128)(2,1)} %fusion) | data formatting | bytes 33554432 | tf_op jit(solution)/shard_map/reshape | solution.py:49
  (1 shorter events, 0.0 us)
Async XLA Ops:
  6.5 15.4 %copy-start = (bf16[1024,256]{1,0:T(8,128)(2,1)S(1)}, bf16[1024,256]{1,0:T(8,128)(2,1)}, u32[]{:S(2)}) copy-start(bf16[1024,256]{1,0:T(8,128)(2,1)} %param.5) | copy-start | bytes 1572868
  6.5 64.7 %all-gather.6.cloned.1.call-start = ((), (), s32[]{:S(2)}) async-start(), calls=%async_computation | async-start | bytes 2621440 | tf_op jit(solution)/shard_map/all_gather | solution.py:41
  6.5 13.7 %collective-permute-start = (bf16[1024,256]{1,0:T(8,128)(2,1)}, bf16[1024,256]{1,0:T(8,128)(2,1)S(1)}, u32[]{:S(2)}, u32[]{:S(2)}) collective-permute-start(bf16[1024,256]{1,0:T(8,128)(2,1)} %param.5), channel_id=1, source_target_pairs={{0,1},{1,2},{2,3},{3,4},{4,5},{5,6},{6,7},{7,8},{8,9},{9,10},{10,1... | collective-permute-start | bytes 1572872 | tf_op jit(solution)/shard_map/ppermute | solution.py:12
  11.3 10.7 %collective-permute-start.1 = (bf16[1024,256]{1,0:T(8,128)(2,1)}, bf16[1024,256]{1,0:T(8,128)(2,1)S(1)}, u32[]{:S(2)}, u32[]{:S(2)}) collective-permute-start(bf16[1024,256]{1,0:T(8,128)(2,1)} %param.5), channel_id=1, source_target_pairs={{1,0},{2,1},{3,2},{4,3},{5,4},{6,5},{7,6},{8,7},{9,8},{10,9},{11,1... | collective-permute-start | bytes 1572872 | tf_op jit(solution)/shard_map/ppermute | solution.py:15
  37.0 107.4 %all-gather.8.cloned.1.call-start = ((), (), s32[]{:S(2)}) async-start(), calls=%async_computation.1 | async-start | bytes 8912896 | tf_op jit(solution)/shard_map/all_gather | solution.py:44
  71.3 107.6 %copy-start.1 = (bf16[4,1024,256]{2,1,0:T(8,128)(2,1)S(1)}, bf16[4,1024,256]{2,1,0:T(8,128)(2,1)}, u32[]{:S(2)}) copy-start(bf16[4,1024,256]{2,1,0:T(8,128)(2,1)} %all-gather.6.cloned.1.call-done) | copy-start | bytes 6291460
  73.3 105.6 %all-gather.10.cloned.1.call-start = ((), (), s32[]{:S(2)}) async-start(), calls=%async_computation.2 | async-start | bytes 25165824 | tf_op jit(solution)/shard_map/all_gather | solution.py:45
Sparse Core Ops, SparseCore 0:
  37.1 34.1 all-gather.5
  73.5 70.8 all-gather.7
  146.1 32.7 all-gather.9

commit v2 on v1

--- a/solution.py
+++ b/solution.py
@@ -38,15 +38,18 @@
         "pbmsn,bsni->pbmi", tiles_five, masked, preferred_element_type=jnp.float32
     )
     half_local = half_sum.astype(jnp.bfloat16).reshape(p_local, rows_local, orbitals)
-    slab_rows = lax.all_gather(half_local, "aux", axis=0, tiled=True)
+    aux_index = lax.axis_index("aux")
+    shifted = [half_local[0]]
+    for shift in range(1, aux_count):
+        pairs = [(i, (i + shift) % aux_count) for i in range(aux_count)]
+        shifted.append(lax.ppermute(half_local[0], "aux", pairs))
+    slab_rows = jnp.stack(shifted)
     share = rows_local // aux_count
-    piece = lax.dynamic_slice_in_dim(slab_rows, lax.axis_index("aux") * share, share, axis=1)
-    plane = lax.all_gather(piece, "rzy", axis=0)
-    partner = lax.all_gather(plane, "core", axis=1)
-    chips, cores = partner.shape[:2]
-    partner = partner.reshape(chips * cores, *piece.shape)
+    piece = lax.dynamic_slice_in_dim(slab_rows, aux_index * share, share, axis=1)
+    partner = lax.all_gather(piece, ROW, axis=0)
+    row_count = partner.shape[0]
     result = jnp.einsum("pmi,rpki->mrk", slab_rows, partner, preferred_element_type=jnp.float32)
-    return result.astype(jnp.bfloat16).reshape(rows_local, chips * cores, 1, share)
+    return result.astype(jnp.bfloat16).reshape(rows_local, row_count, 1, share)
 
 
 def solution(mesh):

time: 228 us -> 188 us (0.82)
  waiting for transfers between devices: 142 us -> 100 us
  starting transfers between devices: 6.72 us -> 10.2 us
    all_gather x3 -> x1, waiting for transfers between devices: 140 us -> 75.7 us  [per_device(): partner = lax.all_gather(piece, ROW, axis=0)]
    ppermute x0 -> x3, waiting for transfers between devices: none -> 22.6 us  [per_device(): shifted.append(lax.ppermute(half_local[0], 'aux', pairs))]
    ppermute x0 -> x3, starting transfers between devices: none -> 3.67 us  [per_device(): shifted.append(lax.ppermute(half_local[0], 'aux', pairs))]
    unnamed x5 -> x3, local copies, waits for them, and re-layouts: 5.56 us -> 5.62 us
  transfers between devices with their start and end apart: 5 -> 6, of which waited for: 4 -> 4; matrix products, arithmetic and copies ran while one was open for 3% -> 4% of each run, Pallas kernels for 0% -> 0%
where the time goes in v2:
time: 188 us
  waiting for transfers between devices  100 us (53%)
  matrix products  31.3 us (17%)
  local copies, waits for them, and re-layouts  31.1 us (17%)
  between operations  13.4 us (7%)
  starting transfers between devices  10.2 us (5%)
    all_gather x1, waiting for transfers between devices, per_device(): partner = lax.all_gather(piece, ROW, axis=0)  75.7 us
    dot_general x1, matrix products, per_device(): jnp.einsum('pmi,rpki->mrk', slab_rows, partner, preferred_element_type=jn...  23.9 us
    ppermute x3, waiting for transfers between devices, per_device(): shifted.append(lax.ppermute(half_local[0], 'aux', pairs))  22.6 us
    reshape x1, local copies, waits for them, and re-layouts, per_device(): return result.astype(jnp.bfloat16).reshape(rows_local, row_count, 1, share)  17.9 us
    dot_general x1, matrix products, per_device(): jnp.einsum('pbmsn,bsni->pbmi', tiles_five, masked, preferred_element_type...  7.35 us
    gather x1, local copies, waits for them, and re-layouts, per_device(): picked = jnp.take(coeff_blocks, local_index, axis=0)  6.73 us
    unnamed x3, local copies, waits for them, and re-layouts  5.62 us
    ppermute x1, starting transfers between devices, with_halo(): lax.ppermute(lax.slice_in_dim(block, block.shape[dim] - width, None, axis...  4.58 us
  transfers between devices with their start and end apart: 6, of which 4 were waited for; matrix products, arithmetic and copies ran while one was open for 4% of the time, Pallas kernels for 0%

profile of v2, /device:TPU:1, one launch (start us, length us, event | category | flops | bytes accessed | tf_op | source)
XLA Modules:
  0.0 187.7 jit_solution(3153428194152655494)
XLA Ops:
  6.5 0.0 all-gather.3.cloned.1.call-start
  6.5 4.6 %collective-permute-start = (bf16[1024,256]{1,0:T(8,128)(2,1)}, bf16[1024,256]{1,0:T(8,128)(2,1)S(1)}, u32[]{:S(2)}, u32[]{:S(2)}) collective-permute-start(bf16[1024,256]{1,0:T(8,128)(2,1)} %param.5), channel_id=1, source_target_pairs={{0,1},{1,2},{2,3},{3,4},{4,5},{5,6},{6,7},{7,8},{8,9},{9,10},{10,1... | collective-permute-start | bytes 1572872 | tf_op jit(solution)/shard_map/ppermute | solution.py:12
  11.1 1.9 %collective-permute-start.1 = (bf16[1024,256]{1,0:T(8,128)(2,1)}, bf16[1024,256]{1,0:T(8,128)(2,1)S(1)}, u32[]{:S(2)}, u32[]{:S(2)}) collective-permute-start(bf16[1024,256]{1,0:T(8,128)(2,1)} %param.5), channel_id=1, source_target_pairs={{1,0},{2,1},{3,2},{4,3},{5,4},{6,5},{7,6},{8,7},{9,8},{10,9},{11,1... | collective-permute-start | bytes 1572872 | tf_op jit(solution)/shard_map/ppermute | solution.py:15
  13.1 0.7 convert_element_type.15
  13.8 0.7 compare_and_fusion
  14.5 0.1 reshape.24
  14.5 0.0 copy-start
  14.5 5.6 %copy.11 = bf16[128,8,16,128]{3,2,1,0:T(8,128)(2,1)} copy(bf16[128,8,16,128]{3,1,2,0:T(8,128)(2,1)} %bitcast.35) | data formatting | bytes 8388608
  20.2 0.0 collective-permute-done
  20.2 1.7 collective-permute-done.1
  21.8 0.0 copy-done
  21.8 0.1 pad_maximum_fusion.1
  22.0 6.7 %gather_fusion = bf16[128,128,256]{2,1,0:T(8,128)(2,1)} fusion(bf16[24,128,256]{2,1,0:T(8,128)(2,1)S(1)} %bitcast.33, s32[1024]{0:T(1024)S(1)} %pad_clamp_fusion), kind=kCustom, calls=%fused_computation | custom fusion | bytes 16777728 | tf_op jit(solution)/shard_map/jit(_take)/gather | solution.py:33
  28.7 7.3 %fusion.14 = bf16[8,256,128]{1,2,0:T(8,128)(2,1)S(1)} fusion(bf16[8,16,128,256]{3,2,1,0:T(8,128)(2,1)} %bitcast.34, pred[8,16]{1,0:T(8,128)(4,1)S(1)} %get-tuple-element.5, bf16[8,16]{1,0:T(8,128)(2,1)S(1)} %convert_element_type.15, bf16[8,128,16,128]{3,2,1,0:T(8,128)(2,1)} %bitcast.36), kind=kOutput, calls=%fused_computation.14 | convolution fusion | flops 1094975488 | bytes 13107584 | tf_op jit(solution)/shard_map/pbmsn,bsni->pbmi/dot_general | solution.py:37
  36.0 2.5 %collective-permute-start.4 = (bf16[1024,256]{1,0:T(8,128)(2,1)S(1)}, bf16[1024,256]{1,0:T(8,128)(2,1)S(1)}, u32[]{:S(2)}, u32[]{:S(2)}) collective-permute-start(bf16[1024,256]{1,0:T(8,128)(2,1)S(1)} %bitcast.37), channel_id=1, source_target_pairs={{0,96},{32,0},{64,32},{96,64},{1,97},{33,1},{65,33},{97,65},{2,98}... | collective-permute-start | bytes 1572872 | tf_op jit(solution)/shard_map/ppermute | solution.py:45
  38.6 0.5 collective-permute-start.3
  39.1 0.6 collective-permute-start.2
  39.7 18.7 %collective-permute-done.4 = bf16[1024,256]{1,0:T(8,128)(2,1)S(1)} collective-permute-done((bf16[1024,256]{1,0:T(8,128)(2,1)S(1)}, bf16[1024,256]{1,0:T(8,128)(2,1)S(1)}, u32[]{:S(2)}, u32[]{:S(2)}) %collective-permute-start.4) | collective-permute-done | bytes 524320 | tf_op jit(solution)/shard_map/ppermute | solution.py:45
  58.4 0.0 collective-permute-done.3
  58.4 3.9 %collective-permute-done.2 = bf16[1024,256]{1,0:T(8,128)(2,1)S(1)} collective-permute-done((bf16[1024,256]{1,0:T(8,128)(2,1)S(1)}, bf16[1024,256]{1,0:T(8,128)(2,1)S(1)}, u32[]{:S(2)}, u32[]{:S(2)}) %collective-permute-start.2) | collective-permute-done | bytes 524320 | tf_op jit(solution)/shard_map/ppermute | solution.py:45
  62.3 0.3 pad_maximum_fusion
  62.6 0.8 constant_dynamic-slice_fusion
  63.4 0.0 all-gather.3.cloned.1.call-update
  63.4 75.7 %all-gather.3.cloned.1.call-done = bf16[128,256,256]{2,1,0:T(8,128)(2,1)} async-done(((bf16[4,256,256]{2,1,0:T(8,128)(2,1)}), bf16[128,256,256]{2,1,0:T(8,128)(2,1)}) %all-gather.3.cloned.1.call-update) | async-done | bytes 16777232 | tf_op jit(solution)/shard_map/all_gather | solution.py:49
  139.1 23.9 %fusion = bf16[1024,32,1,256]{3,0,1,2:T(8,128)(2,1)} fusion(bf16[32,4,256,256]{3,2,1,0:T(8,128)(2,1)} %bitcast.48, bf16[1,1024,256]{2,1,0:T(8,128)(2,1)S(1)} %bitcast.43, bf16[1,1024,256]{2,1,0:T(8,128)(2,1)S(1)} %bitcast.45, bf16[1,1024,256]{2,1,0:T(8,128)(2,1)S(1)} %bitcast.47, bf16[1,1024,256]{2,1,0:T(8,128)(2,1)S(1)} %bitcast.41), kind=kOutput, calls=%fused_computation.2 | convolution fusion | flops 17196646400 | bytes 35651584 | tf_op jit(solution)/shard_map/pmi,rpki->mrk/dot_general | solution.py:51
  163.0 17.9 %copy.8 = bf16[1024,32,1,256]{3,1,2,0:T(8,128)(2,1)} copy(bf16[1024,32,1,256]{3,0,1,2:T(8,128)(2,1)} %fusion) | data formatting | bytes 33554432 | tf_op jit(solution)/shard_map/reshape | solution.py:52
  (1 shorter events, 0.0 us)
Async XLA Ops:
  6.5 132.6 %all-gather.3.cloned.1.call-start = ((), (), s32[]{:S(2)}) async-start(), calls=%async_computation | async-start | bytes 17301504 | tf_op jit(solution)/shard_map/all_gather | solution.py:49
  6.5 13.6 %collective-permute-start = (bf16[1024,256]{1,0:T(8,128)(2,1)}, bf16[1024,256]{1,0:T(8,128)(2,1)S(1)}, u32[]{:S(2)}, u32[]{:S(2)}) collective-permute-start(bf16[1024,256]{1,0:T(8,128)(2,1)} %param.5), channel_id=1, source_target_pairs={{0,1},{1,2},{2,3},{3,4},{4,5},{5,6},{6,7},{7,8},{8,9},{9,10},{10,1... | collective-permute-start | bytes 1572872 | tf_op jit(solution)/shard_map/ppermute | solution.py:12
  11.1 10.7 %collective-permute-start.1 = (bf16[1024,256]{1,0:T(8,128)(2,1)}, bf16[1024,256]{1,0:T(8,128)(2,1)S(1)}, u32[]{:S(2)}, u32[]{:S(2)}) collective-permute-start(bf16[1024,256]{1,0:T(8,128)(2,1)} %param.5), channel_id=1, source_target_pairs={{1,0},{2,1},{3,2},{4,3},{5,4},{6,5},{7,6},{8,7},{9,8},{10,9},{11,1... | collective-permute-start | bytes 1572872 | tf_op jit(solution)/shard_map/ppermute | solution.py:15
  14.5 7.3 %copy-start = (bf16[1024,256]{1,0:T(8,128)(2,1)S(1)}, bf16[1024,256]{1,0:T(8,128)(2,1)}, u32[]{:S(2)}) copy-start(bf16[1024,256]{1,0:T(8,128)(2,1)} %param.5) | copy-start | bytes 1572868
  36.0 22.4 %collective-permute-start.4 = (bf16[1024,256]{1,0:T(8,128)(2,1)S(1)}, bf16[1024,256]{1,0:T(8,128)(2,1)S(1)}, u32[]{:S(2)}, u32[]{:S(2)}) collective-permute-start(bf16[1024,256]{1,0:T(8,128)(2,1)S(1)} %bitcast.37), channel_id=1, source_target_pairs={{0,96},{32,0},{64,32},{96,64},{1,97},{33,1},{65,33},{97,65},{2,98}... | collective-permute-start | bytes 1572872 | tf_op jit(solution)/shard_map/ppermute | solution.py:45
  38.6 19.8 %collective-permute-start.3 = (bf16[1024,256]{1,0:T(8,128)(2,1)S(1)}, bf16[1024,256]{1,0:T(8,128)(2,1)S(1)}, u32[]{:S(2)}, u32[]{:S(2)}) collective-permute-start(bf16[1024,256]{1,0:T(8,128)(2,1)S(1)} %bitcast.38), channel_id=1, source_target_pairs={{0,64},{32,96},{64,0},{96,32},{1,65},{33,97},{65,1},{97,33},{2,66}... | collective-permute-start | bytes 1572872 | tf_op jit(solution)/shard_map/ppermute | solution.py:45
  39.1 23.2 %collective-permute-start.2 = (bf16[1024,256]{1,0:T(8,128)(2,1)S(1)}, bf16[1024,256]{1,0:T(8,128)(2,1)S(1)}, u32[]{:S(2)}, u32[]{:S(2)}) collective-permute-start(bf16[1024,256]{1,0:T(8,128)(2,1)S(1)} %bitcast.39), channel_id=1, source_target_pairs={{0,32},{32,64},{64,96},{96,0},{1,33},{33,65},{65,97},{97,1},{2,34}... | collective-permute-start | bytes 1572872 | tf_op jit(solution)/shard_map/ppermute | solution.py:45
Sparse Core Ops, SparseCore 0:
  63.6 75.5 all-gather.2

commit v3 on v2

--- a/solution.py
+++ b/solution.py
@@ -39,17 +39,30 @@
     )
     half_local = half_sum.astype(jnp.bfloat16).reshape(p_local, rows_local, orbitals)
     aux_index = lax.axis_index("aux")
-    shifted = [half_local[0]]
+    share = rows_local // aux_count
+    own = half_local[0]
+    pieces = [lax.dynamic_slice_in_dim(own, aux_index * share, share, axis=0)]
+    shifted = [own]
     for shift in range(1, aux_count):
         pairs = [(i, (i + shift) % aux_count) for i in range(aux_count)]
-        shifted.append(lax.ppermute(half_local[0], "aux", pairs))
+        target = (aux_index + shift) % aux_count
+        outgoing = lax.dynamic_slice_in_dim(own, target * share, share, axis=0)
+        pieces.append(lax.ppermute(outgoing, "aux", pairs))
+        shifted.append(lax.ppermute(own, "aux", pairs))
+    piece = jnp.stack(pieces)
     slab_rows = jnp.stack(shifted)
-    share = rows_local // aux_count
-    piece = lax.dynamic_slice_in_dim(slab_rows, aux_index * share, share, axis=1)
-    partner = lax.all_gather(piece, ROW, axis=0)
-    row_count = partner.shape[0]
-    result = jnp.einsum("pmi,rpki->mrk", slab_rows, partner, preferred_element_type=jnp.float32)
-    return result.astype(jnp.bfloat16).reshape(rows_local, row_count, 1, share)
+    chunk_count = 2
+    chunk = share // chunk_count
+    results = []
+    for c in range(chunk_count):
+        part = lax.slice_in_dim(piece, c * chunk, (c + 1) * chunk, axis=1)
+        partner = lax.all_gather(part, ROW, axis=0)
+        results.append(
+            jnp.einsum("pmi,rpki->mrk", slab_rows, partner, preferred_element_type=jnp.float32)
+            .astype(jnp.bfloat16)
+        )
+    result = jnp.concatenate(results, axis=2)
+    return result.reshape(rows_local, result.shape[1], 1, share)
 
 
 def solution(mesh):

time: 188 us -> 207 us (1.10)
  other arithmetic: 1.75 us -> 8.37 us
  local copies, waits for them, and re-layouts: 31.1 us -> 37 us
  matrix products: 31.3 us -> 33.4 us
    ppermute x3 -> x6, waiting for transfers between devices: 22.6 us -> 29.8 us  [the longest x3 24.2 us: per_device(): shifted.append(lax.ppermute(own, 'aux', pairs))]
    reshape x0 -> x1, other arithmetic: none -> 6.81 us  [per_device(): return result.reshape(rows_local, result.shape[1], 1, share)]
    reshape x1, local copies, waits for them, and re-layouts: 17.9 us -> 23.7 us  [per_device(): return result.reshape(rows_local, result.shape[1], 1, share)]
    all_gather x1 -> x2, waiting for transfers between devices: 75.7 us -> 70 us  [per_device(): partner = lax.all_gather(part, ROW, axis=0)]
    dot_general x1 -> x2, matrix products: 23.9 us -> 26 us  [per_device(): jnp.einsum('pmi,rpki->mrk', slab_rows, partner, preferred_element_type=jn...]
    ppermute x3 -> x6, starting transfers between devices: 3.67 us -> 5.21 us  [the longest x3 3.67 us: per_device(): pieces.append(lax.ppermute(outgoing, 'aux', pairs))]
    unnamed x3 -> x5, local copies, waits for them, and re-layouts: 5.62 us -> 5.63 us
  transfers between devices with their start and end apart: 6 -> 10, of which waited for: 4 -> 9; matrix products, arithmetic and copies ran while one was open for 4% -> 10% of each run, Pallas kernels for 0% -> 0%
where the time goes in v3:
time: 207 us; the launch traced here: 206 us
  waiting for transfers between devices  102 us (49%)
  local copies, waits for them, and re-layouts  37 us (18%)
  matrix products  33.4 us (16%)
  between operations  13.5 us (7%)
  starting transfers between devices  11.8 us (6%)
  other arithmetic  8.37 us (4%)
    all_gather x2, waiting for transfers between devices, per_device(): partner = lax.all_gather(part, ROW, axis=0)  70 us
    dot_general x2, matrix products, per_device(): jnp.einsum('pmi,rpki->mrk', slab_rows, partner, preferred_element_type=jn...  26 us
    ppermute x3, waiting for transfers between devices, per_device(): shifted.append(lax.ppermute(own, 'aux', pairs))  24.2 us
    reshape x1, local copies, waits for them, and re-layouts, per_device(): return result.reshape(rows_local, result.shape[1], 1, share)  23.7 us
    dot_general x1, matrix products, per_device(): jnp.einsum('pbmsn,bsni->pbmi', tiles_five, masked, preferred_element_type...  7.35 us
    reshape x1, other arithmetic, per_device(): return result.reshape(rows_local, result.shape[1], 1, share)  6.81 us
    gather x1, local copies, waits for them, and re-layouts, per_device(): picked = jnp.take(coeff_blocks, local_index, axis=0)  6.74 us
    unnamed x5, local copies, waits for them, and re-layouts  5.63 us
  transfers between devices with their start and end apart: 10, of which 9 were waited for; matrix products, arithmetic and copies ran while one was open for 10% of the time, Pallas kernels for 0%

profile of v3, /device:TPU:1, one launch (start us, length us, event | category | flops | bytes accessed | tf_op | source)
XLA Modules:
  0.0 206.2 jit_solution(13281085062733981635)
XLA Ops:
  6.5 4.6 %collective-permute-start = (bf16[1024,256]{1,0:T(8,128)(2,1)}, bf16[1024,256]{1,0:T(8,128)(2,1)S(1)}, u32[]{:S(2)}, u32[]{:S(2)}) collective-permute-start(bf16[1024,256]{1,0:T(8,128)(2,1)} %param.5), channel_id=1, source_target_pairs={{0,1},{1,2},{2,3},{3,4},{4,5},{5,6},{6,7},{7,8},{8,9},{9,10},{10,1... | collective-permute-start | bytes 1572872 | tf_op jit(solution)/shard_map/ppermute | solution.py:12
  11.1 1.9 collective-permute-start.1
  13.1 0.7 convert_element_type.18
  13.8 0.7 compare_and_fusion
  14.5 0.1 reshape.24
  14.6 5.6 %copy.12 = bf16[128,8,16,128]{3,2,1,0:T(8,128)(2,1)} copy(bf16[128,8,16,128]{3,1,2,0:T(8,128)(2,1)} %bitcast.44) | data formatting | bytes 8388608
  20.2 1.6 collective-permute-done.1
  21.8 0.1 pad_maximum_fusion
  22.0 6.7 %gather_fusion = bf16[128,128,256]{2,1,0:T(8,128)(2,1)} fusion(bf16[24,128,256]{2,1,0:T(8,128)(2,1)S(1)} %bitcast.42, s32[1024]{0:T(1024)S(1)} %pad_clamp_fusion), kind=kCustom, calls=%fused_computation | custom fusion | bytes 16777728 | tf_op jit(solution)/shard_map/jit(_take)/gather | solution.py:33
  28.7 7.3 %fusion.12 = bf16[8,256,128]{1,2,0:T(8,128)(2,1)S(1)} fusion(bf16[8,16,128,256]{3,2,1,0:T(8,128)(2,1)} %bitcast.43, pred[8,16]{1,0:T(8,128)(4,1)S(1)} %get-tuple-element.5, bf16[8,16]{1,0:T(8,128)(2,1)S(1)} %convert_element_type.18, bf16[8,128,16,128]{3,2,1,0:T(8,128)(2,1)} %bitcast.45), kind=kOutput, calls=%fused_computation.14 | convolution fusion | flops 1094975488 | bytes 13107584 | tf_op jit(solution)/shard_map/pbmsn,bsni->pbmi/dot_general | solution.py:37
  36.1 2.5 %collective-permute-start.7 = (bf16[256,256]{1,0:T(8,128)(2,1)S(1)}, bf16[256,256]{1,0:T(8,128)(2,1)S(1)}, u32[]{:S(2)}, u32[]{:S(2)}) collective-permute-start(bf16[256,256]{1,0:T(8,128)(2,1)S(1)} %get-tuple-element.10), channel_id=1, source_target_pairs={{0,96},{32,0},{64,32},{96,64},{1,97},{33,1},{65,33},{97,65},{2,98}... | collective-permute-start | bytes 393224 | tf_op jit(solution)/shard_map/ppermute | solution.py:50
  38.7 0.5 collective-permute-start.6
  39.2 0.6 collective-permute-start.5
  39.8 2.3 %collective-permute-done.7 = bf16[256,256]{1,0:T(8,128)(2,1)S(1)} collective-permute-done((bf16[256,256]{1,0:T(8,128)(2,1)S(1)}, bf16[256,256]{1,0:T(8,128)(2,1)S(1)}, u32[]{:S(2)}, u32[]{:S(2)}) %collective-permute-start.7) | collective-permute-done | bytes 131104 | tf_op jit(solution)/shard_map/ppermute | solution.py:50
  42.1 2.0 collective-permute-done.6
  44.1 1.3 collective-permute-done.5
  45.4 0.1 pad_maximum_fusion.1
  45.5 0.8 fusion.20
  46.3 0.0 all-gather.5.cloned.1.call-start
  46.4 0.7 all-gather.5.cloned.1.call-update
  47.1 0.4 collective-permute-start.4
  47.4 0.5 collective-permute-start.3
  47.9 0.7 collective-permute-start.2
  48.6 12.5 %collective-permute-done.4 = bf16[1024,256]{1,0:T(8,128)(2,1)S(1)} collective-permute-done((bf16[1024,256]{1,0:T(8,128)(2,1)S(1)}, bf16[1024,256]{1,0:T(8,128)(2,1)S(1)}, u32[]{:S(2)}, u32[]{:S(2)}) %collective-permute-start.4) | collective-permute-done | bytes 524320 | tf_op jit(solution)/shard_map/ppermute | solution.py:51
  61.1 1.5 collective-permute-done.3
  62.7 10.2 %collective-permute-done.2 = bf16[1024,256]{1,0:T(8,128)(2,1)S(1)} collective-permute-done((bf16[1024,256]{1,0:T(8,128)(2,1)S(1)}, bf16[1024,256]{1,0:T(8,128)(2,1)S(1)}, u32[]{:S(2)}, u32[]{:S(2)}) %collective-permute-start.2) | collective-permute-done | bytes 524320 | tf_op jit(solution)/shard_map/ppermute | solution.py:51
  72.8 29.7 %all-gather.7.cloned.1.call-done = bf16[128,128,256]{2,1,0:T(8,128)(2,1)} async-done(((bf16[4,128,256]{2,1,0:T(8,128)(2,1)}), bf16[128,128,256]{2,1,0:T(8,128)(2,1)}) %all-gather.7.cloned.1.call-update) | async-done | bytes 8388624 | tf_op jit(solution)/shard_map/all_gather | solution.py:59
  102.6 14.5 %bitcast_convert_fusion = bf16[1024,32,128]{0,2,1:T(8,128)(2,1)} fusion(bf16[32,4,128,256]{3,2,1,0:T(8,128)(2,1)} %bitcast.55, bf16[1,1024,256]{2,1,0:T(8,128)(2,1)S(1)} %bitcast.57, bf16[1,1024,256]{2,1,0:T(8,128)(2,1)S(1)} %bitcast.59, bf16[1,1024,256]{2,1,0:T(8,128)(2,1)S(1)} %bitcast.61, bf16[1,1024,256]{2,1,0:T(8,128)(2,1)S(1)} %bitcast.50), kind=kOutput, calls=%fused_computation.2 | convolution fusion | flops 8602517504 | bytes 18874368 | tf_op jit(solution)/shard_map/pmi,rpki->mrk/dot_general | solution.py:61
  117.1 40.3 %all-gather.5.cloned.1.call-done = bf16[128,128,256]{2,1,0:T(8,128)(2,1)} async-done(((bf16[4,128,256]{2,1,0:T(8,128)(2,1)}), bf16[128,128,256]{2,1,0:T(8,128)(2,1)}) %all-gather.5.cloned.1.call-update) | async-done | bytes 8388624 | tf_op jit(solution)/shard_map/all_gather | solution.py:59
  157.4 11.5 %bitcast_convert_fusion.1 = bf16[1024,32,128]{0,2,1:T(8,128)(2,1)S(1)} fusion(bf16[32,4,128,256]{3,2,1,0:T(8,128)(2,1)} %bitcast.56, bf16[1,1024,256]{2,1,0:T(8,128)(2,1)S(1)} %bitcast.58, bf16[1,1024,256]{2,1,0:T(8,128)(2,1)S(1)} %bitcast.60, bf16[1,1024,256]{2,1,0:T(8,128)(2,1)S(1)} %bitcast.62, bf16[1,1024,256]{2,1,0:T(8,128)(2,1)S(1)} %bitcast.51), kind=kOutput, calls=%fused_computation.3 | convolution fusion | flops 8602517504 | bytes 18874368 | tf_op jit(solution)/shard_map/pmi,rpki->mrk/dot_general | solution.py:61
  168.9 6.8 %maximum_bitcast_fusion = bf16[1024,32,1,256]{0,3,1,2:T(8,128)(2,1)} fusion(bf16[1024,32,128]{0,2,1:T(8,128)(2,1)S(1)} %copy-done, bf16[1024,32,128]{0,2,1:T(8,128)(2,1)S(1)} %bitcast_convert_fusion.1), kind=kLoop, calls=%fused_computation.1 | loop fusion | flops 33554432 | bytes 33554432 | tf_op jit(solution)/shard_map/reshape | solution.py:65
  175.7 23.7 %copy.8 = bf16[1024,32,1,256]{3,1,2,0:T(8,128)(2,1)} copy(bf16[1024,32,1,256]{0,3,1,2:T(8,128)(2,1)} %maximum_bitcast_fusion) | data formatting | bytes 33554432 | tf_op jit(solution)/shard_map/reshape | solution.py:65
  (9 shorter events, 0.1 us)
Async XLA Ops:
  6.5 96.0 %all-gather.7.cloned.1.call-start = ((), (), s32[]{:S(2)}) async-start(), calls=%async_computation.1 | async-start | bytes 8650752 | tf_op jit(solution)/shard_map/all_gather | solution.py:59
  6.5 13.7 %collective-permute-start = (bf16[1024,256]{1,0:T(8,128)(2,1)}, bf16[1024,256]{1,0:T(8,128)(2,1)S(1)}, u32[]{:S(2)}, u32[]{:S(2)}) collective-permute-start(bf16[1024,256]{1,0:T(8,128)(2,1)} %param.5), channel_id=1, source_target_pairs={{0,1},{1,2},{2,3},{3,4},{4,5},{5,6},{6,7},{7,8},{8,9},{9,10},{10,1... | collective-permute-start | bytes 1572872 | tf_op jit(solution)/shard_map/ppermute | solution.py:12
  11.1 10.7 %collective-permute-start.1 = (bf16[1024,256]{1,0:T(8,128)(2,1)}, bf16[1024,256]{1,0:T(8,128)(2,1)S(1)}, u32[]{:S(2)}, u32[]{:S(2)}) collective-permute-start(bf16[1024,256]{1,0:T(8,128)(2,1)} %param.5), channel_id=1, source_target_pairs={{1,0},{2,1},{3,2},{4,3},{5,4},{6,5},{7,6},{8,7},{9,8},{10,9},{11,1... | collective-permute-start | bytes 1572872 | tf_op jit(solution)/shard_map/ppermute | solution.py:15
  14.6 7.3 %copy-start.1 = (bf16[1024,256]{1,0:T(8,128)(2,1)S(1)}, bf16[1024,256]{1,0:T(8,128)(2,1)}, u32[]{:S(2)}) copy-start(bf16[1024,256]{1,0:T(8,128)(2,1)} %param.5) | copy-start | bytes 1572868
  36.1 6.0 %collective-permute-start.7 = (bf16[256,256]{1,0:T(8,128)(2,1)S(1)}, bf16[256,256]{1,0:T(8,128)(2,1)S(1)}, u32[]{:S(2)}, u32[]{:S(2)}) collective-permute-start(bf16[256,256]{1,0:T(8,128)(2,1)S(1)} %get-tuple-element.10), channel_id=1, source_target_pairs={{0,96},{32,0},{64,32},{96,64},{1,97},{33,1},{65,33},{97,65},{2,98}... | collective-permute-start | bytes 393224 | tf_op jit(solution)/shard_map/ppermute | solution.py:50
  38.7 5.4 %collective-permute-start.6 = (bf16[256,256]{1,0:T(8,128)(2,1)S(1)}, bf16[256,256]{1,0:T(8,128)(2,1)S(1)}, u32[]{:S(2)}, u32[]{:S(2)}) collective-permute-start(bf16[256,256]{1,0:T(8,128)(2,1)S(1)} %get-tuple-element.11), channel_id=1, source_target_pairs={{0,64},{32,96},{64,0},{96,32},{1,65},{33,97},{65,1},{97,33},{2,66}... | collective-permute-start | bytes 393224 | tf_op jit(solution)/shard_map/ppermute | solution.py:50
  39.2 6.2 %collective-permute-start.5 = (bf16[256,256]{1,0:T(8,128)(2,1)S(1)}, bf16[256,256]{1,0:T(8,128)(2,1)S(1)}, u32[]{:S(2)}, u32[]{:S(2)}) collective-permute-start(bf16[256,256]{1,0:T(8,128)(2,1)S(1)} %get-tuple-element.12), channel_id=1, source_target_pairs={{0,32},{32,64},{64,96},{96,0},{1,33},{33,65},{65,97},{97,1},{2,34}... | collective-permute-start | bytes 393224 | tf_op jit(solution)/shard_map/ppermute | solution.py:50
  46.3 111.1 %all-gather.5.cloned.1.call-start = ((), (), s32[]{:S(2)}) async-start(), calls=%async_computation | async-start | bytes 8650752 | tf_op jit(solution)/shard_map/all_gather | solution.py:59
  47.1 14.1 %collective-permute-start.4 = (bf16[1024,256]{1,0:T(8,128)(2,1)S(1)}, bf16[1024,256]{1,0:T(8,128)(2,1)S(1)}, u32[]{:S(2)}, u32[]{:S(2)}) collective-permute-start(bf16[1024,256]{1,0:T(8,128)(2,1)S(1)} %bitcast.47), channel_id=1, source_target_pairs={{0,96},{32,0},{64,32},{96,64},{1,97},{33,1},{65,33},{97,65},{2,98}... | collective-permute-start | bytes 1572872 | tf_op jit(solution)/shard_map/ppermute | solution.py:51
  47.4 15.2 %collective-permute-start.3 = (bf16[1024,256]{1,0:T(8,128)(2,1)S(1)}, bf16[1024,256]{1,0:T(8,128)(2,1)S(1)}, u32[]{:S(2)}, u32[]{:S(2)}) collective-permute-start(bf16[1024,256]{1,0:T(8,128)(2,1)S(1)} %bitcast.48), channel_id=1, source_target_pairs={{0,64},{32,96},{64,0},{96,32},{1,65},{33,97},{65,1},{97,33},{2,66}... | collective-permute-start | bytes 1572872 | tf_op jit(solution)/shard_map/ppermute | solution.py:51
  47.9 24.9 %collective-permute-start.2 = (bf16[1024,256]{1,0:T(8,128)(2,1)S(1)}, bf16[1024,256]{1,0:T(8,128)(2,1)S(1)}, u32[]{:S(2)}, u32[]{:S(2)}) collective-permute-start(bf16[1024,256]{1,0:T(8,128)(2,1)S(1)} %bitcast.49), channel_id=1, source_target_pairs={{0,32},{32,64},{64,96},{96,0},{1,33},{33,65},{65,97},{97,1},{2,34}... | collective-permute-start | bytes 1572872 | tf_op jit(solution)/shard_map/ppermute | solution.py:51
  157.4 11.5 %copy-start = (bf16[1024,32,128]{0,2,1:T(8,128)(2,1)S(1)}, bf16[1024,32,128]{0,2,1:T(8,128)(2,1)}, u32[]{:S(2)}) copy-start(bf16[1024,32,128]{0,2,1:T(8,128)(2,1)} %bitcast_convert_fusion) | copy-start | bytes 25165828
Sparse Core Ops, SparseCore 0:
  46.4 56.0 all-gather.6
  104.8 52.5 all-gather.4

commit v4 on v3

--- a/solution.py
+++ b/solution.py
@@ -51,18 +51,9 @@
         shifted.append(lax.ppermute(own, "aux", pairs))
     piece = jnp.stack(pieces)
     slab_rows = jnp.stack(shifted)
-    chunk_count = 2
-    chunk = share // chunk_count
-    results = []
-    for c in range(chunk_count):
-        part = lax.slice_in_dim(piece, c * chunk, (c + 1) * chunk, axis=1)
-        partner = lax.all_gather(part, ROW, axis=0)
-        results.append(
-            jnp.einsum("pmi,rpki->mrk", slab_rows, partner, preferred_element_type=jnp.float32)
-            .astype(jnp.bfloat16)
-        )
-    result = jnp.concatenate(results, axis=2)
-    return result.reshape(rows_local, result.shape[1], 1, share)
+    partner = lax.all_gather(piece, ROW, axis=0)
+    result = jnp.einsum("pmi,rpki->mrk", slab_rows, partner, preferred_element_type=jnp.float32)
+    return result.astype(jnp.bfloat16).reshape(rows_local, partner.shape[0], 1, share)
 
 
 def solution(mesh):

time: 207 us -> 171 us (0.83)
  waiting for transfers between devices: 102 us -> 81.6 us
  local copies, waits for them, and re-layouts: 37 us -> 30.4 us
  other arithmetic: 8.37 us -> 2.35 us
  matrix products: 33.4 us -> 31.2 us
    all_gather x2 -> x1, waiting for transfers between devices: 70 us -> 50.1 us  [per_device(): partner = lax.all_gather(piece, ROW, axis=0)]
    reshape x1 -> x0, other arithmetic: 6.81 us -> none  [per_device(): return result.reshape(rows_local, result.shape[1], 1, share)]
    reshape x1, local copies, waits for them, and re-layouts: 23.7 us -> 17.9 us  [per_device(): result.astype(jnp.bfloat16).reshape(rows_local, partner.shape[0], 1, share)]
    dot_general x2 -> x1, matrix products: 26 us -> 23.9 us  [per_device(): jnp.einsum('pmi,rpki->mrk', slab_rows, partner, preferred_element_type=jn...]
    unnamed x5 -> x3, local copies, waits for them, and re-layouts: 5.63 us -> 5.62 us
  transfers between devices with their start and end apart: 10 -> 9, of which waited for: 9 -> 8; matrix products, arithmetic and copies ran while one was open for 10% -> 4% of each run, Pallas kernels for 0% -> 0%
where the time goes in v4:
time: 171 us
  waiting for transfers between devices  81.6 us (48%)
  matrix products  31.2 us (18%)
  local copies, waits for them, and re-layouts  30.4 us (18%)
  between operations  13.5 us (8%)
  starting transfers between devices  11.7 us (7%)
  other arithmetic  2.35 us (1%)
    all_gather x1, waiting for transfers between devices, per_device(): partner = lax.all_gather(piece, ROW, axis=0)  50.1 us
    ppermute x3, waiting for transfers between devices, per_device(): shifted.append(lax.ppermute(own, 'aux', pairs))  24.2 us
    dot_general x1, matrix products, per_device(): jnp.einsum('pmi,rpki->mrk', slab_rows, partner, preferred_element_type=jn...  23.9 us
    reshape x1, local copies, waits for them, and re-layouts, per_device(): result.astype(jnp.bfloat16).reshape(rows_local, partner.shape[0], 1, share)  17.9 us
    dot_general x1, matrix products, per_device(): jnp.einsum('pbmsn,bsni->pbmi', tiles_five, masked, preferred_element_type...  7.35 us
    gather x1, local copies, waits for them, and re-layouts, per_device(): picked = jnp.take(coeff_blocks, local_index, axis=0)  6.74 us
    unnamed x3, local copies, waits for them, and re-layouts  5.62 us
    ppermute x3, waiting for transfers between devices, per_device(): pieces.append(lax.ppermute(outgoing, 'aux', pairs))  5.6 us
  transfers between devices with their start and end apart: 9, of which 8 were waited for; matrix products, arithmetic and copies ran while one was open for 4% of the time, Pallas kernels for 0%

profile of v4, /device:TPU:1, one launch (start us, length us, event | category | flops | bytes accessed | tf_op | source)
XLA Modules:
  0.0 170.7 jit_solution(16439519776263693180)
XLA Ops:
  6.5 0.0 all-gather.3.cloned.1.call-start
  6.5 4.6 %collective-permute-start = (bf16[1024,256]{1,0:T(8,128)(2,1)}, bf16[1024,256]{1,0:T(8,128)(2,1)S(1)}, u32[]{:S(2)}, u32[]{:S(2)}) collective-permute-start(bf16[1024,256]{1,0:T(8,128)(2,1)} %param.5), channel_id=1, source_target_pairs={{0,1},{1,2},{2,3},{3,4},{4,5},{5,6},{6,7},{7,8},{8,9},{9,10},{10,1... | collective-permute-start | bytes 1572872 | tf_op jit(solution)/shard_map/ppermute | solution.py:12
  11.1 1.9 %collective-permute-start.1 = (bf16[1024,256]{1,0:T(8,128)(2,1)}, bf16[1024,256]{1,0:T(8,128)(2,1)S(1)}, u32[]{:S(2)}, u32[]{:S(2)}) collective-permute-start(bf16[1024,256]{1,0:T(8,128)(2,1)} %param.5), channel_id=1, source_target_pairs={{1,0},{2,1},{3,2},{4,3},{5,4},{6,5},{7,6},{8,7},{9,8},{10,9},{11,1... | collective-permute-start | bytes 1572872 | tf_op jit(solution)/shard_map/ppermute | solution.py:15
  13.1 0.7 convert_element_type.15
  13.8 0.7 compare_and_fusion
  14.5 0.1 reshape.24
  14.6 0.0 copy-start
  14.6 5.6 %copy.11 = bf16[128,8,16,128]{3,2,1,0:T(8,128)(2,1)} copy(bf16[128,8,16,128]{3,1,2,0:T(8,128)(2,1)} %bitcast.40) | data formatting | bytes 8388608
  20.2 0.0 collective-permute-done
  20.2 1.6 collective-permute-done.1
  21.8 0.0 copy-done
  21.8 0.1 pad_maximum_fusion
  22.0 6.7 %gather_fusion = bf16[128,128,256]{2,1,0:T(8,128)(2,1)} fusion(bf16[24,128,256]{2,1,0:T(8,128)(2,1)S(1)} %bitcast.38, s32[1024]{0:T(1024)S(1)} %pad_clamp_fusion), kind=kCustom, calls=%fused_computation | custom fusion | bytes 16777728 | tf_op jit(solution)/shard_map/jit(_take)/gather | solution.py:33
  28.7 7.3 %fusion.19 = bf16[8,256,128]{1,2,0:T(8,128)(2,1)S(1)} fusion(bf16[8,16,128,256]{3,2,1,0:T(8,128)(2,1)} %bitcast.39, pred[8,16]{1,0:T(8,128)(4,1)S(1)} %get-tuple-element.5, bf16[8,16]{1,0:T(8,128)(2,1)S(1)} %convert_element_type.15, bf16[8,128,16,128]{3,2,1,0:T(8,128)(2,1)} %bitcast.41), kind=kOutput, calls=%fused_computation.19 | convolution fusion | flops 1094975488 | bytes 13107584 | tf_op jit(solution)/shard_map/pbmsn,bsni->pbmi/dot_general | solution.py:37
  36.1 2.5 %collective-permute-start.7 = (bf16[256,256]{1,0:T(8,128)(2,1)S(1)}, bf16[256,256]{1,0:T(8,128)(2,1)S(1)}, u32[]{:S(2)}, u32[]{:S(2)}) collective-permute-start(bf16[256,256]{1,0:T(8,128)(2,1)S(1)} %get-tuple-element.8), channel_id=1, source_target_pairs={{0,96},{32,0},{64,32},{96,64},{1,97},{33,1},{65,33},{97,65},{2,98}... | collective-permute-start | bytes 393224 | tf_op jit(solution)/shard_map/ppermute | solution.py:50
  38.7 0.5 collective-permute-start.6
  39.2 0.6 collective-permute-start.5
  39.8 2.3 %collective-permute-done.7 = bf16[256,256]{1,0:T(8,128)(2,1)S(1)} collective-permute-done((bf16[256,256]{1,0:T(8,128)(2,1)S(1)}, bf16[256,256]{1,0:T(8,128)(2,1)S(1)}, u32[]{:S(2)}, u32[]{:S(2)}) %collective-permute-start.7) | collective-permute-done | bytes 131104 | tf_op jit(solution)/shard_map/ppermute | solution.py:50
  42.0 2.0 %collective-permute-done.6 = bf16[256,256]{1,0:T(8,128)(2,1)S(1)} collective-permute-done((bf16[256,256]{1,0:T(8,128)(2,1)S(1)}, bf16[256,256]{1,0:T(8,128)(2,1)S(1)}, u32[]{:S(2)}, u32[]{:S(2)}) %collective-permute-start.6) | collective-permute-done | bytes 131104 | tf_op jit(solution)/shard_map/ppermute | solution.py:50
  44.1 1.3 collective-permute-done.5
  45.4 0.9 pad_maximum_fusion.1
  46.2 0.0 all-gather.3.cloned.1.call-update
  46.3 0.4 collective-permute-start.4
  46.6 0.5 collective-permute-start.3
  47.1 0.7 collective-permute-start.2
  47.8 12.5 %collective-permute-done.4 = bf16[1024,256]{1,0:T(8,128)(2,1)S(1)} collective-permute-done((bf16[1024,256]{1,0:T(8,128)(2,1)S(1)}, bf16[1024,256]{1,0:T(8,128)(2,1)S(1)}, u32[]{:S(2)}, u32[]{:S(2)}) %collective-permute-start.4) | collective-permute-done | bytes 524320 | tf_op jit(solution)/shard_map/ppermute | solution.py:51
  60.3 1.5 collective-permute-done.3
  61.9 10.1 %collective-permute-done.2 = bf16[1024,256]{1,0:T(8,128)(2,1)S(1)} collective-permute-done((bf16[1024,256]{1,0:T(8,128)(2,1)S(1)}, bf16[1024,256]{1,0:T(8,128)(2,1)S(1)}, u32[]{:S(2)}, u32[]{:S(2)}) %collective-permute-start.2) | collective-permute-done | bytes 524320 | tf_op jit(solution)/shard_map/ppermute | solution.py:51
  72.0 50.1 %all-gather.3.cloned.1.call-done = bf16[128,256,256]{2,1,0:T(8,128)(2,1)} async-done(((bf16[4,256,256]{2,1,0:T(8,128)(2,1)}), bf16[128,256,256]{2,1,0:T(8,128)(2,1)}) %all-gather.3.cloned.1.call-update) | async-done | bytes 16777232 | tf_op jit(solution)/shard_map/all_gather | solution.py:54
  122.1 23.9 %fusion = bf16[1024,32,1,256]{3,0,1,2:T(8,128)(2,1)} fusion(bf16[32,4,256,256]{3,2,1,0:T(8,128)(2,1)} %bitcast.50, bf16[1,1024,256]{2,1,0:T(8,128)(2,1)S(1)} %bitcast.51, bf16[1,1024,256]{2,1,0:T(8,128)(2,1)S(1)} %bitcast.52, bf16[1,1024,256]{2,1,0:T(8,128)(2,1)S(1)} %bitcast.53, bf16[1,1024,256]{2,1,0:T(8,128)(2,1)S(1)} %bitcast.46), kind=kOutput, calls=%fused_computation.2 | convolution fusion | flops 17196646400 | bytes 35651584 | tf_op jit(solution)/shard_map/pmi,rpki->mrk/dot_general | solution.py:55
  146.0 17.9 %copy.8 = bf16[1024,32,1,256]{3,1,2,0:T(8,128)(2,1)} copy(bf16[1024,32,1,256]{3,0,1,2:T(8,128)(2,1)} %fusion) | data formatting | bytes 33554432 | tf_op jit(solution)/shard_map/reshape | solution.py:56
  (2 shorter events, 0.1 us)
Async XLA Ops:
  6.5 115.6 %all-gather.3.cloned.1.call-start = ((), (), s32[]{:S(2)}) async-start(), calls=%async_computation | async-start | bytes 17301504 | tf_op jit(solution)/shard_map/all_gather | solution.py:54
  6.5 13.7 %collective-permute-start = (bf16[1024,256]{1,0:T(8,128)(2,1)}, bf16[1024,256]{1,0:T(8,128)(2,1)S(1)}, u32[]{:S(2)}, u32[]{:S(2)}) collective-permute-start(bf16[1024,256]{1,0:T(8,128)(2,1)} %param.5), channel_id=1, source_target_pairs={{0,1},{1,2},{2,3},{3,4},{4,5},{5,6},{6,7},{7,8},{8,9},{9,10},{10,1... | collective-permute-start | bytes 1572872 | tf_op jit(solution)/shard_map/ppermute | solution.py:12
  11.1 10.7 %collective-permute-start.1 = (bf16[1024,256]{1,0:T(8,128)(2,1)}, bf16[1024,256]{1,0:T(8,128)(2,1)S(1)}, u32[]{:S(2)}, u32[]{:S(2)}) collective-permute-start(bf16[1024,256]{1,0:T(8,128)(2,1)} %param.5), channel_id=1, source_target_pairs={{1,0},{2,1},{3,2},{4,3},{5,4},{6,5},{7,6},{8,7},{9,8},{10,9},{11,1... | collective-permute-start | bytes 1572872 | tf_op jit(solution)/shard_map/ppermute | solution.py:15
  14.6 7.3 %copy-start = (bf16[1024,256]{1,0:T(8,128)(2,1)S(1)}, bf16[1024,256]{1,0:T(8,128)(2,1)}, u32[]{:S(2)}) copy-start(bf16[1024,256]{1,0:T(8,128)(2,1)} %param.5) | copy-start | bytes 1572868
  36.1 5.9 %collective-permute-start.7 = (bf16[256,256]{1,0:T(8,128)(2,1)S(1)}, bf16[256,256]{1,0:T(8,128)(2,1)S(1)}, u32[]{:S(2)}, u32[]{:S(2)}) collective-permute-start(bf16[256,256]{1,0:T(8,128)(2,1)S(1)} %get-tuple-element.8), channel_id=1, source_target_pairs={{0,96},{32,0},{64,32},{96,64},{1,97},{33,1},{65,33},{97,65},{2,98}... | collective-permute-start | bytes 393224 | tf_op jit(solution)/shard_map/ppermute | solution.py:50
  38.7 5.4 %collective-permute-start.6 = (bf16[256,256]{1,0:T(8,128)(2,1)S(1)}, bf16[256,256]{1,0:T(8,128)(2,1)S(1)}, u32[]{:S(2)}, u32[]{:S(2)}) collective-permute-start(bf16[256,256]{1,0:T(8,128)(2,1)S(1)} %get-tuple-element.9), channel_id=1, source_target_pairs={{0,64},{32,96},{64,0},{96,32},{1,65},{33,97},{65,1},{97,33},{2,66}... | collective-permute-start | bytes 393224 | tf_op jit(solution)/shard_map/ppermute | solution.py:50
  39.2 6.2 %collective-permute-start.5 = (bf16[256,256]{1,0:T(8,128)(2,1)S(1)}, bf16[256,256]{1,0:T(8,128)(2,1)S(1)}, u32[]{:S(2)}, u32[]{:S(2)}) collective-permute-start(bf16[256,256]{1,0:T(8,128)(2,1)S(1)} %get-tuple-element.10), channel_id=1, source_target_pairs={{0,32},{32,64},{64,96},{96,0},{1,33},{33,65},{65,97},{97,1},{2,34}... | collective-permute-start | bytes 393224 | tf_op jit(solution)/shard_map/ppermute | solution.py:50
  46.3 14.1 %collective-permute-start.4 = (bf16[1024,256]{1,0:T(8,128)(2,1)S(1)}, bf16[1024,256]{1,0:T(8,128)(2,1)S(1)}, u32[]{:S(2)}, u32[]{:S(2)}) collective-permute-start(bf16[1024,256]{1,0:T(8,128)(2,1)S(1)} %bitcast.43), channel_id=1, source_target_pairs={{0,96},{32,0},{64,32},{96,64},{1,97},{33,1},{65,33},{97,65},{2,98}... | collective-permute-start | bytes 1572872 | tf_op jit(solution)/shard_map/ppermute | solution.py:51
  46.6 15.2 %collective-permute-start.3 = (bf16[1024,256]{1,0:T(8,128)(2,1)S(1)}, bf16[1024,256]{1,0:T(8,128)(2,1)S(1)}, u32[]{:S(2)}, u32[]{:S(2)}) collective-permute-start(bf16[1024,256]{1,0:T(8,128)(2,1)S(1)} %bitcast.44), channel_id=1, source_target_pairs={{0,64},{32,96},{64,0},{96,32},{1,65},{33,97},{65,1},{97,33},{2,66}... | collective-permute-start | bytes 1572872 | tf_op jit(solution)/shard_map/ppermute | solution.py:51
  47.1 24.9 %collective-permute-start.2 = (bf16[1024,256]{1,0:T(8,128)(2,1)S(1)}, bf16[1024,256]{1,0:T(8,128)(2,1)S(1)}, u32[]{:S(2)}, u32[]{:S(2)}) collective-permute-start(bf16[1024,256]{1,0:T(8,128)(2,1)S(1)} %bitcast.45), channel_id=1, source_target_pairs={{0,32},{32,64},{64,96},{96,0},{1,33},{33,65},{65,97},{97,1},{2,34}... | collective-permute-start | bytes 1572872 | tf_op jit(solution)/shard_map/ppermute | solution.py:51
Sparse Core Ops, SparseCore 0:
  46.4 75.6 all-gather.2

commit v5 on v4

--- a/solution.py
+++ b/solution.py
@@ -1,6 +1,8 @@
 import jax
 import jax.numpy as jnp
 from jax import lax
+from jax.experimental import pallas as pl
+from jax.experimental.pallas import tpu as pltpu
 from jax.sharding import Mesh, PartitionSpec as P
 
 
@@ -30,14 +32,38 @@
     extended = with_halo(occ_coeff, ((ROW, 0),), rows_local)
     coeff_blocks = extended.reshape(3 * blocks_local, block_size, orbitals)
     local_index = tile_blocks - (row_index - 1) * blocks_local
-    picked = jnp.take(coeff_blocks, local_index, axis=0)
-    keep_mask = screen_mask.astype(jnp.bfloat16)
-    tiles_five = b_tiles.reshape(p_local, blocks_local, block_size, slot_count, block_size)
-    masked = picked * keep_mask[:, :, None, None]
-    half_sum = jnp.einsum(
-        "pbmsn,bsni->pbmi", tiles_five, masked, preferred_element_type=jnp.float32
-    )
-    half_local = half_sum.astype(jnp.bfloat16).reshape(p_local, rows_local, orbitals)
+    window = coeff_blocks.shape[0]
+    local_index = jnp.clip(local_index, 0, window - 1).astype(jnp.int32)
+    tiles = b_tiles.reshape(rows_local, stored)
+    extended = extended.reshape(window * block_size, orbitals)
+
+    def kernel(index_ref, mask_ref, tile_ref, coeff_ref, out_ref, acc_ref):
+        b = pl.program_id(0)
+        acc_ref[...] = jnp.zeros_like(acc_ref)
+        for s in range(slot_count):
+            @pl.when(mask_ref[b, s] != 0)
+            def _():
+                start = pl.multiple_of(index_ref[b, s] * block_size, block_size)
+                coeff = coeff_ref[pl.ds(start, block_size), :]
+                tile = tile_ref[:, s * block_size:(s + 1) * block_size]
+                acc_ref[...] += jnp.dot(tile, coeff, preferred_element_type=jnp.float32)
+        out_ref[...] = acc_ref[...].astype(out_ref.dtype)
+
+    half_local = pl.pallas_call(
+        kernel,
+        grid_spec=pltpu.PrefetchScalarGridSpec(
+            num_scalar_prefetch=2,
+            grid=(blocks_local,),
+            in_specs=[
+                pl.BlockSpec((block_size, stored), lambda b, li, mk: (b, 0)),
+                pl.BlockSpec((window * block_size, orbitals), lambda b, li, mk: (0, 0)),
+            ],
+            out_specs=pl.BlockSpec((block_size, orbitals), lambda b, li, mk: (b, 0)),
+            scratch_shapes=[pltpu.VMEM((block_size, orbitals), jnp.float32)],
+        ),
+        out_shape=jax.ShapeDtypeStruct((rows_local, orbitals), jnp.bfloat16),
+    )(local_index, screen_mask, tiles, extended)
+    half_local = half_local.reshape(p_local, rows_local, orbitals)
     aux_index = lax.axis_index("aux")
     share = rows_local // aux_count
     own = half_local[0]

time: 171 us -> 182 us (1.064)
  Pallas kernels: 0 us -> 19.8 us
  local copies, waits for them, and re-layouts: 30.4 us -> 19 us
  matrix products: 31.2 us -> 23.5 us
  waiting for transfers between devices: 81.6 us -> 86.6 us
  starting transfers between devices: 11.7 us -> 14.6 us
  other arithmetic: 2.35 us -> 4.42 us
    pallas_call x0 -> x1, Pallas kernels: none -> 19.8 us  [per_device(): pl.pallas_call(kernel, grid_spec=pltpu.PrefetchScalarGridSpec(num_scalar_...]
    ppermute x3, waiting for transfers between devices: 24.2 us -> 14.8 us  [per_device(): shifted.append(lax.ppermute(own, 'aux', pairs))]
    dot_general x1 -> x0, matrix products: 7.35 us -> none  [per_device(): jnp.einsum('pbmsn,bsni->pbmi', tiles_five, masked, preferred_element_type...]
    gather x1 -> x0, local copies, waits for them, and re-layouts: 6.74 us -> none  [per_device(): picked = jnp.take(coeff_blocks, local_index, axis=0)]
    all_gather x1, waiting for transfers between devices: 50.1 us -> 56.8 us  [per_device(): partner = lax.all_gather(piece, ROW, axis=0)]
    unnamed x3 -> x0, local copies, waits for them, and re-layouts: 5.62 us -> none
    ppermute x1, waiting for transfers between devices: 0.01 us -> 3.16 us  [with_halo(): lax.ppermute(lax.slice_in_dim(block, block.shape[dim] - width, None, axis...]
    ppermute x3, starting transfers between devices: 1.54 us -> 4.39 us  [per_device(): shifted.append(lax.ppermute(own, 'aux', pairs))]
  transfers between devices with their start and end apart: 9 -> 9, of which waited for: 8 -> 8; matrix products, arithmetic and copies ran while one was open for 4% -> 1% of each run, Pallas kernels for 0% -> 0%
where the time goes in v5:
time: 182 us; the launch traced here: 181 us
  waiting for transfers between devices  86.6 us (48%)
  matrix products  23.5 us (13%)
  Pallas kernels  19.8 us (11%)
  local copies, waits for them, and re-layouts  19 us (10%)
  starting transfers between devices  14.6 us (8%)
  between operations  13.5 us (7%)
  other arithmetic  4.42 us (2%)
    all_gather x1, waiting for transfers between devices, per_device(): partner = lax.all_gather(piece, ROW, axis=0)  56.8 us
    dot_general x1, matrix products, per_device(): jnp.einsum('pmi,rpki->mrk', slab_rows, partner, preferred_element_type=jn...  23.5 us
    pallas_call x1, Pallas kernels, per_device(): pl.pallas_call(kernel, grid_spec=pltpu.PrefetchScalarGridSpec(num_scalar_...  19.8 us
    reshape x1, local copies, waits for them, and re-layouts, per_device(): result.astype(jnp.bfloat16).reshape(rows_local, partner.shape[0], 1, share)  17.9 us
    ppermute x3, waiting for transfers between devices, per_device(): shifted.append(lax.ppermute(own, 'aux', pairs))  14.8 us
    ppermute x3, waiting for transfers between devices, per_device(): pieces.append(lax.ppermute(outgoing, 'aux', pairs))  7.51 us
    ppermute x1, starting transfers between devices, with_halo(): lax.ppermute(lax.slice_in_dim(block, block.shape[dim] - width, None, axis...  4.58 us
    ppermute x3, starting transfers between devices, per_device(): shifted.append(lax.ppermute(own, 'aux', pairs))  4.39 us
  transfers between devices with their start and end apart: 9, of which 8 were waited for; matrix products, arithmetic and copies ran while one was open for 1% of the time, Pallas kernels for 0%

profile of v5, /device:TPU:1, one launch (start us, length us, event | category | flops | bytes accessed | tf_op | source)
XLA Modules:
  0.0 181.3 jit_solution(455280412773604866)
XLA Ops:
  6.5 0.0 all-gather.3.cloned.1.call-start
  6.5 4.6 %collective-permute-start = (bf16[1024,256]{1,0:T(8,128)(2,1)}, bf16[1024,256]{1,0:T(8,128)(2,1)S(1)}, u32[]{:S(2)}, u32[]{:S(2)}) collective-permute-start(bf16[1024,256]{1,0:T(8,128)(2,1)} %param.5), channel_id=1, source_target_pairs={{0,1},{1,2},{2,3},{3,4},{4,5},{5,6},{6,7},{7,8},{8,9},{9,10},{10,1... | collective-permute-start | bytes 1572872 | tf_op jit(solution)/shard_map/ppermute | solution.py:14
  11.1 1.9 %collective-permute-start.1 = (bf16[1024,256]{1,0:T(8,128)(2,1)}, bf16[1024,256]{1,0:T(8,128)(2,1)S(1)}, u32[]{:S(2)}, u32[]{:S(2)}) collective-permute-start(bf16[1024,256]{1,0:T(8,128)(2,1)} %param.5), channel_id=1, source_target_pairs={{1,0},{2,1},{3,2},{4,3},{5,4},{6,5},{7,6},{8,7},{9,8},{10,9},{11,1... | collective-permute-start | bytes 1572872 | tf_op jit(solution)/shard_map/ppermute | solution.py:17
  13.1 1.3 subtract_clamp_fusion.index_ref
  14.4 3.2 %collective-permute-done = bf16[1024,256]{1,0:T(8,128)(2,1)S(1)} collective-permute-done((bf16[1024,256]{1,0:T(8,128)(2,1)}, bf16[1024,256]{1,0:T(8,128)(2,1)S(1)}, u32[]{:S(2)}, u32[]{:S(2)}) %collective-permute-start) | collective-permute-done | bytes 524320 | tf_op jit(solution)/shard_map/ppermute | solution.py:14
  17.6 4.3 %collective-permute-done.1 = bf16[1024,256]{1,0:T(8,128)(2,1)S(1)} collective-permute-done((bf16[1024,256]{1,0:T(8,128)(2,1)}, bf16[1024,256]{1,0:T(8,128)(2,1)S(1)}, u32[]{:S(2)}, u32[]{:S(2)}) %collective-permute-start.1) | collective-permute-done | bytes 524320 | tf_op jit(solution)/shard_map/ppermute | solution.py:17
  21.8 2.3 %pad_maximum_fusion.coeff_ref = bf16[3072,256]{1,0:T(8,128)(2,1)} fusion(bf16[1024,256]{1,0:T(8,128)(2,1)S(1)} %collective-permute-done.1, bf16[1024,256]{1,0:T(8,128)(2,1)} %param.5, bf16[1024,256]{1,0:T(8,128)(2,1)S(1)} %collective-permute-done), kind=kLoop, calls=%fused_computation.9 | loop fusion | flops 4718592 | bytes 3145728 | tf_op jit(solution)/shard_map/concatenate | solution.py:18
  24.1 19.8 %shard_map.46 = bf16[1024,256]{1,0:T(8,128)(2,1)} custom-call(s32[8,16]{1,0:T(8,128)} %subtract_clamp_fusion.index_ref, s32[8,16]{1,0:T(8,128)} %mask_ref.1, bf16[1024,2048]{1,0:T(8,128)(2,1)} %bitcast.22, bf16[3072,256]{1,0:T(8,128)(2,1)} %pad_maximum_fusion.coeff_ref), custom_call_target="tpu_custom_call" | custom-call | tf_op jit(solution)/shard_map/pallas_call | solution.py:52
  43.9 1.1 dynamic-slice_bitcast_fusion
  45.0 2.5 %collective-permute-start.7 = (bf16[256,256]{1,0:T(8,128)(2,1)S(1)}, bf16[256,256]{1,0:T(8,128)(2,1)S(1)}, u32[]{:S(2)}, u32[]{:S(2)}) collective-permute-start(bf16[256,256]{1,0:T(8,128)(2,1)S(1)} %get-tuple-element.6), channel_id=1, source_target_pairs={{0,96},{32,0},{64,32},{96,64},{1,97},{33,1},{65,33},{97,65},{2,98}... | collective-permute-start | bytes 393224 | tf_op jit(solution)/shard_map/ppermute | solution.py:76
  47.6 0.5 collective-permute-start.6
  48.1 0.6 collective-permute-start.5
  48.7 2.0 %collective-permute-done.7 = bf16[256,256]{1,0:T(8,128)(2,1)S(1)} collective-permute-done((bf16[256,256]{1,0:T(8,128)(2,1)S(1)}, bf16[256,256]{1,0:T(8,128)(2,1)S(1)}, u32[]{:S(2)}, u32[]{:S(2)}) %collective-permute-start.7) | collective-permute-done | bytes 131104 | tf_op jit(solution)/shard_map/ppermute | solution.py:76
  50.7 3.7 %collective-permute-done.6 = bf16[256,256]{1,0:T(8,128)(2,1)S(1)} collective-permute-done((bf16[256,256]{1,0:T(8,128)(2,1)S(1)}, bf16[256,256]{1,0:T(8,128)(2,1)S(1)}, u32[]{:S(2)}, u32[]{:S(2)}) %collective-permute-start.6) | collective-permute-done | bytes 131104 | tf_op jit(solution)/shard_map/ppermute | solution.py:76
  54.4 1.8 %collective-permute-done.5 = bf16[256,256]{1,0:T(8,128)(2,1)S(1)} collective-permute-done((bf16[256,256]{1,0:T(8,128)(2,1)S(1)}, bf16[256,256]{1,0:T(8,128)(2,1)S(1)}, u32[]{:S(2)}, u32[]{:S(2)}) %collective-permute-start.5) | collective-permute-done | bytes 131104 | tf_op jit(solution)/shard_map/ppermute | solution.py:76
  56.2 0.9 pad_maximum_fusion.1
  57.1 0.0 all-gather.3.cloned.1.call-update
  57.1 3.7 %collective-permute-start.4 = (bf16[1024,256]{1,0:T(8,128)(2,1)}, bf16[1024,256]{1,0:T(8,128)(2,1)S(1)}, u32[]{:S(2)}, u32[]{:S(2)}) collective-permute-start(bf16[1024,256]{1,0:T(8,128)(2,1)} %shard_map.46), channel_id=1, source_target_pairs={{0,96},{32,0},{64,32},{96,64},{1,97},{33,1},{65,33},{97,65},{2,98}... | collective-permute-start | bytes 1572872 | tf_op jit(solution)/shard_map/ppermute | solution.py:77
  60.8 0.0 collective-permute-start.3
  60.8 0.7 collective-permute-start.2
  61.5 11.4 %collective-permute-done.4 = bf16[1024,256]{1,0:T(8,128)(2,1)S(1)} collective-permute-done((bf16[1024,256]{1,0:T(8,128)(2,1)}, bf16[1024,256]{1,0:T(8,128)(2,1)S(1)}, u32[]{:S(2)}, u32[]{:S(2)}) %collective-permute-start.4) | collective-permute-done | bytes 524320 | tf_op jit(solution)/shard_map/ppermute | solution.py:77
  72.9 0.0 collective-permute-done.3
  72.9 3.4 %collective-permute-done.2 = bf16[1024,256]{1,0:T(8,128)(2,1)S(1)} collective-permute-done((bf16[1024,256]{1,0:T(8,128)(2,1)}, bf16[1024,256]{1,0:T(8,128)(2,1)S(1)}, u32[]{:S(2)}, u32[]{:S(2)}) %collective-permute-start.2) | collective-permute-done | bytes 524320 | tf_op jit(solution)/shard_map/ppermute | solution.py:77
  76.3 56.8 %all-gather.3.cloned.1.call-done = bf16[128,256,256]{2,1,0:T(8,128)(2,1)} async-done(((bf16[4,256,256]{2,1,0:T(8,128)(2,1)}), bf16[128,256,256]{2,1,0:T(8,128)(2,1)}) %all-gather.3.cloned.1.call-update) | async-done | bytes 16777232 | tf_op jit(solution)/shard_map/all_gather | solution.py:80
  133.1 23.5 %fusion = bf16[1024,32,1,256]{3,0,1,2:T(8,128)(2,1)} fusion(bf16[32,4,256,256]{3,2,1,0:T(8,128)(2,1)} %bitcast.27, bf16[1,1024,256]{2,1,0:T(8,128)(2,1)S(1)} %bitcast.28, bf16[1,1024,256]{2,1,0:T(8,128)(2,1)S(1)} %bitcast.29, bf16[1,1024,256]{2,1,0:T(8,128)(2,1)S(1)} %bitcast.30, bf16[1,1024,256]{2,1,0:T(8,128)(2,1)} %bitcast.23), kind=kOutput, calls=%fused_computation.1 | convolution fusion | flops 17196646400 | bytes 35651584 | tf_op jit(solution)/shard_map/pmi,rpki->mrk/dot_general | solution.py:81
  156.6 17.9 %copy.6 = bf16[1024,32,1,256]{3,1,2,0:T(8,128)(2,1)} copy(bf16[1024,32,1,256]{3,0,1,2:T(8,128)(2,1)} %fusion) | data formatting | bytes 33554432 | tf_op jit(solution)/shard_map/reshape | solution.py:82
Async XLA Ops:
  6.5 126.5 %all-gather.3.cloned.1.call-start = ((), (), s32[]{:S(2)}) async-start(), calls=%async_computation | async-start | bytes 17301504 | tf_op jit(solution)/shard_map/all_gather | solution.py:80
  6.5 11.0 %collective-permute-start = (bf16[1024,256]{1,0:T(8,128)(2,1)}, bf16[1024,256]{1,0:T(8,128)(2,1)S(1)}, u32[]{:S(2)}, u32[]{:S(2)}) collective-permute-start(bf16[1024,256]{1,0:T(8,128)(2,1)} %param.5), channel_id=1, source_target_pairs={{0,1},{1,2},{2,3},{3,4},{4,5},{5,6},{6,7},{7,8},{8,9},{9,10},{10,1... | collective-permute-start | bytes 1572872 | tf_op jit(solution)/shard_map/ppermute | solution.py:14
  11.1 10.7 %collective-permute-start.1 = (bf16[1024,256]{1,0:T(8,128)(2,1)}, bf16[1024,256]{1,0:T(8,128)(2,1)S(1)}, u32[]{:S(2)}, u32[]{:S(2)}) collective-permute-start(bf16[1024,256]{1,0:T(8,128)(2,1)} %param.5), channel_id=1, source_target_pairs={{1,0},{2,1},{3,2},{4,3},{5,4},{6,5},{7,6},{8,7},{9,8},{10,9},{11,1... | collective-permute-start | bytes 1572872 | tf_op jit(solution)/shard_map/ppermute | solution.py:17
  45.0 5.7 %collective-permute-start.7 = (bf16[256,256]{1,0:T(8,128)(2,1)S(1)}, bf16[256,256]{1,0:T(8,128)(2,1)S(1)}, u32[]{:S(2)}, u32[]{:S(2)}) collective-permute-start(bf16[256,256]{1,0:T(8,128)(2,1)S(1)} %get-tuple-element.6), channel_id=1, source_target_pairs={{0,96},{32,0},{64,32},{96,64},{1,97},{33,1},{65,33},{97,65},{2,98}... | collective-permute-start | bytes 393224 | tf_op jit(solution)/shard_map/ppermute | solution.py:76
  47.6 6.8 %collective-permute-start.6 = (bf16[256,256]{1,0:T(8,128)(2,1)S(1)}, bf16[256,256]{1,0:T(8,128)(2,1)S(1)}, u32[]{:S(2)}, u32[]{:S(2)}) collective-permute-start(bf16[256,256]{1,0:T(8,128)(2,1)S(1)} %get-tuple-element.7), channel_id=1, source_target_pairs={{0,64},{32,96},{64,0},{96,32},{1,65},{33,97},{65,1},{97,33},{2,66}... | collective-permute-start | bytes 393224 | tf_op jit(solution)/shard_map/ppermute | solution.py:76
  48.1 8.1 %collective-permute-start.5 = (bf16[256,256]{1,0:T(8,128)(2,1)S(1)}, bf16[256,256]{1,0:T(8,128)(2,1)S(1)}, u32[]{:S(2)}, u32[]{:S(2)}) collective-permute-start(bf16[256,256]{1,0:T(8,128)(2,1)S(1)} %get-tuple-element.8), channel_id=1, source_target_pairs={{0,32},{32,64},{64,96},{96,0},{1,33},{33,65},{65,97},{97,1},{2,34}... | collective-permute-start | bytes 393224 | tf_op jit(solution)/shard_map/ppermute | solution.py:76
  57.1 15.8 %collective-permute-start.4 = (bf16[1024,256]{1,0:T(8,128)(2,1)}, bf16[1024,256]{1,0:T(8,128)(2,1)S(1)}, u32[]{:S(2)}, u32[]{:S(2)}) collective-permute-start(bf16[1024,256]{1,0:T(8,128)(2,1)} %shard_map.46), channel_id=1, source_target_pairs={{0,96},{32,0},{64,32},{96,64},{1,97},{33,1},{65,33},{97,65},{2,98}... | collective-permute-start | bytes 1572872 | tf_op jit(solution)/shard_map/ppermute | solution.py:77
  60.8 12.1 %collective-permute-start.3 = (bf16[1024,256]{1,0:T(8,128)(2,1)}, bf16[1024,256]{1,0:T(8,128)(2,1)S(1)}, u32[]{:S(2)}, u32[]{:S(2)}) collective-permute-start(bf16[1024,256]{1,0:T(8,128)(2,1)} %shard_map.46), channel_id=1, source_target_pairs={{0,64},{32,96},{64,0},{96,32},{1,65},{33,97},{65,1},{97,33},{2,66}... | collective-permute-start | bytes 1572872 | tf_op jit(solution)/shard_map/ppermute | solution.py:77
  60.8 15.5 %collective-permute-start.2 = (bf16[1024,256]{1,0:T(8,128)(2,1)}, bf16[1024,256]{1,0:T(8,128)(2,1)S(1)}, u32[]{:S(2)}, u32[]{:S(2)}) collective-permute-start(bf16[1024,256]{1,0:T(8,128)(2,1)} %shard_map.46), channel_id=1, source_target_pairs={{0,32},{32,64},{64,96},{96,0},{1,33},{33,65},{65,97},{97,1},{2,34}... | collective-permute-start | bytes 1572872 | tf_op jit(solution)/shard_map/ppermute | solution.py:77
Sparse Core Ops, SparseCore 0:
  57.2 75.7 all-gather.2

commit v6 on v5

--- a/solution.py
+++ b/solution.py
@@ -37,17 +37,16 @@
     tiles = b_tiles.reshape(rows_local, stored)
     extended = extended.reshape(window * block_size, orbitals)
 
-    def kernel(index_ref, mask_ref, tile_ref, coeff_ref, out_ref, acc_ref):
+    def kernel(index_ref, mask_ref, tile_ref, coeff_ref, out_ref):
         b = pl.program_id(0)
-        acc_ref[...] = jnp.zeros_like(acc_ref)
+        acc = jnp.zeros(out_ref.shape, jnp.float32)
         for s in range(slot_count):
-            @pl.when(mask_ref[b, s] != 0)
-            def _():
-                start = pl.multiple_of(index_ref[b, s] * block_size, block_size)
-                coeff = coeff_ref[pl.ds(start, block_size), :]
-                tile = tile_ref[:, s * block_size:(s + 1) * block_size]
-                acc_ref[...] += jnp.dot(tile, coeff, preferred_element_type=jnp.float32)
-        out_ref[...] = acc_ref[...].astype(out_ref.dtype)
+            start = pl.multiple_of(index_ref[b, s] * block_size, block_size)
+            coeff = coeff_ref[pl.ds(start, block_size), :]
+            coeff = jnp.where(mask_ref[b, s] != 0, coeff, jnp.zeros_like(coeff))
+            tile = tile_ref[:, s * block_size:(s + 1) * block_size]
+            acc = acc + jnp.dot(tile, coeff, preferred_element_type=jnp.float32)
+        out_ref[...] = acc.astype(out_ref.dtype)
 
     half_local = pl.pallas_call(
         kernel,
@@ -59,7 +58,6 @@
                 pl.BlockSpec((window * block_size, orbitals), lambda b, li, mk: (0, 0)),
             ],
             out_specs=pl.BlockSpec((block_size, orbitals), lambda b, li, mk: (b, 0)),
-            scratch_shapes=[pltpu.VMEM((block_size, orbitals), jnp.float32)],
         ),
         out_shape=jax.ShapeDtypeStruct((rows_local, orbitals), jnp.bfloat16),
     )(local_index, screen_mask, tiles, extended)

time: 182 us -> 173 us (0.951)
  Pallas kernels: 19.8 us -> 8.64 us
  waiting for transfers between devices: 86.6 us -> 91 us
  starting transfers between devices: 14.6 us -> 11.9 us
    pallas_call x1, Pallas kernels: 19.8 us -> 8.64 us  [per_device(): pl.pallas_call(kernel, grid_spec=pltpu.PrefetchScalarGridSpec(num_scalar_...]
    ppermute x3, waiting for transfers between devices: 14.8 us -> 21.1 us  [per_device(): shifted.append(lax.ppermute(own, 'aux', pairs))]
    ppermute x3, starting transfers between devices: 4.39 us -> 1.75 us  [per_device(): shifted.append(lax.ppermute(own, 'aux', pairs))]
    ppermute x3, waiting for transfers between devices: 7.51 us -> 5.6 us  [per_device(): pieces.append(lax.ppermute(outgoing, 'aux', pairs))]
  transfers between devices with their start and end apart: 9 -> 9, of which waited for: 8 -> 9; matrix products, arithmetic and copies ran while one was open for 1% -> 1% of each run, Pallas kernels for 0% -> 0%
where the time goes in v6:
time: 173 us; the launch traced here: 172 us
  waiting for transfers between devices  91 us (53%)
  matrix products  23.5 us (14%)
  local copies, waits for them, and re-layouts  19 us (11%)
  between operations  13.5 us (8%)
  starting transfers between devices  11.9 us (7%)
  Pallas kernels  8.64 us (5%)
  other arithmetic  4.42 us (3%)
    all_gather x1, waiting for transfers between devices, per_device(): partner = lax.all_gather(piece, ROW, axis=0)  56.9 us
    dot_general x1, matrix products, per_device(): jnp.einsum('pmi,rpki->mrk', slab_rows, partner, preferred_element_type=jn...  23.5 us
    ppermute x3, waiting for transfers between devices, per_device(): shifted.append(lax.ppermute(own, 'aux', pairs))  21.1 us
    reshape x1, local copies, waits for them, and re-layouts, per_device(): result.astype(jnp.bfloat16).reshape(rows_local, partner.shape[0], 1, share)  17.9 us
    pallas_call x1, Pallas kernels, per_device(): pl.pallas_call(kernel, grid_spec=pltpu.PrefetchScalarGridSpec(num_scalar_...  8.64 us
    ppermute x3, waiting for transfers between devices, per_device(): pieces.append(lax.ppermute(outgoing, 'aux', pairs))  5.6 us
    ppermute x1, starting transfers between devices, with_halo(): lax.ppermute(lax.slice_in_dim(block, block.shape[dim] - width, None, axis...  4.58 us
    ppermute x1, waiting for transfers between devices, with_halo(): lax.ppermute(lax.slice_in_dim(block, 0, width, axis=dim), axis, backward)  4.29 us
  transfers between devices with their start and end apart: 9, of which 9 were waited for; matrix products, arithmetic and copies ran while one was open for 1% of the time, Pallas kernels for 0%

profile of v6, /device:TPU:1, one launch (start us, length us, event | category | flops | bytes accessed | tf_op | source)
XLA Modules:
  0.0 172.0 jit_solution(7694357668317119176)
XLA Ops:
  6.5 0.0 all-gather.3.cloned.1.call-start
  6.5 4.6 %collective-permute-start = (bf16[1024,256]{1,0:T(8,128)(2,1)}, bf16[1024,256]{1,0:T(8,128)(2,1)S(1)}, u32[]{:S(2)}, u32[]{:S(2)}) collective-permute-start(bf16[1024,256]{1,0:T(8,128)(2,1)} %param.5), channel_id=1, source_target_pairs={{0,1},{1,2},{2,3},{3,4},{4,5},{5,6},{6,7},{7,8},{8,9},{9,10},{10,1... | collective-permute-start | bytes 1572872 | tf_op jit(solution)/shard_map/ppermute | solution.py:14
  11.1 1.9 %collective-permute-start.1 = (bf16[1024,256]{1,0:T(8,128)(2,1)}, bf16[1024,256]{1,0:T(8,128)(2,1)S(1)}, u32[]{:S(2)}, u32[]{:S(2)}) collective-permute-start(bf16[1024,256]{1,0:T(8,128)(2,1)} %param.5), channel_id=1, source_target_pairs={{1,0},{2,1},{3,2},{4,3},{5,4},{6,5},{7,6},{8,7},{9,8},{10,9},{11,1... | collective-permute-start | bytes 1572872 | tf_op jit(solution)/shard_map/ppermute | solution.py:17
  13.1 1.3 subtract_clamp_fusion.index_ref
  14.4 3.2 %collective-permute-done = bf16[1024,256]{1,0:T(8,128)(2,1)S(1)} collective-permute-done((bf16[1024,256]{1,0:T(8,128)(2,1)}, bf16[1024,256]{1,0:T(8,128)(2,1)S(1)}, u32[]{:S(2)}, u32[]{:S(2)}) %collective-permute-start) | collective-permute-done | bytes 524320 | tf_op jit(solution)/shard_map/ppermute | solution.py:14
  17.6 4.3 %collective-permute-done.1 = bf16[1024,256]{1,0:T(8,128)(2,1)S(1)} collective-permute-done((bf16[1024,256]{1,0:T(8,128)(2,1)}, bf16[1024,256]{1,0:T(8,128)(2,1)S(1)}, u32[]{:S(2)}, u32[]{:S(2)}) %collective-permute-start.1) | collective-permute-done | bytes 524320 | tf_op jit(solution)/shard_map/ppermute | solution.py:17
  21.8 2.3 %pad_maximum_fusion.coeff_ref = bf16[3072,256]{1,0:T(8,128)(2,1)} fusion(bf16[1024,256]{1,0:T(8,128)(2,1)S(1)} %collective-permute-done.1, bf16[1024,256]{1,0:T(8,128)(2,1)} %param.5, bf16[1024,256]{1,0:T(8,128)(2,1)S(1)} %collective-permute-done), kind=kLoop, calls=%fused_computation.9 | loop fusion | flops 4718592 | bytes 3145728 | tf_op jit(solution)/shard_map/concatenate | solution.py:18
  24.1 8.6 %shard_map.46 = bf16[1024,256]{1,0:T(8,128)(2,1)} custom-call(s32[8,16]{1,0:T(8,128)} %subtract_clamp_fusion.index_ref, s32[8,16]{1,0:T(8,128)} %mask_ref.1, bf16[1024,2048]{1,0:T(8,128)(2,1)} %bitcast.22, bf16[3072,256]{1,0:T(8,128)(2,1)} %pad_maximum_fusion.coeff_ref), custom_call_target="tpu_custom_call" | custom-call | tf_op jit(solution)/shard_map/pallas_call | solution.py:51
  32.8 1.1 dynamic-slice_bitcast_fusion
  33.9 2.5 %collective-permute-start.7 = (bf16[256,256]{1,0:T(8,128)(2,1)S(1)}, bf16[256,256]{1,0:T(8,128)(2,1)S(1)}, u32[]{:S(2)}, u32[]{:S(2)}) collective-permute-start(bf16[256,256]{1,0:T(8,128)(2,1)S(1)} %get-tuple-element.6), channel_id=1, source_target_pairs={{0,96},{32,0},{64,32},{96,64},{1,97},{33,1},{65,33},{97,65},{2,98}... | collective-permute-start | bytes 393224 | tf_op jit(solution)/shard_map/ppermute | solution.py:74
  36.4 0.5 collective-permute-start.6
  37.0 0.6 collective-permute-start.5
  37.6 2.2 %collective-permute-done.7 = bf16[256,256]{1,0:T(8,128)(2,1)S(1)} collective-permute-done((bf16[256,256]{1,0:T(8,128)(2,1)S(1)}, bf16[256,256]{1,0:T(8,128)(2,1)S(1)}, u32[]{:S(2)}, u32[]{:S(2)}) %collective-permute-start.7) | collective-permute-done | bytes 131104 | tf_op jit(solution)/shard_map/ppermute | solution.py:74
  39.8 2.1 %collective-permute-done.6 = bf16[256,256]{1,0:T(8,128)(2,1)S(1)} collective-permute-done((bf16[256,256]{1,0:T(8,128)(2,1)S(1)}, bf16[256,256]{1,0:T(8,128)(2,1)S(1)}, u32[]{:S(2)}, u32[]{:S(2)}) %collective-permute-start.6) | collective-permute-done | bytes 131104 | tf_op jit(solution)/shard_map/ppermute | solution.py:74
  41.9 1.3 collective-permute-done.5
  43.2 0.9 pad_maximum_fusion.1
  44.0 0.0 all-gather.3.cloned.1.call-update
  44.1 0.6 collective-permute-start.4
  44.7 0.5 collective-permute-start.3
  45.2 0.6 collective-permute-start.2
  45.8 12.5 %collective-permute-done.4 = bf16[1024,256]{1,0:T(8,128)(2,1)S(1)} collective-permute-done((bf16[1024,256]{1,0:T(8,128)(2,1)}, bf16[1024,256]{1,0:T(8,128)(2,1)S(1)}, u32[]{:S(2)}, u32[]{:S(2)}) %collective-permute-start.4) | collective-permute-done | bytes 524320 | tf_op jit(solution)/shard_map/ppermute | solution.py:75
  58.3 1.8 %collective-permute-done.3 = bf16[1024,256]{1,0:T(8,128)(2,1)S(1)} collective-permute-done((bf16[1024,256]{1,0:T(8,128)(2,1)}, bf16[1024,256]{1,0:T(8,128)(2,1)S(1)}, u32[]{:S(2)}, u32[]{:S(2)}) %collective-permute-start.3) | collective-permute-done | bytes 524320 | tf_op jit(solution)/shard_map/ppermute | solution.py:75
  60.1 6.8 %collective-permute-done.2 = bf16[1024,256]{1,0:T(8,128)(2,1)S(1)} collective-permute-done((bf16[1024,256]{1,0:T(8,128)(2,1)}, bf16[1024,256]{1,0:T(8,128)(2,1)S(1)}, u32[]{:S(2)}, u32[]{:S(2)}) %collective-permute-start.2) | collective-permute-done | bytes 524320 | tf_op jit(solution)/shard_map/ppermute | solution.py:75
  66.9 56.9 %all-gather.3.cloned.1.call-done = bf16[128,256,256]{2,1,0:T(8,128)(2,1)} async-done(((bf16[4,256,256]{2,1,0:T(8,128)(2,1)}), bf16[128,256,256]{2,1,0:T(8,128)(2,1)}) %all-gather.3.cloned.1.call-update) | async-done | bytes 16777232 | tf_op jit(solution)/shard_map/all_gather | solution.py:78
  123.7 23.5 %fusion = bf16[1024,32,1,256]{3,0,1,2:T(8,128)(2,1)} fusion(bf16[32,4,256,256]{3,2,1,0:T(8,128)(2,1)} %bitcast.27, bf16[1,1024,256]{2,1,0:T(8,128)(2,1)S(1)} %bitcast.28, bf16[1,1024,256]{2,1,0:T(8,128)(2,1)S(1)} %bitcast.29, bf16[1,1024,256]{2,1,0:T(8,128)(2,1)S(1)} %bitcast.30, bf16[1,1024,256]{2,1,0:T(8,128)(2,1)} %bitcast.23), kind=kOutput, calls=%fused_computation.1 | convolution fusion | flops 17196646400 | bytes 35651584 | tf_op jit(solution)/shard_map/pmi,rpki->mrk/dot_general | solution.py:79
  147.3 17.9 %copy.6 = bf16[1024,32,1,256]{3,1,2,0:T(8,128)(2,1)} copy(bf16[1024,32,1,256]{3,0,1,2:T(8,128)(2,1)} %fusion) | data formatting | bytes 33554432 | tf_op jit(solution)/shard_map/reshape | solution.py:80
Async XLA Ops:
  6.5 117.2 %all-gather.3.cloned.1.call-start = ((), (), s32[]{:S(2)}) async-start(), calls=%async_computation | async-start | bytes 17301504 | tf_op jit(solution)/shard_map/all_gather | solution.py:78
  6.5 11.0 %collective-permute-start = (bf16[1024,256]{1,0:T(8,128)(2,1)}, bf16[1024,256]{1,0:T(8,128)(2,1)S(1)}, u32[]{:S(2)}, u32[]{:S(2)}) collective-permute-start(bf16[1024,256]{1,0:T(8,128)(2,1)} %param.5), channel_id=1, source_target_pairs={{0,1},{1,2},{2,3},{3,4},{4,5},{5,6},{6,7},{7,8},{8,9},{9,10},{10,1... | collective-permute-start | bytes 1572872 | tf_op jit(solution)/shard_map/ppermute | solution.py:14
  11.1 10.7 %collective-permute-start.1 = (bf16[1024,256]{1,0:T(8,128)(2,1)}, bf16[1024,256]{1,0:T(8,128)(2,1)S(1)}, u32[]{:S(2)}, u32[]{:S(2)}) collective-permute-start(bf16[1024,256]{1,0:T(8,128)(2,1)} %param.5), channel_id=1, source_target_pairs={{1,0},{2,1},{3,2},{4,3},{5,4},{6,5},{7,6},{8,7},{9,8},{10,9},{11,1... | collective-permute-start | bytes 1572872 | tf_op jit(solution)/shard_map/ppermute | solution.py:17
  33.9 5.9 %collective-permute-start.7 = (bf16[256,256]{1,0:T(8,128)(2,1)S(1)}, bf16[256,256]{1,0:T(8,128)(2,1)S(1)}, u32[]{:S(2)}, u32[]{:S(2)}) collective-permute-start(bf16[256,256]{1,0:T(8,128)(2,1)S(1)} %get-tuple-element.6), channel_id=1, source_target_pairs={{0,96},{32,0},{64,32},{96,64},{1,97},{33,1},{65,33},{97,65},{2,98}... | collective-permute-start | bytes 393224 | tf_op jit(solution)/shard_map/ppermute | solution.py:74
  36.4 5.4 %collective-permute-start.6 = (bf16[256,256]{1,0:T(8,128)(2,1)S(1)}, bf16[256,256]{1,0:T(8,128)(2,1)S(1)}, u32[]{:S(2)}, u32[]{:S(2)}) collective-permute-start(bf16[256,256]{1,0:T(8,128)(2,1)S(1)} %get-tuple-element.7), channel_id=1, source_target_pairs={{0,64},{32,96},{64,0},{96,32},{1,65},{33,97},{65,1},{97,33},{2,66}... | collective-permute-start | bytes 393224 | tf_op jit(solution)/shard_map/ppermute | solution.py:74
  37.0 6.2 %collective-permute-start.5 = (bf16[256,256]{1,0:T(8,128)(2,1)S(1)}, bf16[256,256]{1,0:T(8,128)(2,1)S(1)}, u32[]{:S(2)}, u32[]{:S(2)}) collective-permute-start(bf16[256,256]{1,0:T(8,128)(2,1)S(1)} %get-tuple-element.8), channel_id=1, source_target_pairs={{0,32},{32,64},{64,96},{96,0},{1,33},{33,65},{65,97},{97,1},{2,34}... | collective-permute-start | bytes 393224 | tf_op jit(solution)/shard_map/ppermute | solution.py:74
  44.1 14.3 %collective-permute-start.4 = (bf16[1024,256]{1,0:T(8,128)(2,1)}, bf16[1024,256]{1,0:T(8,128)(2,1)S(1)}, u32[]{:S(2)}, u32[]{:S(2)}) collective-permute-start(bf16[1024,256]{1,0:T(8,128)(2,1)} %shard_map.46), channel_id=1, source_target_pairs={{0,96},{32,0},{64,32},{96,64},{1,97},{33,1},{65,33},{97,65},{2,98}... | collective-permute-start | bytes 1572872 | tf_op jit(solution)/shard_map/ppermute | solution.py:75
  44.7 15.4 %collective-permute-start.3 = (bf16[1024,256]{1,0:T(8,128)(2,1)}, bf16[1024,256]{1,0:T(8,128)(2,1)S(1)}, u32[]{:S(2)}, u32[]{:S(2)}) collective-permute-start(bf16[1024,256]{1,0:T(8,128)(2,1)} %shard_map.46), channel_id=1, source_target_pairs={{0,64},{32,96},{64,0},{96,32},{1,65},{33,97},{65,1},{97,33},{2,66}... | collective-permute-start | bytes 1572872 | tf_op jit(solution)/shard_map/ppermute | solution.py:75
  45.2 21.7 %collective-permute-start.2 = (bf16[1024,256]{1,0:T(8,128)(2,1)}, bf16[1024,256]{1,0:T(8,128)(2,1)S(1)}, u32[]{:S(2)}, u32[]{:S(2)}) collective-permute-start(bf16[1024,256]{1,0:T(8,128)(2,1)} %shard_map.46), channel_id=1, source_target_pairs={{0,32},{32,64},{64,96},{96,0},{1,33},{33,65},{65,97},{97,1},{2,34}... | collective-permute-start | bytes 1572872 | tf_op jit(solution)/shard_map/ppermute | solution.py:75
Sparse Core Ops, SparseCore 0:
  44.2 79.5 all-gather.2

commit v7 on v6

--- a/solution.py
+++ b/solution.py
@@ -6,17 +6,13 @@
 from jax.sharding import Mesh, PartitionSpec as P
 
 
-def with_halo(block, sides, width):
-    for axis, dim in sides:
-        count = lax.axis_size(axis)
-        forward = [(i, i + 1) for i in range(count - 1)]
-        backward = [(target, source) for source, target in forward]
-        low = lax.ppermute(
-            lax.slice_in_dim(block, block.shape[dim] - width, None, axis=dim), axis, forward
-        )
-        high = lax.ppermute(lax.slice_in_dim(block, 0, width, axis=dim), axis, backward)
-        block = jnp.concatenate([low, block, high], axis=dim)
-    return block
+def halo_pieces(block, axis, width):
+    count = lax.axis_size(axis)
+    forward = [(i, i + 1) for i in range(count - 1)]
+    backward = [(target, source) for source, target in forward]
+    low = lax.ppermute(lax.slice_in_dim(block, block.shape[0] - width, None, axis=0), axis, forward)
+    high = lax.ppermute(lax.slice_in_dim(block, 0, width, axis=0), axis, backward)
+    return low, high
 
 
 ROW = ("rzy", "core")
@@ -29,25 +25,30 @@
     orbitals = occ_coeff.shape[1]
     aux_count = lax.axis_size("aux")
     row_index = lax.axis_index(ROW)
-    extended = with_halo(occ_coeff, ((ROW, 0),), rows_local)
-    coeff_blocks = extended.reshape(3 * blocks_local, block_size, orbitals)
+    low, high = halo_pieces(occ_coeff, ROW, rows_local)
+    window = 3 * blocks_local
     local_index = tile_blocks - (row_index - 1) * blocks_local
-    window = coeff_blocks.shape[0]
     local_index = jnp.clip(local_index, 0, window - 1).astype(jnp.int32)
     tiles = b_tiles.reshape(rows_local, stored)
-    extended = extended.reshape(window * block_size, orbitals)
 
-    def kernel(index_ref, mask_ref, tile_ref, coeff_ref, out_ref):
+    def kernel(index_ref, mask_ref, tile_ref, low_ref, own_ref, high_ref, out_ref, coeff_ref, rhs_ref):
         b = pl.program_id(0)
-        acc = jnp.zeros(out_ref.shape, jnp.float32)
+
+        @pl.when(b == 0)
+        def _():
+            coeff_ref[0:rows_local, :] = low_ref[...]
+            coeff_ref[rows_local:2 * rows_local, :] = own_ref[...]
+            coeff_ref[2 * rows_local:3 * rows_local, :] = high_ref[...]
+
         for s in range(slot_count):
             start = pl.multiple_of(index_ref[b, s] * block_size, block_size)
             coeff = coeff_ref[pl.ds(start, block_size), :]
             coeff = jnp.where(mask_ref[b, s] != 0, coeff, jnp.zeros_like(coeff))
-            tile = tile_ref[:, s * block_size:(s + 1) * block_size]
-            acc = acc + jnp.dot(tile, coeff, preferred_element_type=jnp.float32)
+            rhs_ref[s * block_size:(s + 1) * block_size, :] = coeff
+        acc = jnp.dot(tile_ref[...], rhs_ref[...], preferred_element_type=jnp.float32)
         out_ref[...] = acc.astype(out_ref.dtype)
 
+    whole = pl.BlockSpec((rows_local, orbitals), lambda b, li, mk: (0, 0))
     half_local = pl.pallas_call(
         kernel,
         grid_spec=pltpu.PrefetchScalarGridSpec(
@@ -55,12 +56,19 @@
             grid=(blocks_local,),
             in_specs=[
                 pl.BlockSpec((block_size, stored), lambda b, li, mk: (b, 0)),
-                pl.BlockSpec((window * block_size, orbitals), lambda b, li, mk: (0, 0)),
+                whole,
+                whole,
+                whole,
             ],
             out_specs=pl.BlockSpec((block_size, orbitals), lambda b, li, mk: (b, 0)),
+            scratch_shapes=[
+                pltpu.VMEM((window * block_size, orbitals), occ_coeff.dtype),
+                pltpu.VMEM((stored, orbitals), occ_coeff.dtype),
+            ],
         ),
         out_shape=jax.ShapeDtypeStruct((rows_local, orbitals), jnp.bfloat16),
-    )(local_index, screen_mask, tiles, extended)
+        compiler_params=pltpu.CompilerParams(dimension_semantics=("arbitrary",)),
+    )(local_index, screen_mask, tiles, low, occ_coeff, high)
     half_local = half_local.reshape(p_local, rows_local, orbitals)
     aux_index = lax.axis_index("aux")
     share = rows_local // aux_count

time: 173 us -> 171 us (0.988)
  other arithmetic: 4.42 us -> 2.13 us
    concatenate x1 -> x0, other arithmetic: 2.29 us -> none  [with_halo(): block = jnp.concatenate([low, block, high], axis=dim)]
where the time goes in v7:
time: 171 us; the launch traced here: 170 us
  waiting for transfers between devices  91 us (53%)
  matrix products  23.5 us (14%)
  local copies, waits for them, and re-layouts  19.8 us (12%)
  between operations  13.5 us (8%)
  starting transfers between devices  11.9 us (7%)
  Pallas kernels  8.26 us (5%)
  other arithmetic  2.13 us (1%)
    all_gather x1, waiting for transfers between devices, per_device(): partner = lax.all_gather(piece, ROW, axis=0)  56.9 us
    dot_general x1, matrix products, per_device(): jnp.einsum('pmi,rpki->mrk', slab_rows, partner, preferred_element_type=jn...  23.5 us
    ppermute x3, waiting for transfers between devices, per_device(): shifted.append(lax.ppermute(own, 'aux', pairs))  21.1 us
    reshape x1, local copies, waits for them, and re-layouts, per_device(): result.astype(jnp.bfloat16).reshape(rows_local, partner.shape[0], 1, share)  17.9 us
    pallas_call x1, Pallas kernels, per_device(): pl.pallas_call(kernel, grid_spec=pltpu.PrefetchScalarGridSpec(num_scalar_...  8.26 us
    ppermute x3, waiting for transfers between devices, per_device(): pieces.append(lax.ppermute(outgoing, 'aux', pairs))  5.59 us
    ppermute x1, starting transfers between devices, halo_pieces(): lax.ppermute(lax.slice_in_dim(block, block.shape[0] - width, None, axis=0...  4.58 us
    ppermute x1, waiting for transfers between devices, halo_pieces(): lax.ppermute(lax.slice_in_dim(block, 0, width, axis=0), axis, backward)  4.29 us
  transfers between devices with their start and end apart: 9, of which 9 were waited for; matrix products, arithmetic and copies ran while one was open for 1% of the time, Pallas kernels for 0%

profile of v7, /device:TPU:1, one launch (start us, length us, event | category | flops | bytes accessed | tf_op | source)
XLA Modules:
  0.0 170.1 jit_solution(7314600724741817081)
XLA Ops:
  6.5 0.0 all-gather.3.cloned.1.call-start
  6.5 4.6 %collective-permute-start = (bf16[1024,256]{1,0:T(8,128)(2,1)}, bf16[1024,256]{1,0:T(8,128)(2,1)S(1)}, u32[]{:S(2)}, u32[]{:S(2)}) collective-permute-start(bf16[1024,256]{1,0:T(8,128)(2,1)} %own_ref.1), channel_id=1, source_target_pairs={{0,1},{1,2},{2,3},{3,4},{4,5},{5,6},{6,7},{7,8},{8,9},{9,10},{10,1... | collective-permute-start | bytes 1572872 | tf_op jit(solution)/shard_map/ppermute | solution.py:13
  11.1 1.9 %collective-permute-start.1 = (bf16[1024,256]{1,0:T(8,128)(2,1)}, bf16[1024,256]{1,0:T(8,128)(2,1)S(1)}, u32[]{:S(2)}, u32[]{:S(2)}) collective-permute-start(bf16[1024,256]{1,0:T(8,128)(2,1)} %own_ref.1), channel_id=1, source_target_pairs={{1,0},{2,1},{3,2},{4,3},{5,4},{6,5},{7,6},{8,7},{9,8},{10,9},{11,1... | collective-permute-start | bytes 1572872 | tf_op jit(solution)/shard_map/ppermute | solution.py:14
  13.1 1.3 subtract_clamp_fusion.index_ref
  14.4 3.2 %collective-permute-done.low_ref = bf16[1024,256]{1,0:T(8,128)(2,1)S(1)} collective-permute-done((bf16[1024,256]{1,0:T(8,128)(2,1)}, bf16[1024,256]{1,0:T(8,128)(2,1)S(1)}, u32[]{:S(2)}, u32[]{:S(2)}) %collective-permute-start) | collective-permute-done | bytes 524320 | tf_op jit(solution)/shard_map/ppermute | solution.py:13
  17.6 0.0 copy-start
  17.6 4.3 %collective-permute-done.1.high_ref = bf16[1024,256]{1,0:T(8,128)(2,1)S(1)} collective-permute-done((bf16[1024,256]{1,0:T(8,128)(2,1)}, bf16[1024,256]{1,0:T(8,128)(2,1)S(1)}, u32[]{:S(2)}, u32[]{:S(2)}) %collective-permute-start.1) | collective-permute-done | bytes 524320 | tf_op jit(solution)/shard_map/ppermute | solution.py:14
  21.8 0.0 copy-start.1
  21.8 0.0 copy-done
  21.8 0.8 copy-done.1
  22.6 8.3 %shard_map.46 = bf16[1024,256]{1,0:T(8,128)(2,1)} custom-call(s32[8,16]{1,0:T(8,128)} %subtract_clamp_fusion.index_ref, s32[8,16]{1,0:T(8,128)} %mask_ref.1, bf16[1024,2048]{1,0:T(8,128)(2,1)} %bitcast.22, bf16[1024,256]{1,0:T(8,128)(2,1)} %copy-done, bf16[1024,256]{1,0:T(8,128)(2,1)} %own_ref.1, bf16[1024,256]{1,0:T(8,128)(2,1)} %copy-done.1), custom_call_target="tpu_custom_call" | custom-call | tf_op jit(solution)/shard_map/pallas_call | solution.py:52
  30.9 1.1 dynamic-slice_bitcast_fusion
  32.0 2.5 %collective-permute-start.7 = (bf16[256,256]{1,0:T(8,128)(2,1)S(1)}, bf16[256,256]{1,0:T(8,128)(2,1)S(1)}, u32[]{:S(2)}, u32[]{:S(2)}) collective-permute-start(bf16[256,256]{1,0:T(8,128)(2,1)S(1)} %get-tuple-element.6), channel_id=1, source_target_pairs={{0,96},{32,0},{64,32},{96,64},{1,97},{33,1},{65,33},{97,65},{2,98}... | collective-permute-start | bytes 393224 | tf_op jit(solution)/shard_map/ppermute | solution.py:82
  34.6 0.5 collective-permute-start.6
  35.1 0.6 collective-permute-start.5
  35.7 2.2 %collective-permute-done.7 = bf16[256,256]{1,0:T(8,128)(2,1)S(1)} collective-permute-done((bf16[256,256]{1,0:T(8,128)(2,1)S(1)}, bf16[256,256]{1,0:T(8,128)(2,1)S(1)}, u32[]{:S(2)}, u32[]{:S(2)}) %collective-permute-start.7) | collective-permute-done | bytes 131104 | tf_op jit(solution)/shard_map/ppermute | solution.py:82
  37.9 2.1 %collective-permute-done.6 = bf16[256,256]{1,0:T(8,128)(2,1)S(1)} collective-permute-done((bf16[256,256]{1,0:T(8,128)(2,1)S(1)}, bf16[256,256]{1,0:T(8,128)(2,1)S(1)}, u32[]{:S(2)}, u32[]{:S(2)}) %collective-permute-start.6) | collective-permute-done | bytes 131104 | tf_op jit(solution)/shard_map/ppermute | solution.py:82
  40.0 1.3 collective-permute-done.5
  41.3 0.9 pad_maximum_fusion
  42.2 0.0 all-gather.3.cloned.1.call-update
  42.2 0.4 collective-permute-start.4
  42.5 0.8 collective-permute-start.3
  43.4 0.6 collective-permute-start.2
  43.9 12.5 %collective-permute-done.4 = bf16[1024,256]{1,0:T(8,128)(2,1)S(1)} collective-permute-done((bf16[1024,256]{1,0:T(8,128)(2,1)}, bf16[1024,256]{1,0:T(8,128)(2,1)S(1)}, u32[]{:S(2)}, u32[]{:S(2)}) %collective-permute-start.4) | collective-permute-done | bytes 524320 | tf_op jit(solution)/shard_map/ppermute | solution.py:83
  56.5 1.5 collective-permute-done.3
  58.0 7.1 %collective-permute-done.2 = bf16[1024,256]{1,0:T(8,128)(2,1)S(1)} collective-permute-done((bf16[1024,256]{1,0:T(8,128)(2,1)}, bf16[1024,256]{1,0:T(8,128)(2,1)S(1)}, u32[]{:S(2)}, u32[]{:S(2)}) %collective-permute-start.2) | collective-permute-done | bytes 524320 | tf_op jit(solution)/shard_map/ppermute | solution.py:83
  65.0 56.9 %all-gather.3.cloned.1.call-done = bf16[128,256,256]{2,1,0:T(8,128)(2,1)} async-done(((bf16[4,256,256]{2,1,0:T(8,128)(2,1)}), bf16[128,256,256]{2,1,0:T(8,128)(2,1)}) %all-gather.3.cloned.1.call-update) | async-done | bytes 16777232 | tf_op jit(solution)/shard_map/all_gather | solution.py:86
  121.9 23.5 %fusion = bf16[1024,32,1,256]{3,0,1,2:T(8,128)(2,1)} fusion(bf16[32,4,256,256]{3,2,1,0:T(8,128)(2,1)} %bitcast.27, bf16[1,1024,256]{2,1,0:T(8,128)(2,1)S(1)} %bitcast.28, bf16[1,1024,256]{2,1,0:T(8,128)(2,1)S(1)} %bitcast.29, bf16[1,1024,256]{2,1,0:T(8,128)(2,1)S(1)} %bitcast.30, bf16[1,1024,256]{2,1,0:T(8,128)(2,1)} %bitcast.23), kind=kOutput, calls=%fused_computation.1 | convolution fusion | flops 17196646400 | bytes 35651584 | tf_op jit(solution)/shard_map/pmi,rpki->mrk/dot_general | solution.py:87
  145.4 17.9 %copy.6 = bf16[1024,32,1,256]{3,1,2,0:T(8,128)(2,1)} copy(bf16[1024,32,1,256]{3,0,1,2:T(8,128)(2,1)} %fusion) | data formatting | bytes 33554432 | tf_op jit(solution)/shard_map/reshape | solution.py:88
Async XLA Ops:
  6.5 115.3 %all-gather.3.cloned.1.call-start = ((), (), s32[]{:S(2)}) async-start(), calls=%async_computation | async-start | bytes 17301504 | tf_op jit(solution)/shard_map/all_gather | solution.py:86
  6.5 11.0 %collective-permute-start = (bf16[1024,256]{1,0:T(8,128)(2,1)}, bf16[1024,256]{1,0:T(8,128)(2,1)S(1)}, u32[]{:S(2)}, u32[]{:S(2)}) collective-permute-start(bf16[1024,256]{1,0:T(8,128)(2,1)} %own_ref.1), channel_id=1, source_target_pairs={{0,1},{1,2},{2,3},{3,4},{4,5},{5,6},{6,7},{7,8},{8,9},{9,10},{10,1... | collective-permute-start | bytes 1572872 | tf_op jit(solution)/shard_map/ppermute | solution.py:13
  11.1 10.7 %collective-permute-start.1 = (bf16[1024,256]{1,0:T(8,128)(2,1)}, bf16[1024,256]{1,0:T(8,128)(2,1)S(1)}, u32[]{:S(2)}, u32[]{:S(2)}) collective-permute-start(bf16[1024,256]{1,0:T(8,128)(2,1)} %own_ref.1), channel_id=1, source_target_pairs={{1,0},{2,1},{3,2},{4,3},{5,4},{6,5},{7,6},{8,7},{9,8},{10,9},{11,1... | collective-permute-start | bytes 1572872 | tf_op jit(solution)/shard_map/ppermute | solution.py:14
  17.6 4.3 %copy-start = (bf16[1024,256]{1,0:T(8,128)(2,1)}, bf16[1024,256]{1,0:T(8,128)(2,1)S(1)}, u32[]{:S(2)}) copy-start(bf16[1024,256]{1,0:T(8,128)(2,1)S(1)} %collective-permute-done.low_ref) | copy-start | bytes 1572868
  21.8 0.8 copy-start.1
  32.0 5.9 %collective-permute-start.7 = (bf16[256,256]{1,0:T(8,128)(2,1)S(1)}, bf16[256,256]{1,0:T(8,128)(2,1)S(1)}, u32[]{:S(2)}, u32[]{:S(2)}) collective-permute-start(bf16[256,256]{1,0:T(8,128)(2,1)S(1)} %get-tuple-element.6), channel_id=1, source_target_pairs={{0,96},{32,0},{64,32},{96,64},{1,97},{33,1},{65,33},{97,65},{2,98}... | collective-permute-start | bytes 393224 | tf_op jit(solution)/shard_map/ppermute | solution.py:82
  34.6 5.4 %collective-permute-start.6 = (bf16[256,256]{1,0:T(8,128)(2,1)S(1)}, bf16[256,256]{1,0:T(8,128)(2,1)S(1)}, u32[]{:S(2)}, u32[]{:S(2)}) collective-permute-start(bf16[256,256]{1,0:T(8,128)(2,1)S(1)} %get-tuple-element.7), channel_id=1, source_target_pairs={{0,64},{32,96},{64,0},{96,32},{1,65},{33,97},{65,1},{97,33},{2,66}... | collective-permute-start | bytes 393224 | tf_op jit(solution)/shard_map/ppermute | solution.py:82
  35.1 6.2 %collective-permute-start.5 = (bf16[256,256]{1,0:T(8,128)(2,1)S(1)}, bf16[256,256]{1,0:T(8,128)(2,1)S(1)}, u32[]{:S(2)}, u32[]{:S(2)}) collective-permute-start(bf16[256,256]{1,0:T(8,128)(2,1)S(1)} %get-tuple-element.8), channel_id=1, source_target_pairs={{0,32},{32,64},{64,96},{96,0},{1,33},{33,65},{65,97},{97,1},{2,34}... | collective-permute-start | bytes 393224 | tf_op jit(solution)/shard_map/ppermute | solution.py:82
  42.2 14.3 %collective-permute-start.4 = (bf16[1024,256]{1,0:T(8,128)(2,1)}, bf16[1024,256]{1,0:T(8,128)(2,1)S(1)}, u32[]{:S(2)}, u32[]{:S(2)}) collective-permute-start(bf16[1024,256]{1,0:T(8,128)(2,1)} %shard_map.46), channel_id=1, source_target_pairs={{0,96},{32,0},{64,32},{96,64},{1,97},{33,1},{65,33},{97,65},{2,98}... | collective-permute-start | bytes 1572872 | tf_op jit(solution)/shard_map/ppermute | solution.py:83
  42.5 15.4 %collective-permute-start.3 = (bf16[1024,256]{1,0:T(8,128)(2,1)}, bf16[1024,256]{1,0:T(8,128)(2,1)S(1)}, u32[]{:S(2)}, u32[]{:S(2)}) collective-permute-start(bf16[1024,256]{1,0:T(8,128)(2,1)} %shard_map.46), channel_id=1, source_target_pairs={{0,64},{32,96},{64,0},{96,32},{1,65},{33,97},{65,1},{97,33},{2,66}... | collective-permute-start | bytes 1572872 | tf_op jit(solution)/shard_map/ppermute | solution.py:83
  43.4 21.7 %collective-permute-start.2 = (bf16[1024,256]{1,0:T(8,128)(2,1)}, bf16[1024,256]{1,0:T(8,128)(2,1)S(1)}, u32[]{:S(2)}, u32[]{:S(2)}) collective-permute-start(bf16[1024,256]{1,0:T(8,128)(2,1)} %shard_map.46), channel_id=1, source_target_pairs={{0,32},{32,64},{64,96},{96,0},{1,33},{33,65},{65,97},{97,1},{2,34}... | collective-permute-start | bytes 1572872 | tf_op jit(solution)/shard_map/ppermute | solution.py:83
Sparse Core Ops, SparseCore 0:
  42.3 79.5 all-gather.2

commit v8 on v7

--- a/solution.py
+++ b/solution.py
@@ -84,8 +84,23 @@
     piece = jnp.stack(pieces)
     slab_rows = jnp.stack(shifted)
     partner = lax.all_gather(piece, ROW, axis=0)
-    result = jnp.einsum("pmi,rpki->mrk", slab_rows, partner, preferred_element_type=jnp.float32)
-    return result.astype(jnp.bfloat16).reshape(rows_local, partner.shape[0], 1, share)
+    result = jnp.einsum("pmi,rpki->rmk", slab_rows, partner, preferred_element_type=jnp.float32)
+    result = result.astype(jnp.bfloat16)
+    row_count = partner.shape[0]
+    rows_tile = 64
+
+    def relayout(in_ref, out_ref):
+        x = in_ref[...].astype(jnp.float32)
+        out_ref[...] = pltpu.einshape("rmk->mrk", x).astype(out_ref.dtype)
+
+    result = pl.pallas_call(
+        relayout,
+        grid=(rows_local // rows_tile,),
+        in_specs=[pl.BlockSpec((row_count, rows_tile, share), lambda i: (0, i, 0))],
+        out_specs=pl.BlockSpec((rows_tile, row_count, share), lambda i: (i, 0, 0)),
+        out_shape=jax.ShapeDtypeStruct((rows_local, row_count, share), jnp.bfloat16),
+    )(result)
+    return result.reshape(rows_local, row_count, 1, share)
 
 
 def solution(mesh):

time: 171 us -> 177 us (1.035)
  Pallas kernels: 8.26 us -> 29.1 us
  local copies, waits for them, and re-layouts: 19.8 us -> 1.92 us
  matrix products: 23.5 us -> 26.4 us
    pallas_call x0 -> x1, Pallas kernels: none -> 20.8 us  [per_device(): pl.pallas_call(relayout, grid=(rows_local // rows_tile,), in_specs=[pl.Bl...]
    reshape x1 -> x0, local copies, waits for them, and re-layouts: 17.9 us -> none  [per_device(): result.astype(jnp.bfloat16).reshape(rows_local, partner.shape[0], 1, share)]
    dot_general x1, matrix products: 23.5 us -> 26.4 us  [per_device(): jnp.einsum('pmi,rpki->rmk', slab_rows, partner, preferred_element_type=jn...]
where the time goes in v8:
time: 177 us; the launch traced here: 176 us
  waiting for transfers between devices  91 us (51%)
  Pallas kernels  29.1 us (16%)
  matrix products  26.4 us (15%)
  between operations  13.5 us (8%)
  starting transfers between devices  11.9 us (7%)
  other arithmetic  2.13 us (1%)
  local copies, waits for them, and re-layouts  1.92 us (1%)
    all_gather x1, waiting for transfers between devices, per_device(): partner = lax.all_gather(piece, ROW, axis=0)  56.9 us
    dot_general x1, matrix products, per_device(): jnp.einsum('pmi,rpki->rmk', slab_rows, partner, preferred_element_type=jn...  26.4 us
    ppermute x3, waiting for transfers between devices, per_device(): shifted.append(lax.ppermute(own, 'aux', pairs))  21.1 us
    pallas_call x1, Pallas kernels, per_device(): pl.pallas_call(relayout, grid=(rows_local // rows_tile,), in_specs=[pl.Bl...  20.8 us
    pallas_call x1, Pallas kernels, per_device(): pl.pallas_call(kernel, grid_spec=pltpu.PrefetchScalarGridSpec(num_scalar_...  8.26 us
    ppermute x3, waiting for transfers between devices, per_device(): pieces.append(lax.ppermute(outgoing, 'aux', pairs))  5.59 us
    ppermute x1, starting transfers between devices, halo_pieces(): lax.ppermute(lax.slice_in_dim(block, block.shape[0] - width, None, axis=0...  4.58 us
    ppermute x1, waiting for transfers between devices, halo_pieces(): lax.ppermute(lax.slice_in_dim(block, 0, width, axis=0), axis, backward)  4.29 us
  transfers between devices with their start and end apart: 9, of which 9 were waited for; matrix products, arithmetic and copies ran while one was open for 1% of the time, Pallas kernels for 0%

profile of v8, /device:TPU:1, one launch (start us, length us, event | category | flops | bytes accessed | tf_op | source)
XLA Modules:
  0.0 175.9 jit_solution(14395457605491231874)
XLA Ops:
  6.5 0.0 all-gather.3.cloned.1.call-start
  6.5 4.6 %collective-permute-start = (bf16[1024,256]{1,0:T(8,128)(2,1)}, bf16[1024,256]{1,0:T(8,128)(2,1)S(1)}, u32[]{:S(2)}, u32[]{:S(2)}) collective-permute-start(bf16[1024,256]{1,0:T(8,128)(2,1)} %own_ref.1), channel_id=1, source_target_pairs={{0,1},{1,2},{2,3},{3,4},{4,5},{5,6},{6,7},{7,8},{8,9},{9,10},{10,1... | collective-permute-start | bytes 1572872 | tf_op jit(solution)/shard_map/ppermute | solution.py:13
  11.1 1.9 %collective-permute-start.1 = (bf16[1024,256]{1,0:T(8,128)(2,1)}, bf16[1024,256]{1,0:T(8,128)(2,1)S(1)}, u32[]{:S(2)}, u32[]{:S(2)}) collective-permute-start(bf16[1024,256]{1,0:T(8,128)(2,1)} %own_ref.1), channel_id=1, source_target_pairs={{1,0},{2,1},{3,2},{4,3},{5,4},{6,5},{7,6},{8,7},{9,8},{10,9},{11,1... | collective-permute-start | bytes 1572872 | tf_op jit(solution)/shard_map/ppermute | solution.py:14
  13.1 1.3 subtract_clamp_fusion.index_ref
  14.4 3.2 %collective-permute-done.low_ref = bf16[1024,256]{1,0:T(8,128)(2,1)S(1)} collective-permute-done((bf16[1024,256]{1,0:T(8,128)(2,1)}, bf16[1024,256]{1,0:T(8,128)(2,1)S(1)}, u32[]{:S(2)}, u32[]{:S(2)}) %collective-permute-start) | collective-permute-done | bytes 524320 | tf_op jit(solution)/shard_map/ppermute | solution.py:13
  17.6 0.0 copy-start
  17.6 4.3 %collective-permute-done.1.high_ref = bf16[1024,256]{1,0:T(8,128)(2,1)S(1)} collective-permute-done((bf16[1024,256]{1,0:T(8,128)(2,1)}, bf16[1024,256]{1,0:T(8,128)(2,1)S(1)}, u32[]{:S(2)}, u32[]{:S(2)}) %collective-permute-start.1) | collective-permute-done | bytes 524320 | tf_op jit(solution)/shard_map/ppermute | solution.py:14
  21.8 0.0 copy-start.1
  21.8 0.0 copy-done
  21.8 0.8 copy-done.1
  22.6 8.3 %shard_map.46 = bf16[1024,256]{1,0:T(8,128)(2,1)} custom-call(s32[8,16]{1,0:T(8,128)} %subtract_clamp_fusion.index_ref, s32[8,16]{1,0:T(8,128)} %mask_ref.1, bf16[1024,2048]{1,0:T(8,128)(2,1)} %bitcast.24, bf16[1024,256]{1,0:T(8,128)(2,1)} %copy-done, bf16[1024,256]{1,0:T(8,128)(2,1)} %own_ref.1, bf16[1024,256]{1,0:T(8,128)(2,1)} %copy-done.1), custom_call_target="tpu_custom_call" | custom-call | tf_op jit(solution)/shard_map/pallas_call | solution.py:52
  30.9 1.1 dynamic-slice_bitcast_fusion
  32.0 2.5 %collective-permute-start.4 = (bf16[256,256]{1,0:T(8,128)(2,1)S(1)}, bf16[256,256]{1,0:T(8,128)(2,1)S(1)}, u32[]{:S(2)}, u32[]{:S(2)}) collective-permute-start(bf16[256,256]{1,0:T(8,128)(2,1)S(1)} %get-tuple-element.6), channel_id=1, source_target_pairs={{0,96},{32,0},{64,32},{96,64},{1,97},{33,1},{65,33},{97,65},{2,98}... | collective-permute-start | bytes 393224 | tf_op jit(solution)/shard_map/ppermute | solution.py:82
  34.6 0.5 collective-permute-start.3
  35.1 0.6 collective-permute-start.2
  35.7 2.2 %collective-permute-done.4 = bf16[256,256]{1,0:T(8,128)(2,1)S(1)} collective-permute-done((bf16[256,256]{1,0:T(8,128)(2,1)S(1)}, bf16[256,256]{1,0:T(8,128)(2,1)S(1)}, u32[]{:S(2)}, u32[]{:S(2)}) %collective-permute-start.4) | collective-permute-done | bytes 131104 | tf_op jit(solution)/shard_map/ppermute | solution.py:82
  37.9 2.1 %collective-permute-done.3 = bf16[256,256]{1,0:T(8,128)(2,1)S(1)} collective-permute-done((bf16[256,256]{1,0:T(8,128)(2,1)S(1)}, bf16[256,256]{1,0:T(8,128)(2,1)S(1)}, u32[]{:S(2)}, u32[]{:S(2)}) %collective-permute-start.3) | collective-permute-done | bytes 131104 | tf_op jit(solution)/shard_map/ppermute | solution.py:82
  40.0 1.3 collective-permute-done.2
  41.3 0.9 pad_maximum_fusion
  42.2 0.0 all-gather.3.cloned.1.call-update
  42.2 0.4 collective-permute-start.7
  42.5 0.8 collective-permute-start.6
  43.4 0.6 collective-permute-start.5
  43.9 12.5 %collective-permute-done.7 = bf16[1024,256]{1,0:T(8,128)(2,1)S(1)} collective-permute-done((bf16[1024,256]{1,0:T(8,128)(2,1)}, bf16[1024,256]{1,0:T(8,128)(2,1)S(1)}, u32[]{:S(2)}, u32[]{:S(2)}) %collective-permute-start.7) | collective-permute-done | bytes 524320 | tf_op jit(solution)/shard_map/ppermute | solution.py:83
  56.5 1.5 collective-permute-done.6
  58.0 7.1 %collective-permute-done.5 = bf16[1024,256]{1,0:T(8,128)(2,1)S(1)} collective-permute-done((bf16[1024,256]{1,0:T(8,128)(2,1)}, bf16[1024,256]{1,0:T(8,128)(2,1)S(1)}, u32[]{:S(2)}, u32[]{:S(2)}) %collective-permute-start.5) | collective-permute-done | bytes 524320 | tf_op jit(solution)/shard_map/ppermute | solution.py:83
  65.0 56.9 %all-gather.3.cloned.1.call-done = bf16[128,256,256]{2,1,0:T(8,128)(2,1)} async-done(((bf16[4,256,256]{2,1,0:T(8,128)(2,1)}), bf16[128,256,256]{2,1,0:T(8,128)(2,1)}) %all-gather.3.cloned.1.call-update) | async-done | bytes 16777232 | tf_op jit(solution)/shard_map/all_gather | solution.py:86
  121.9 26.4 %fusion.in_ref = bf16[32,1024,256]{2,1,0:T(8,128)(2,1)} fusion(bf16[32,4,256,256]{3,2,1,0:T(8,128)(2,1)} %bitcast.29, bf16[1,1024,256]{2,1,0:T(8,128)(2,1)S(1)} %bitcast.30, bf16[1,1024,256]{2,1,0:T(8,128)(2,1)S(1)} %bitcast.31, bf16[1,1024,256]{2,1,0:T(8,128)(2,1)S(1)} %bitcast.32, bf16[1,1024,256]{2,1,0:T(8,128)(2,1)} %bitcast.25), kind=kOutput, calls=%fused_computation.1 | convolution fusion | flops 17191403520 | bytes 35651584 | tf_op jit(solution)/shard_map/pmi,rpki->rmk/dot_general | solution.py:87
  148.3 20.8 %shard_map.47 = bf16[1024,32,256]{2,1,0:T(8,128)(2,1)} custom-call(bf16[32,1024,256]{2,1,0:T(8,128)(2,1)} %fusion.in_ref), custom_call_target="tpu_custom_call" | custom-call | tf_op jit(solution)/shard_map/pallas_call | solution.py:96
Async XLA Ops:
  6.5 115.3 %all-gather.3.cloned.1.call-start = ((), (), s32[]{:S(2)}) async-start(), calls=%async_computation | async-start | bytes 17301504 | tf_op jit(solution)/shard_map/all_gather | solution.py:86
  6.5 11.0 %collective-permute-start = (bf16[1024,256]{1,0:T(8,128)(2,1)}, bf16[1024,256]{1,0:T(8,128)(2,1)S(1)}, u32[]{:S(2)}, u32[]{:S(2)}) collective-permute-start(bf16[1024,256]{1,0:T(8,128)(2,1)} %own_ref.1), channel_id=1, source_target_pairs={{0,1},{1,2},{2,3},{3,4},{4,5},{5,6},{6,7},{7,8},{8,9},{9,10},{10,1... | collective-permute-start | bytes 1572872 | tf_op jit(solution)/shard_map/ppermute | solution.py:13
  11.1 10.7 %collective-permute-start.1 = (bf16[1024,256]{1,0:T(8,128)(2,1)}, bf16[1024,256]{1,0:T(8,128)(2,1)S(1)}, u32[]{:S(2)}, u32[]{:S(2)}) collective-permute-start(bf16[1024,256]{1,0:T(8,128)(2,1)} %own_ref.1), channel_id=1, source_target_pairs={{1,0},{2,1},{3,2},{4,3},{5,4},{6,5},{7,6},{8,7},{9,8},{10,9},{11,1... | collective-permute-start | bytes 1572872 | tf_op jit(solution)/shard_map/ppermute | solution.py:14
  17.6 4.3 %copy-start = (bf16[1024,256]{1,0:T(8,128)(2,1)}, bf16[1024,256]{1,0:T(8,128)(2,1)S(1)}, u32[]{:S(2)}) copy-start(bf16[1024,256]{1,0:T(8,128)(2,1)S(1)} %collective-permute-done.low_ref) | copy-start | bytes 1572868
  21.8 0.8 copy-start.1
  32.0 5.9 %collective-permute-start.4 = (bf16[256,256]{1,0:T(8,128)(2,1)S(1)}, bf16[256,256]{1,0:T(8,128)(2,1)S(1)}, u32[]{:S(2)}, u32[]{:S(2)}) collective-permute-start(bf16[256,256]{1,0:T(8,128)(2,1)S(1)} %get-tuple-element.6), channel_id=1, source_target_pairs={{0,96},{32,0},{64,32},{96,64},{1,97},{33,1},{65,33},{97,65},{2,98}... | collective-permute-start | bytes 393224 | tf_op jit(solution)/shard_map/ppermute | solution.py:82
  34.6 5.4 %collective-permute-start.3 = (bf16[256,256]{1,0:T(8,128)(2,1)S(1)}, bf16[256,256]{1,0:T(8,128)(2,1)S(1)}, u32[]{:S(2)}, u32[]{:S(2)}) collective-permute-start(bf16[256,256]{1,0:T(8,128)(2,1)S(1)} %get-tuple-element.7), channel_id=1, source_target_pairs={{0,64},{32,96},{64,0},{96,32},{1,65},{33,97},{65,1},{97,33},{2,66}... | collective-permute-start | bytes 393224 | tf_op jit(solution)/shard_map/ppermute | solution.py:82
  35.1 6.2 %collective-permute-start.2 = (bf16[256,256]{1,0:T(8,128)(2,1)S(1)}, bf16[256,256]{1,0:T(8,128)(2,1)S(1)}, u32[]{:S(2)}, u32[]{:S(2)}) collective-permute-start(bf16[256,256]{1,0:T(8,128)(2,1)S(1)} %get-tuple-element.8), channel_id=1, source_target_pairs={{0,32},{32,64},{64,96},{96,0},{1,33},{33,65},{65,97},{97,1},{2,34}... | collective-permute-start | bytes 393224 | tf_op jit(solution)/shard_map/ppermute | solution.py:82
  42.2 14.3 %collective-permute-start.7 = (bf16[1024,256]{1,0:T(8,128)(2,1)}, bf16[1024,256]{1,0:T(8,128)(2,1)S(1)}, u32[]{:S(2)}, u32[]{:S(2)}) collective-permute-start(bf16[1024,256]{1,0:T(8,128)(2,1)} %shard_map.46), channel_id=1, source_target_pairs={{0,96},{32,0},{64,32},{96,64},{1,97},{33,1},{65,33},{97,65},{2,98}... | collective-permute-start | bytes 1572872 | tf_op jit(solution)/shard_map/ppermute | solution.py:83
  42.5 15.4 %collective-permute-start.6 = (bf16[1024,256]{1,0:T(8,128)(2,1)}, bf16[1024,256]{1,0:T(8,128)(2,1)S(1)}, u32[]{:S(2)}, u32[]{:S(2)}) collective-permute-start(bf16[1024,256]{1,0:T(8,128)(2,1)} %shard_map.46), channel_id=1, source_target_pairs={{0,64},{32,96},{64,0},{96,32},{1,65},{33,97},{65,1},{97,33},{2,66}... | collective-permute-start | bytes 1572872 | tf_op jit(solution)/shard_map/ppermute | solution.py:83
  43.4 21.7 %collective-permute-start.5 = (bf16[1024,256]{1,0:T(8,128)(2,1)}, bf16[1024,256]{1,0:T(8,128)(2,1)S(1)}, u32[]{:S(2)}, u32[]{:S(2)}) collective-permute-start(bf16[1024,256]{1,0:T(8,128)(2,1)} %shard_map.46), channel_id=1, source_target_pairs={{0,32},{32,64},{64,96},{96,0},{1,33},{33,65},{65,97},{97,1},{2,34}... | collective-permute-start | bytes 1572872 | tf_op jit(solution)/shard_map/ppermute | solution.py:83
Sparse Core Ops, SparseCore 0:
  42.3 79.5 all-gather.2

commit v9 on v7

--- a/solution.py
+++ b/solution.py
@@ -73,16 +73,15 @@
     aux_index = lax.axis_index("aux")
     share = rows_local // aux_count
     own = half_local[0]
-    pieces = [lax.dynamic_slice_in_dim(own, aux_index * share, share, axis=0)]
     shifted = [own]
     for shift in range(1, aux_count):
         pairs = [(i, (i + shift) % aux_count) for i in range(aux_count)]
-        target = (aux_index + shift) % aux_count
-        outgoing = lax.dynamic_slice_in_dim(own, target * share, share, axis=0)
-        pieces.append(lax.ppermute(outgoing, "aux", pairs))
         shifted.append(lax.ppermute(own, "aux", pairs))
-    piece = jnp.stack(pieces)
-    slab_rows = jnp.stack(shifted)
+    piece = lax.all_to_all(
+        own.reshape(aux_count, share, orbitals), "aux", 0, 0, tiled=True
+    )
+    order = (aux_index - jnp.arange(aux_count)) % aux_count
+    slab_rows = jnp.take(jnp.stack(shifted), order, axis=0)
     partner = lax.all_gather(piece, ROW, axis=0)
     result = jnp.einsum("pmi,rpki->mrk", slab_rows, partner, preferred_element_type=jnp.float32)
     return result.astype(jnp.bfloat16).reshape(rows_local, partner.shape[0], 1, share)

time: 171 us -> 170 us (level)
  waiting for transfers between devices: 91 us -> 76.9 us
  blocking collectives: 0 us -> 11.1 us
    all_to_all x0 -> x1, blocking collectives: none -> 11.1 us  [per_device(): lax.all_to_all(own.reshape(aux_count, share, orbitals), 'aux', 0, 0, tile...]
    all_gather x1, waiting for transfers between devices: 56.9 us -> 51 us  [per_device(): partner = lax.all_gather(piece, ROW, axis=0)]
    ppermute x3 -> x0, waiting for transfers between devices: 5.59 us -> none  [per_device(): pieces.append(lax.ppermute(outgoing, 'aux', pairs))]
    ppermute x3 -> x0, starting transfers between devices: 3.67 us -> none  [per_device(): pieces.append(lax.ppermute(outgoing, 'aux', pairs))]
    ppermute x3, starting transfers between devices: 1.75 us -> 4.65 us  [per_device(): shifted.append(lax.ppermute(own, 'aux', pairs))]
    ppermute x3, waiting for transfers between devices: 21.1 us -> 18.4 us  [per_device(): shifted.append(lax.ppermute(own, 'aux', pairs))]
    gather x0 -> x1, local copies, waits for them, and re-layouts: none -> 2 us  [per_device(): slab_rows = jnp.take(jnp.stack(shifted), order, axis=0)]
  transfers between devices with their start and end apart: 9 -> 6, of which waited for: 9 -> 6; matrix products, arithmetic and copies ran while one was open for 1% -> 3% of each run, Pallas kernels for 0% -> 0%
where the time goes in v9:
time: 170 us; the launch traced here: 169 us
  waiting for transfers between devices  76.9 us (45%)
  matrix products  24.1 us (14%)
  local copies, waits for them, and re-layouts  21.5 us (13%)
  between operations  13.4 us (8%)
  starting transfers between devices  11.2 us (7%)
  blocking collectives  11.1 us (7%)
  Pallas kernels  8.26 us (5%)
  other arithmetic  2.78 us (2%)
    all_gather x1, waiting for transfers between devices, per_device(): partner = lax.all_gather(piece, ROW, axis=0)  51 us
    dot_general x1, matrix products, per_device(): jnp.einsum('pmi,rpki->mrk', slab_rows, partner, preferred_element_type=jn...  24.1 us
    ppermute x3, waiting for transfers between devices, per_device(): shifted.append(lax.ppermute(own, 'aux', pairs))  18.4 us
    reshape x1, local copies, waits for them, and re-layouts, per_device(): result.astype(jnp.bfloat16).reshape(rows_local, partner.shape[0], 1, share)  17.9 us
    all_to_all x1, blocking collectives, per_device(): lax.all_to_all(own.reshape(aux_count, share, orbitals), 'aux', 0, 0, tile...  11.1 us
    pallas_call x1, Pallas kernels, per_device(): pl.pallas_call(kernel, grid_spec=pltpu.PrefetchScalarGridSpec(num_scalar_...  8.26 us
    ppermute x3, starting transfers between devices, per_device(): shifted.append(lax.ppermute(own, 'aux', pairs))  4.65 us
    ppermute x1, starting transfers between devices, halo_pieces(): lax.ppermute(lax.slice_in_dim(block, block.shape[0] - width, None, axis=0...  4.58 us
  transfers between devices with their start and end apart: 6, of which 6 were waited for; matrix products, arithmetic and copies ran while one was open for 3% of the time, Pallas kernels for 0%

profile of v9, /device:TPU:1, one launch (start us, length us, event | category | flops | bytes accessed | tf_op | source)
XLA Modules:
  0.0 169.3 jit_solution(15176927134484836638)
XLA Ops:
  6.5 0.0 all-gather.3.cloned.1.call-start
  6.5 4.6 %collective-permute-start = (bf16[1024,256]{1,0:T(8,128)(2,1)}, bf16[1024,256]{1,0:T(8,128)(2,1)S(1)}, u32[]{:S(2)}, u32[]{:S(2)}) collective-permute-start(bf16[1024,256]{1,0:T(8,128)(2,1)} %own_ref.1), channel_id=1, source_target_pairs={{0,1},{1,2},{2,3},{3,4},{4,5},{5,6},{6,7},{7,8},{8,9},{9,10},{10,1... | collective-permute-start | bytes 1572872 | tf_op jit(solution)/shard_map/ppermute | solution.py:13
  11.1 1.9 %collective-permute-start.1 = (bf16[1024,256]{1,0:T(8,128)(2,1)}, bf16[1024,256]{1,0:T(8,128)(2,1)S(1)}, u32[]{:S(2)}, u32[]{:S(2)}) collective-permute-start(bf16[1024,256]{1,0:T(8,128)(2,1)} %own_ref.1), channel_id=1, source_target_pairs={{1,0},{2,1},{3,2},{4,3},{5,4},{6,5},{7,6},{8,7},{9,8},{10,9},{11,1... | collective-permute-start | bytes 1572872 | tf_op jit(solution)/shard_map/ppermute | solution.py:14
  13.1 1.3 subtract_clamp_fusion.index_ref
  14.4 3.2 %collective-permute-done.low_ref = bf16[1024,256]{1,0:T(8,128)(2,1)S(1)} collective-permute-done((bf16[1024,256]{1,0:T(8,128)(2,1)}, bf16[1024,256]{1,0:T(8,128)(2,1)S(1)}, u32[]{:S(2)}, u32[]{:S(2)}) %collective-permute-start) | collective-permute-done | bytes 524320 | tf_op jit(solution)/shard_map/ppermute | solution.py:13
  17.6 0.0 copy-start
  17.6 4.3 %collective-permute-done.1.high_ref = bf16[1024,256]{1,0:T(8,128)(2,1)S(1)} collective-permute-done((bf16[1024,256]{1,0:T(8,128)(2,1)}, bf16[1024,256]{1,0:T(8,128)(2,1)S(1)}, u32[]{:S(2)}, u32[]{:S(2)}) %collective-permute-start.1) | collective-permute-done | bytes 524320 | tf_op jit(solution)/shard_map/ppermute | solution.py:14
  21.8 0.0 copy-start.1
  21.8 0.0 copy-done
  21.8 0.8 copy-done.1
  22.6 8.3 %shard_map.46 = bf16[1024,256]{1,0:T(8,128)(2,1)} custom-call(s32[8,16]{1,0:T(8,128)} %subtract_clamp_fusion.index_ref, s32[8,16]{1,0:T(8,128)} %mask_ref.1, bf16[1024,2048]{1,0:T(8,128)(2,1)} %bitcast.22, bf16[1024,256]{1,0:T(8,128)(2,1)} %copy-done, bf16[1024,256]{1,0:T(8,128)(2,1)} %own_ref.1, bf16[1024,256]{1,0:T(8,128)(2,1)} %copy-done.1), custom_call_target="tpu_custom_call" | custom-call | tf_op jit(solution)/shard_map/pallas_call | solution.py:52
  30.9 11.1 %all_to_all.5 = bf16[4,256,256]{2,1,0:T(8,128)(2,1)} all-to-all(bf16[4,256,256]{2,1,0:T(8,128)(2,1)} %bitcast.20), channel_id=1, replica_groups=mesh['aux'=4,'rzy'=16,'core'=2] {'aux'}, dimensions={0} | all-to-all | bytes 1048576 | tf_op jit(solution)/shard_map/all_to_all | solution.py:80
  42.0 0.0 all-gather.3.cloned.1.call-update
  42.0 1.8 %collective-permute-start.4 = (bf16[1024,256]{1,0:T(8,128)(2,1)}, bf16[1024,256]{1,0:T(8,128)(2,1)S(1)}, u32[]{:S(2)}, u32[]{:S(2)}) collective-permute-start(bf16[1024,256]{1,0:T(8,128)(2,1)} %shard_map.46), channel_id=1, source_target_pairs={{0,96},{32,0},{64,32},{96,64},{1,97},{33,1},{65,33},{97,65},{2,98}... | collective-permute-start | bytes 1572872 | tf_op jit(solution)/shard_map/ppermute | solution.py:79
  43.9 2.8 %collective-permute-start.3 = (bf16[1024,256]{1,0:T(8,128)(2,1)}, bf16[1024,256]{1,0:T(8,128)(2,1)S(1)}, u32[]{:S(2)}, u32[]{:S(2)}) collective-permute-start(bf16[1024,256]{1,0:T(8,128)(2,1)} %shard_map.46), channel_id=1, source_target_pairs={{0,64},{32,96},{64,0},{96,32},{1,65},{33,97},{65,1},{97,33},{2,66}... | collective-permute-start | bytes 1572872 | tf_op jit(solution)/shard_map/ppermute | solution.py:79
  46.7 0.0 collective-permute-start.2
  46.7 10.8 %collective-permute-done.4 = bf16[1024,256]{1,0:T(8,128)(2,1)S(1)} collective-permute-done((bf16[1024,256]{1,0:T(8,128)(2,1)}, bf16[1024,256]{1,0:T(8,128)(2,1)S(1)}, u32[]{:S(2)}, u32[]{:S(2)}) %collective-permute-start.4) | collective-permute-done | bytes 524320 | tf_op jit(solution)/shard_map/ppermute | solution.py:79
  57.6 1.8 %collective-permute-done.3 = bf16[1024,256]{1,0:T(8,128)(2,1)S(1)} collective-permute-done((bf16[1024,256]{1,0:T(8,128)(2,1)}, bf16[1024,256]{1,0:T(8,128)(2,1)S(1)}, u32[]{:S(2)}, u32[]{:S(2)}) %collective-permute-start.3) | collective-permute-done | bytes 524320 | tf_op jit(solution)/shard_map/ppermute | solution.py:79
  59.3 5.8 %collective-permute-done.2 = bf16[1024,256]{1,0:T(8,128)(2,1)S(1)} collective-permute-done((bf16[1024,256]{1,0:T(8,128)(2,1)}, bf16[1024,256]{1,0:T(8,128)(2,1)S(1)}, u32[]{:S(2)}, u32[]{:S(2)}) %collective-permute-start.2) | collective-permute-done | bytes 524320 | tf_op jit(solution)/shard_map/ppermute | solution.py:79
  65.1 0.0 copy-start.2
  65.1 0.8 copy-done.2
  65.9 1.5 pad_maximum_fusion
  67.4 2.0 %gather_fusion = bf16[4,1024,256]{2,1,0:T(8,128)(2,1)} fusion(bf16[4,1024,256]{2,1,0:T(8,128)(2,1)S(1)} %pad_maximum_fusion, s32[1024]{0:T(1024)S(1)} %pad_clamp_fusion), kind=kCustom, calls=%fused_computation | custom fusion | bytes 4194320 | tf_op jit(solution)/shard_map/jit(_take)/gather | solution.py:84
  69.4 51.0 %all-gather.3.cloned.1.call-done = bf16[128,256,256]{2,1,0:T(8,128)(2,1)} async-done(((bf16[4,256,256]{2,1,0:T(8,128)(2,1)}), bf16[128,256,256]{2,1,0:T(8,128)(2,1)}) %all-gather.3.cloned.1.call-update) | async-done | bytes 16777232 | tf_op jit(solution)/shard_map/all_gather | solution.py:85
  120.4 24.1 %fusion = bf16[1024,32,1,256]{3,0,1,2:T(8,128)(2,1)} fusion(bf16[32,4,256,256]{3,2,1,0:T(8,128)(2,1)} %bitcast.26, bf16[4,1024,256]{2,1,0:T(8,128)(2,1)} %gather_fusion, pred[4]{0:T(512)(128)(4,1)S(1)} %compare_and_fusion), kind=kOutput, calls=%fused_computation.2 | convolution fusion | flops 17189306368 | bytes 35651588 | tf_op jit(solution)/shard_map/pmi,rpki->mrk/dot_general | solution.py:86
  144.6 17.9 %copy.6 = bf16[1024,32,1,256]{3,1,2,0:T(8,128)(2,1)} copy(bf16[1024,32,1,256]{3,0,1,2:T(8,128)(2,1)} %fusion) | data formatting | bytes 33554432 | tf_op jit(solution)/shard_map/reshape | solution.py:87
  (3 shorter events, 0.0 us)
Async XLA Ops:
  6.5 113.9 %all-gather.3.cloned.1.call-start = ((), (), s32[]{:S(2)}) async-start(), calls=%async_computation.1 | async-start | bytes 17301504 | tf_op jit(solution)/shard_map/all_gather | solution.py:85
  6.5 11.0 %collective-permute-start = (bf16[1024,256]{1,0:T(8,128)(2,1)}, bf16[1024,256]{1,0:T(8,128)(2,1)S(1)}, u32[]{:S(2)}, u32[]{:S(2)}) collective-permute-start(bf16[1024,256]{1,0:T(8,128)(2,1)} %own_ref.1), channel_id=1, source_target_pairs={{0,1},{1,2},{2,3},{3,4},{4,5},{5,6},{6,7},{7,8},{8,9},{9,10},{10,1... | collective-permute-start | bytes 1572872 | tf_op jit(solution)/shard_map/ppermute | solution.py:13
  11.1 10.7 %collective-permute-start.1 = (bf16[1024,256]{1,0:T(8,128)(2,1)}, bf16[1024,256]{1,0:T(8,128)(2,1)S(1)}, u32[]{:S(2)}, u32[]{:S(2)}) collective-permute-start(bf16[1024,256]{1,0:T(8,128)(2,1)} %own_ref.1), channel_id=1, source_target_pairs={{1,0},{2,1},{3,2},{4,3},{5,4},{6,5},{7,6},{8,7},{9,8},{10,9},{11,1... | collective-permute-start | bytes 1572872 | tf_op jit(solution)/shard_map/ppermute | solution.py:14
  17.6 4.3 %copy-start = (bf16[1024,256]{1,0:T(8,128)(2,1)}, bf16[1024,256]{1,0:T(8,128)(2,1)S(1)}, u32[]{:S(2)}) copy-start(bf16[1024,256]{1,0:T(8,128)(2,1)S(1)} %collective-permute-done.low_ref) | copy-start | bytes 1572868
  21.8 0.8 copy-start.1
  42.0 15.5 %collective-permute-start.4 = (bf16[1024,256]{1,0:T(8,128)(2,1)}, bf16[1024,256]{1,0:T(8,128)(2,1)S(1)}, u32[]{:S(2)}, u32[]{:S(2)}) collective-permute-start(bf16[1024,256]{1,0:T(8,128)(2,1)} %shard_map.46), channel_id=1, source_target_pairs={{0,96},{32,0},{64,32},{96,64},{1,97},{33,1},{65,33},{97,65},{2,98}... | collective-permute-start | bytes 1572872 | tf_op jit(solution)/shard_map/ppermute | solution.py:79
  43.9 15.4 %collective-permute-start.3 = (bf16[1024,256]{1,0:T(8,128)(2,1)}, bf16[1024,256]{1,0:T(8,128)(2,1)S(1)}, u32[]{:S(2)}, u32[]{:S(2)}) collective-permute-start(bf16[1024,256]{1,0:T(8,128)(2,1)} %shard_map.46), channel_id=1, source_target_pairs={{0,64},{32,96},{64,0},{96,32},{1,65},{33,97},{65,1},{97,33},{2,66}... | collective-permute-start | bytes 1572872 | tf_op jit(solution)/shard_map/ppermute | solution.py:79
  46.7 18.5 %collective-permute-start.2 = (bf16[1024,256]{1,0:T(8,128)(2,1)}, bf16[1024,256]{1,0:T(8,128)(2,1)S(1)}, u32[]{:S(2)}, u32[]{:S(2)}) collective-permute-start(bf16[1024,256]{1,0:T(8,128)(2,1)} %shard_map.46), channel_id=1, source_target_pairs={{0,32},{32,64},{64,96},{96,0},{1,33},{33,65},{65,97},{97,1},{2,34}... | collective-permute-start | bytes 1572872 | tf_op jit(solution)/shard_map/ppermute | solution.py:79
  65.1 0.8 copy-start.2
Sparse Core Ops, SparseCore 0:
  42.2 78.2 all-gather.2

commit v10 on v9

--- a/solution.py
+++ b/solution.py
@@ -31,7 +31,12 @@
     local_index = jnp.clip(local_index, 0, window - 1).astype(jnp.int32)
     tiles = b_tiles.reshape(rows_local, stored)
 
-    def kernel(index_ref, mask_ref, tile_ref, low_ref, own_ref, high_ref, out_ref, coeff_ref, rhs_ref):
+    quarters = 4
+    quarter = stored // quarters
+
+    def kernel(index_ref, mask_ref, *refs):
+        tile_refs = refs[:quarters]
+        low_ref, own_ref, high_ref, out_ref, coeff_ref, rhs_ref = refs[quarters:]
         b = pl.program_id(0)
 
         @pl.when(b == 0)
@@ -45,7 +50,10 @@
             coeff = coeff_ref[pl.ds(start, block_size), :]
             coeff = jnp.where(mask_ref[b, s] != 0, coeff, jnp.zeros_like(coeff))
             rhs_ref[s * block_size:(s + 1) * block_size, :] = coeff
-        acc = jnp.dot(tile_ref[...], rhs_ref[...], preferred_element_type=jnp.float32)
+        acc = jnp.zeros(out_ref.shape, jnp.float32)
+        for q in range(quarters):
+            rhs = rhs_ref[q * quarter:(q + 1) * quarter, :]
+            acc = acc + jnp.dot(tile_refs[q][...], rhs, preferred_element_type=jnp.float32)
         out_ref[...] = acc.astype(out_ref.dtype)
 
     whole = pl.BlockSpec((rows_local, orbitals), lambda b, li, mk: (0, 0))
@@ -55,7 +63,10 @@
             num_scalar_prefetch=2,
             grid=(blocks_local,),
             in_specs=[
-                pl.BlockSpec((block_size, stored), lambda b, li, mk: (b, 0)),
+                pl.BlockSpec((block_size, quarter), lambda b, li, mk, q=q: (b, q))
+                for q in range(quarters)
+            ]
+            + [
                 whole,
                 whole,
                 whole,
@@ -68,7 +79,7 @@
         ),
         out_shape=jax.ShapeDtypeStruct((rows_local, orbitals), jnp.bfloat16),
         compiler_params=pltpu.CompilerParams(dimension_semantics=("arbitrary",)),
-    )(local_index, screen_mask, tiles, low, occ_coeff, high)
+    )(local_index, screen_mask, *([tiles] * quarters), low, occ_coeff, high)
     half_local = half_local.reshape(p_local, rows_local, orbitals)
     aux_index = lax.axis_index("aux")
     share = rows_local // aux_count

time: 170 us -> 170 us (level)
  no operation moved by 1% of the time
where the time goes in v10:
time: 170 us; the launch traced here: 169 us
  waiting for transfers between devices  77 us (45%)
  matrix products  24.2 us (14%)
  local copies, waits for them, and re-layouts  21.5 us (13%)
  between operations  13.4 us (8%)
  starting transfers between devices  11.1 us (7%)
  blocking collectives  11.1 us (7%)
  Pallas kernels  8.4 us (5%)
  other arithmetic  2.78 us (2%)
    all_gather x1, waiting for transfers between devices, per_device(): partner = lax.all_gather(piece, ROW, axis=0)  51 us
    dot_general x1, matrix products, per_device(): jnp.einsum('pmi,rpki->mrk', slab_rows, partner, preferred_element_type=jn...  24.2 us
    ppermute x3, waiting for transfers between devices, per_device(): shifted.append(lax.ppermute(own, 'aux', pairs))  18.4 us
    reshape x1, local copies, waits for them, and re-layouts, per_device(): result.astype(jnp.bfloat16).reshape(rows_local, partner.shape[0], 1, share)  17.9 us
    all_to_all x1, blocking collectives, per_device(): lax.all_to_all(own.reshape(aux_count, share, orbitals), 'aux', 0, 0, tile...  11.1 us
    pallas_call x1, Pallas kernels, per_device(): pl.pallas_call(kernel, grid_spec=pltpu.PrefetchScalarGridSpec(num_scalar_...  8.4 us
    ppermute x3, starting transfers between devices, per_device(): shifted.append(lax.ppermute(own, 'aux', pairs))  4.62 us
    ppermute x1, starting transfers between devices, halo_pieces(): lax.ppermute(lax.slice_in_dim(block, block.shape[0] - width, None, axis=0...  4.58 us
  transfers between devices with their start and end apart: 6, of which 6 were waited for; matrix products, arithmetic and copies ran while one was open for 3% of the time, Pallas kernels for 0%

profile of v10, /device:TPU:1, one launch (start us, length us, event | category | flops | bytes accessed | tf_op | source)
XLA Modules:
  0.0 169.4 jit_solution(10262015982433778983)
XLA Ops:
  6.5 0.0 all-gather.3.cloned.1.call-start
  6.5 4.6 %collective-permute-start = (bf16[1024,256]{1,0:T(8,128)(2,1)}, bf16[1024,256]{1,0:T(8,128)(2,1)S(1)}, u32[]{:S(2)}, u32[]{:S(2)}) collective-permute-start(bf16[1024,256]{1,0:T(8,128)(2,1)} %refs_5_.1), channel_id=1, source_target_pairs={{0,1},{1,2},{2,3},{3,4},{4,5},{5,6},{6,7},{7,8},{8,9},{9,10},{10,1... | collective-permute-start | bytes 1572872 | tf_op jit(solution)/shard_map/ppermute | solution.py:13
  11.1 1.9 %collective-permute-start.1 = (bf16[1024,256]{1,0:T(8,128)(2,1)}, bf16[1024,256]{1,0:T(8,128)(2,1)S(1)}, u32[]{:S(2)}, u32[]{:S(2)}) collective-permute-start(bf16[1024,256]{1,0:T(8,128)(2,1)} %refs_5_.1), channel_id=1, source_target_pairs={{1,0},{2,1},{3,2},{4,3},{5,4},{6,5},{7,6},{8,7},{9,8},{10,9},{11,1... | collective-permute-start | bytes 1572872 | tf_op jit(solution)/shard_map/ppermute | solution.py:14
  13.1 1.3 subtract_clamp_fusion.index_ref
  14.4 3.2 %collective-permute-done.refs_4_ = bf16[1024,256]{1,0:T(8,128)(2,1)S(1)} collective-permute-done((bf16[1024,256]{1,0:T(8,128)(2,1)}, bf16[1024,256]{1,0:T(8,128)(2,1)S(1)}, u32[]{:S(2)}, u32[]{:S(2)}) %collective-permute-start) | collective-permute-done | bytes 524320 | tf_op jit(solution)/shard_map/ppermute | solution.py:13
  17.6 0.0 copy-start
  17.6 4.3 %collective-permute-done.1.refs_6_ = bf16[1024,256]{1,0:T(8,128)(2,1)S(1)} collective-permute-done((bf16[1024,256]{1,0:T(8,128)(2,1)}, bf16[1024,256]{1,0:T(8,128)(2,1)S(1)}, u32[]{:S(2)}, u32[]{:S(2)}) %collective-permute-start.1) | collective-permute-done | bytes 524320 | tf_op jit(solution)/shard_map/ppermute | solution.py:14
  21.8 0.0 copy-start.1
  21.8 0.0 copy-done
  21.8 0.8 copy-done.1
  22.6 8.4 %shard_map.46 = bf16[1024,256]{1,0:T(8,128)(2,1)} custom-call(s32[8,16]{1,0:T(8,128)} %subtract_clamp_fusion.index_ref, s32[8,16]{1,0:T(8,128)} %mask_ref.1, bf16[1024,2048]{1,0:T(8,128)(2,1)} %bitcast.20, bf16[1024,2048]{1,0:T(8,128)(2,1)} %bitcast.21, bf16[1024,2048]{1,0:T(8,128)(2,1)} %bitcast.22, bf16[1024,2048]{1,0:T(8,128)(2,1)} %bitcast.23, ...), custom_call_target="tpu_custom_call" | custom-call | tf_op jit(solution)/shard_map/pallas_call | solution.py:60
  31.0 11.1 %all_to_all.5 = bf16[4,256,256]{2,1,0:T(8,128)(2,1)} all-to-all(bf16[4,256,256]{2,1,0:T(8,128)(2,1)} %bitcast.24), channel_id=1, replica_groups=mesh['aux'=4,'rzy'=16,'core'=2] {'aux'}, dimensions={0} | all-to-all | bytes 1048576 | tf_op jit(solution)/shard_map/all_to_all | solution.py:91
  42.2 0.0 all-gather.3.cloned.1.call-update
  42.2 1.8 %collective-permute-start.4 = (bf16[1024,256]{1,0:T(8,128)(2,1)}, bf16[1024,256]{1,0:T(8,128)(2,1)S(1)}, u32[]{:S(2)}, u32[]{:S(2)}) collective-permute-start(bf16[1024,256]{1,0:T(8,128)(2,1)} %shard_map.46), channel_id=1, source_target_pairs={{0,96},{32,0},{64,32},{96,64},{1,97},{33,1},{65,33},{97,65},{2,98}... | collective-permute-start | bytes 1572872 | tf_op jit(solution)/shard_map/ppermute | solution.py:90
  44.0 2.8 %collective-permute-start.3 = (bf16[1024,256]{1,0:T(8,128)(2,1)}, bf16[1024,256]{1,0:T(8,128)(2,1)S(1)}, u32[]{:S(2)}, u32[]{:S(2)}) collective-permute-start(bf16[1024,256]{1,0:T(8,128)(2,1)} %shard_map.46), channel_id=1, source_target_pairs={{0,64},{32,96},{64,0},{96,32},{1,65},{33,97},{65,1},{97,33},{2,66}... | collective-permute-start | bytes 1572872 | tf_op jit(solution)/shard_map/ppermute | solution.py:90
  46.8 0.0 collective-permute-start.2
  46.9 10.8 %collective-permute-done.4 = bf16[1024,256]{1,0:T(8,128)(2,1)S(1)} collective-permute-done((bf16[1024,256]{1,0:T(8,128)(2,1)}, bf16[1024,256]{1,0:T(8,128)(2,1)S(1)}, u32[]{:S(2)}, u32[]{:S(2)}) %collective-permute-start.4) | collective-permute-done | bytes 524320 | tf_op jit(solution)/shard_map/ppermute | solution.py:90
  57.7 1.7 %collective-permute-done.3 = bf16[1024,256]{1,0:T(8,128)(2,1)S(1)} collective-permute-done((bf16[1024,256]{1,0:T(8,128)(2,1)}, bf16[1024,256]{1,0:T(8,128)(2,1)S(1)}, u32[]{:S(2)}, u32[]{:S(2)}) %collective-permute-start.3) | collective-permute-done | bytes 524320 | tf_op jit(solution)/shard_map/ppermute | solution.py:90
  59.4 5.9 %collective-permute-done.2 = bf16[1024,256]{1,0:T(8,128)(2,1)S(1)} collective-permute-done((bf16[1024,256]{1,0:T(8,128)(2,1)}, bf16[1024,256]{1,0:T(8,128)(2,1)S(1)}, u32[]{:S(2)}, u32[]{:S(2)}) %collective-permute-start.2) | collective-permute-done | bytes 524320 | tf_op jit(solution)/shard_map/ppermute | solution.py:90
  65.3 0.0 copy-start.2
  65.3 0.8 copy-done.2
  66.1 1.5 pad_maximum_fusion
  67.5 2.0 %gather_fusion = bf16[4,1024,256]{2,1,0:T(8,128)(2,1)} fusion(bf16[4,1024,256]{2,1,0:T(8,128)(2,1)S(1)} %pad_maximum_fusion, s32[1024]{0:T(1024)S(1)} %pad_clamp_fusion), kind=kCustom, calls=%fused_computation | custom fusion | bytes 4194320 | tf_op jit(solution)/shard_map/jit(_take)/gather | solution.py:95
  69.5 51.0 %all-gather.3.cloned.1.call-done = bf16[128,256,256]{2,1,0:T(8,128)(2,1)} async-done(((bf16[4,256,256]{2,1,0:T(8,128)(2,1)}), bf16[128,256,256]{2,1,0:T(8,128)(2,1)}) %all-gather.3.cloned.1.call-update) | async-done | bytes 16777232 | tf_op jit(solution)/shard_map/all_gather | solution.py:96
  120.6 24.2 %fusion = bf16[1024,32,1,256]{3,0,1,2:T(8,128)(2,1)} fusion(bf16[32,4,256,256]{3,2,1,0:T(8,128)(2,1)} %bitcast.29, bf16[4,1024,256]{2,1,0:T(8,128)(2,1)} %gather_fusion, pred[4]{0:T(512)(128)(4,1)S(1)} %compare_and_fusion), kind=kOutput, calls=%fused_computation.2 | convolution fusion | flops 17189306368 | bytes 35651588 | tf_op jit(solution)/shard_map/pmi,rpki->mrk/dot_general | solution.py:97
  144.7 17.9 %copy.6 = bf16[1024,32,1,256]{3,1,2,0:T(8,128)(2,1)} copy(bf16[1024,32,1,256]{3,0,1,2:T(8,128)(2,1)} %fusion) | data formatting | bytes 33554432 | tf_op jit(solution)/shard_map/reshape | solution.py:98
  (3 shorter events, 0.0 us)
Async XLA Ops:
  6.5 114.0 %all-gather.3.cloned.1.call-start = ((), (), s32[]{:S(2)}) async-start(), calls=%async_computation.1 | async-start | bytes 17301504 | tf_op jit(solution)/shard_map/all_gather | solution.py:96
  6.5 11.0 %collective-permute-start = (bf16[1024,256]{1,0:T(8,128)(2,1)}, bf16[1024,256]{1,0:T(8,128)(2,1)S(1)}, u32[]{:S(2)}, u32[]{:S(2)}) collective-permute-start(bf16[1024,256]{1,0:T(8,128)(2,1)} %refs_5_.1), channel_id=1, source_target_pairs={{0,1},{1,2},{2,3},{3,4},{4,5},{5,6},{6,7},{7,8},{8,9},{9,10},{10,1... | collective-permute-start | bytes 1572872 | tf_op jit(solution)/shard_map/ppermute | solution.py:13
  11.1 10.7 %collective-permute-start.1 = (bf16[1024,256]{1,0:T(8,128)(2,1)}, bf16[1024,256]{1,0:T(8,128)(2,1)S(1)}, u32[]{:S(2)}, u32[]{:S(2)}) collective-permute-start(bf16[1024,256]{1,0:T(8,128)(2,1)} %refs_5_.1), channel_id=1, source_target_pairs={{1,0},{2,1},{3,2},{4,3},{5,4},{6,5},{7,6},{8,7},{9,8},{10,9},{11,1... | collective-permute-start | bytes 1572872 | tf_op jit(solution)/shard_map/ppermute | solution.py:14
  17.6 4.3 %copy-start = (bf16[1024,256]{1,0:T(8,128)(2,1)}, bf16[1024,256]{1,0:T(8,128)(2,1)S(1)}, u32[]{:S(2)}) copy-start(bf16[1024,256]{1,0:T(8,128)(2,1)S(1)} %collective-permute-done.refs_4_) | copy-start | bytes 1572868
  21.8 0.8 copy-start.1
  42.2 15.5 %collective-permute-start.4 = (bf16[1024,256]{1,0:T(8,128)(2,1)}, bf16[1024,256]{1,0:T(8,128)(2,1)S(1)}, u32[]{:S(2)}, u32[]{:S(2)}) collective-permute-start(bf16[1024,256]{1,0:T(8,128)(2,1)} %shard_map.46), channel_id=1, source_target_pairs={{0,96},{32,0},{64,32},{96,64},{1,97},{33,1},{65,33},{97,65},{2,98}... | collective-permute-start | bytes 1572872 | tf_op jit(solution)/shard_map/ppermute | solution.py:90
  44.0 15.4 %collective-permute-start.3 = (bf16[1024,256]{1,0:T(8,128)(2,1)}, bf16[1024,256]{1,0:T(8,128)(2,1)S(1)}, u32[]{:S(2)}, u32[]{:S(2)}) collective-permute-start(bf16[1024,256]{1,0:T(8,128)(2,1)} %shard_map.46), channel_id=1, source_target_pairs={{0,64},{32,96},{64,0},{96,32},{1,65},{33,97},{65,1},{97,33},{2,66}... | collective-permute-start | bytes 1572872 | tf_op jit(solution)/shard_map/ppermute | solution.py:90
  46.8 18.5 %collective-permute-start.2 = (bf16[1024,256]{1,0:T(8,128)(2,1)}, bf16[1024,256]{1,0:T(8,128)(2,1)S(1)}, u32[]{:S(2)}, u32[]{:S(2)}) collective-permute-start(bf16[1024,256]{1,0:T(8,128)(2,1)} %shard_map.46), channel_id=1, source_target_pairs={{0,32},{32,64},{64,96},{96,0},{1,33},{33,65},{65,97},{97,1},{2,34}... | collective-permute-start | bytes 1572872 | tf_op jit(solution)/shard_map/ppermute | solution.py:90
  65.3 0.8 copy-start.2
Sparse Core Ops, SparseCore 0:
  42.3 78.2 all-gather.2

commit v11 on v10

--- a/solution.py
+++ b/solution.py
@@ -93,9 +93,13 @@
     )
     order = (aux_index - jnp.arange(aux_count)) % aux_count
     slab_rows = jnp.take(jnp.stack(shifted), order, axis=0)
+    piece = jnp.transpose(piece, (1, 0, 2))
     partner = lax.all_gather(piece, ROW, axis=0)
-    result = jnp.einsum("pmi,rpki->mrk", slab_rows, partner, preferred_element_type=jnp.float32)
-    return result.astype(jnp.bfloat16).reshape(rows_local, partner.shape[0], 1, share)
+    row_count = partner.shape[0]
+    partner = partner.reshape(row_count * share, aux_count * orbitals)
+    slab_rows = jnp.transpose(slab_rows, (1, 0, 2)).reshape(rows_local, aux_count * orbitals)
+    result = jnp.einsum("mq,lq->ml", slab_rows, partner, preferred_element_type=jnp.float32)
+    return result.astype(jnp.bfloat16).reshape(rows_local, row_count, 1, share)
 
 
 def solution(mesh):

time: 170 us -> 181 us (1.065)
  waiting for transfers between devices: 77 us -> 81.4 us
  matrix products: 24.2 us -> 27.3 us
  other arithmetic: 2.78 us -> 4.7 us
    reshape x1 -> x0, local copies, waits for them, and re-layouts: 17.9 us -> none  [per_device(): result.astype(jnp.bfloat16).reshape(rows_local, partner.shape[0], 1, share)]
    unnamed x6 -> x11, local copies, waits for them, and re-layouts: 1.59 us -> 17.3 us
    all_gather x1, waiting for transfers between devices: 51 us -> 55.4 us  [per_device(): partner = lax.all_gather(piece, ROW, axis=0)]
    dot_general x1, matrix products: 24.2 us -> 27.3 us  [per_device(): jnp.einsum('mq,lq->ml', slab_rows, partner, preferred_element_type=jnp.fl...]
    select_n x0 -> x1, local copies, waits for them, and re-layouts: none -> 2.38 us  [per_device(): slab_rows = jnp.take(jnp.stack(shifted), order, axis=0)]
    select_n x1 -> x2, other arithmetic: 0.01 us -> 1.91 us  [per_device(): slab_rows = jnp.take(jnp.stack(shifted), order, axis=0)]
  transfers between devices with their start and end apart: 6 -> 6, of which waited for: 6 -> 6; matrix products, arithmetic and copies ran while one was open for 3% -> 5% of each run, Pallas kernels for 0% -> 0%
where the time goes in v11:
time: 181 us; the launch traced here: 180 us
  waiting for transfers between devices  81.4 us (45%)
  matrix products  27.3 us (15%)
  local copies, waits for them, and re-layouts  22.9 us (13%)
  between operations  13.5 us (7%)
  starting transfers between devices  11.2 us (6%)
  blocking collectives  10.8 us (6%)
  Pallas kernels  8.38 us (5%)
  other arithmetic  4.7 us (3%)
    all_gather x1, waiting for transfers between devices, per_device(): partner = lax.all_gather(piece, ROW, axis=0)  55.4 us
    dot_general x1, matrix products, per_device(): jnp.einsum('mq,lq->ml', slab_rows, partner, preferred_element_type=jnp.fl...  27.3 us
    ppermute x3, waiting for transfers between devices, per_device(): shifted.append(lax.ppermute(own, 'aux', pairs))  18.5 us
    unnamed x11, local copies, waits for them, and re-layouts  17.3 us
    all_to_all x1, blocking collectives, per_device(): lax.all_to_all(own.reshape(aux_count, share, orbitals), 'aux', 0, 0, tile...  10.8 us
    pallas_call x1, Pallas kernels, per_device(): pl.pallas_call(kernel, grid_spec=pltpu.PrefetchScalarGridSpec(num_scalar_...  8.38 us
    ppermute x3, starting transfers between devices, per_device(): shifted.append(lax.ppermute(own, 'aux', pairs))  4.67 us
    ppermute x1, starting transfers between devices, halo_pieces(): lax.ppermute(lax.slice_in_dim(block, block.shape[0] - width, None, axis=0...  4.58 us
  transfers between devices with their start and end apart: 6, of which 6 were waited for; matrix products, arithmetic and copies ran while one was open for 5% of the time, Pallas kernels for 0%

profile of v11, /device:TPU:1, one launch (start us, length us, event | category | flops | bytes accessed | tf_op | source)
XLA Modules:
  0.0 180.1 jit_solution(17149587376269485986)
XLA Ops:
  6.5 0.0 all-gather.3.cloned.1.call-start
  6.5 4.6 %collective-permute-start = (bf16[1024,256]{1,0:T(8,128)(2,1)}, bf16[1024,256]{1,0:T(8,128)(2,1)S(1)}, u32[]{:S(2)}, u32[]{:S(2)}) collective-permute-start(bf16[1024,256]{1,0:T(8,128)(2,1)} %refs_5_.1), channel_id=1, source_target_pairs={{0,1},{1,2},{2,3},{3,4},{4,5},{5,6},{6,7},{7,8},{8,9},{9,10},{10,1... | collective-permute-start | bytes 1572872 | tf_op jit(solution)/shard_map/ppermute | solution.py:13
  11.1 1.9 %collective-permute-start.1 = (bf16[1024,256]{1,0:T(8,128)(2,1)}, bf16[1024,256]{1,0:T(8,128)(2,1)S(1)}, u32[]{:S(2)}, u32[]{:S(2)}) collective-permute-start(bf16[1024,256]{1,0:T(8,128)(2,1)} %refs_5_.1), channel_id=1, source_target_pairs={{1,0},{2,1},{3,2},{4,3},{5,4},{6,5},{7,6},{8,7},{9,8},{10,9},{11,1... | collective-permute-start | bytes 1572872 | tf_op jit(solution)/shard_map/ppermute | solution.py:14
  13.1 1.3 subtract_clamp_fusion.index_ref
  14.4 3.2 %collective-permute-done.refs_4_ = bf16[1024,256]{1,0:T(8,128)(2,1)S(1)} collective-permute-done((bf16[1024,256]{1,0:T(8,128)(2,1)}, bf16[1024,256]{1,0:T(8,128)(2,1)S(1)}, u32[]{:S(2)}, u32[]{:S(2)}) %collective-permute-start) | collective-permute-done | bytes 524320 | tf_op jit(solution)/shard_map/ppermute | solution.py:13
  17.6 0.0 copy-start.1
  17.6 4.3 %collective-permute-done.1.refs_6_ = bf16[1024,256]{1,0:T(8,128)(2,1)S(1)} collective-permute-done((bf16[1024,256]{1,0:T(8,128)(2,1)}, bf16[1024,256]{1,0:T(8,128)(2,1)S(1)}, u32[]{:S(2)}, u32[]{:S(2)}) %collective-permute-start.1) | collective-permute-done | bytes 524320 | tf_op jit(solution)/shard_map/ppermute | solution.py:14
  21.8 0.0 copy-start.2
  21.8 0.0 copy-done.1
  21.8 0.8 copy-done.2
  22.6 8.4 %shard_map.46 = bf16[1024,256]{1,0:T(8,128)(2,1)} custom-call(s32[8,16]{1,0:T(8,128)} %subtract_clamp_fusion.index_ref, s32[8,16]{1,0:T(8,128)} %mask_ref.1, bf16[1024,2048]{1,0:T(8,128)(2,1)} %bitcast.21, bf16[1024,2048]{1,0:T(8,128)(2,1)} %bitcast.22, bf16[1024,2048]{1,0:T(8,128)(2,1)} %bitcast.23, bf16[1024,2048]{1,0:T(8,128)(2,1)} %bitcast.24, ...), custom_call_target="tpu_custom_call" | custom-call | tf_op jit(solution)/shard_map/pallas_call | solution.py:60
  31.0 0.0 copy-start
  31.0 1.3 copy.7
  32.4 10.8 %all_to_all.5 = bf16[4,256,256]{1,2,0:T(8,128)(2,1)} all-to-all(bf16[4,256,256]{1,2,0:T(8,128)(2,1)S(1)} %copy.7), channel_id=1, replica_groups=mesh['aux'=4,'rzy'=16,'core'=2] {'aux'}, dimensions={0} | all-to-all | bytes 1048576 | tf_op jit(solution)/shard_map/all_to_all | solution.py:91
  43.2 0.0 all-gather.3.cloned.1.call-update
  43.2 0.0 copy-done
  43.2 1.8 collective-permute-start.4
  45.0 2.9 %collective-permute-start.3 = (bf16[1024,256]{1,0:T(8,128)(2,1)S(1)}, bf16[1024,256]{1,0:T(8,128)(2,1)S(1)}, u32[]{:S(2)}, u32[]{:S(2)}) collective-permute-start(bf16[1024,256]{1,0:T(8,128)(2,1)S(1)} %copy-done), channel_id=1, source_target_pairs={{0,64},{32,96},{64,0},{96,32},{1,65},{33,97},{65,1},{97,33},{2,66}... | collective-permute-start | bytes 1572872 | tf_op jit(solution)/shard_map/ppermute | solution.py:90
  47.9 0.0 collective-permute-start.2
  47.9 10.7 %collective-permute-done.4 = bf16[1024,256]{1,0:T(8,128)(2,1)S(1)} collective-permute-done((bf16[1024,256]{1,0:T(8,128)(2,1)S(1)}, bf16[1024,256]{1,0:T(8,128)(2,1)S(1)}, u32[]{:S(2)}, u32[]{:S(2)}) %collective-permute-start.4) | collective-permute-done | bytes 524320 | tf_op jit(solution)/shard_map/ppermute | solution.py:90
  58.7 1.5 collective-permute-done.3
  60.2 0.0 copy-start.3
  60.2 6.3 %collective-permute-done.2 = bf16[1024,256]{1,0:T(8,128)(2,1)S(1)} collective-permute-done((bf16[1024,256]{1,0:T(8,128)(2,1)S(1)}, bf16[1024,256]{1,0:T(8,128)(2,1)S(1)}, u32[]{:S(2)}, u32[]{:S(2)}) %collective-permute-start.2) | collective-permute-done | bytes 524320 | tf_op jit(solution)/shard_map/ppermute | solution.py:90
  66.5 0.0 copy-done.3
  66.5 0.8 copy-done.4
  67.3 1.5 pad_maximum_fusion
  68.8 2.0 %gather_fusion = bf16[4,1024,256]{2,1,0:T(8,128)(2,1)} fusion(bf16[4,1024,256]{2,1,0:T(8,128)(2,1)S(1)} %pad_maximum_fusion, s32[1024]{0:T(1024)S(1)} %pad_clamp_fusion), kind=kCustom, calls=%fused_computation | custom fusion | bytes 4194320 | tf_op jit(solution)/shard_map/jit(_take)/gather | solution.py:95
  70.8 1.9 %select_bitcast_fusion = bf16[1024,4,256]{2,0,1:T(8,128)(2,1)S(1)} fusion(bf16[4,1024,256]{2,1,0:T(8,128)(2,1)} %gather_fusion, pred[4]{0:T(512)(128)(4,1)S(1)} %compare_and_fusion), kind=kLoop, calls=%fused_computation.3 | loop fusion | flops 1048576 | bytes 4194308 | tf_op jit(solution)/shard_map/jit(_take)/select_n | solution.py:95
  72.7 2.4 %copy.6 = bf16[1024,4,256]{0,2,1:T(8,128)(2,1)} copy(bf16[1024,4,256]{2,0,1:T(8,128)(2,1)S(1)} %select_bitcast_fusion) | data formatting | bytes 4194304 | tf_op jit(solution)/shard_map/jit(_take)/select_n | solution.py:95
  75.0 55.4 %all-gather.3.cloned.1.call-done = bf16[8192,4,256]{0,2,1:T(8,128)(2,1)} async-done(((bf16[256,4,256]{0,2,1:T(8,128)(2,1)}), bf16[8192,4,256]{0,2,1:T(8,128)(2,1)}) %all-gather.3.cloned.1.call-update) | async-done | bytes 16777232 | tf_op jit(solution)/shard_map/all_gather | solution.py:97
  130.4 27.3 %convolution_convert_fusion = bf16[1024,8192]{1,0:T(8,128)(2,1)} fusion(bf16[1024,1024]{0,1:T(8,128)(2,1)} %bitcast.28, bf16[8192,1024]{0,1:T(8,128)(2,1)} %bitcast.33), kind=kOutput, calls=%fused_computation.1 | convolution fusion | flops 17188257792 | bytes 35651584 | tf_op jit(solution)/shard_map/mq,lq->ml/dot_general | solution.py:101
  157.6 15.6 %copy.9 = bf16[128,8,32,256]{3,2,1,0:T(8,128)(2,1)} copy(bf16[128,8,32,256]{3,1,2,0:T(8,128)(2,1)} %bitcast.25) | data formatting | bytes 33554432
  (4 shorter events, 0.0 us)
Async XLA Ops:
  6.5 123.8 %all-gather.3.cloned.1.call-start = ((), (), s32[]{:S(2)}) async-start(), calls=%async_computation.1 | async-start | bytes 17301504 | tf_op jit(solution)/shard_map/all_gather | solution.py:97
  6.5 11.0 %collective-permute-start = (bf16[1024,256]{1,0:T(8,128)(2,1)}, bf16[1024,256]{1,0:T(8,128)(2,1)S(1)}, u32[]{:S(2)}, u32[]{:S(2)}) collective-permute-start(bf16[1024,256]{1,0:T(8,128)(2,1)} %refs_5_.1), channel_id=1, source_target_pairs={{0,1},{1,2},{2,3},{3,4},{4,5},{5,6},{6,7},{7,8},{8,9},{9,10},{10,1... | collective-permute-start | bytes 1572872 | tf_op jit(solution)/shard_map/ppermute | solution.py:13
  11.1 10.7 %collective-permute-start.1 = (bf16[1024,256]{1,0:T(8,128)(2,1)}, bf16[1024,256]{1,0:T(8,128)(2,1)S(1)}, u32[]{:S(2)}, u32[]{:S(2)}) collective-permute-start(bf16[1024,256]{1,0:T(8,128)(2,1)} %refs_5_.1), channel_id=1, source_target_pairs={{1,0},{2,1},{3,2},{4,3},{5,4},{6,5},{7,6},{8,7},{9,8},{10,9},{11,1... | collective-permute-start | bytes 1572872 | tf_op jit(solution)/shard_map/ppermute | solution.py:14
  17.6 4.3 %copy-start.1 = (bf16[1024,256]{1,0:T(8,128)(2,1)}, bf16[1024,256]{1,0:T(8,128)(2,1)S(1)}, u32[]{:S(2)}) copy-start(bf16[1024,256]{1,0:T(8,128)(2,1)S(1)} %collective-permute-done.refs_4_) | copy-start | bytes 1572868
  21.8 0.8 copy-start.2
  31.0 12.2 %copy-start = (bf16[1024,256]{1,0:T(8,128)(2,1)S(1)}, bf16[1024,256]{1,0:T(8,128)(2,1)}, u32[]{:S(2)}) copy-start(bf16[1024,256]{1,0:T(8,128)(2,1)} %shard_map.46) | copy-start | bytes 1572868
  43.2 15.4 %collective-permute-start.4 = (bf16[1024,256]{1,0:T(8,128)(2,1)S(1)}, bf16[1024,256]{1,0:T(8,128)(2,1)S(1)}, u32[]{:S(2)}, u32[]{:S(2)}) collective-permute-start(bf16[1024,256]{1,0:T(8,128)(2,1)S(1)} %copy-done), channel_id=1, source_target_pairs={{0,96},{32,0},{64,32},{96,64},{1,97},{33,1},{65,33},{97,65},{2,98}... | collective-permute-start | bytes 1572872 | tf_op jit(solution)/shard_map/ppermute | solution.py:90
  45.0 15.2 %collective-permute-start.3 = (bf16[1024,256]{1,0:T(8,128)(2,1)S(1)}, bf16[1024,256]{1,0:T(8,128)(2,1)S(1)}, u32[]{:S(2)}, u32[]{:S(2)}) collective-permute-start(bf16[1024,256]{1,0:T(8,128)(2,1)S(1)} %copy-done), channel_id=1, source_target_pairs={{0,64},{32,96},{64,0},{96,32},{1,65},{33,97},{65,1},{97,33},{2,66}... | collective-permute-start | bytes 1572872 | tf_op jit(solution)/shard_map/ppermute | solution.py:90
  47.9 18.6 %collective-permute-start.2 = (bf16[1024,256]{1,0:T(8,128)(2,1)S(1)}, bf16[1024,256]{1,0:T(8,128)(2,1)S(1)}, u32[]{:S(2)}, u32[]{:S(2)}) collective-permute-start(bf16[1024,256]{1,0:T(8,128)(2,1)S(1)} %copy-done), channel_id=1, source_target_pairs={{0,32},{32,64},{64,96},{96,0},{1,33},{33,65},{65,97},{97,1},{2,34}... | collective-permute-start | bytes 1572872 | tf_op jit(solution)/shard_map/ppermute | solution.py:90
  60.2 6.3 %copy-start.3 = (bf16[1024,256]{1,0:T(8,128)(2,1)}, bf16[1024,256]{1,0:T(8,128)(2,1)S(1)}, u32[]{:S(2)}) copy-start(bf16[1024,256]{1,0:T(8,128)(2,1)S(1)} %collective-permute-done.3) | copy-start | bytes 1572868
  66.5 0.8 copy-start.4
Sparse Core Ops, SparseCore 0:
  43.3 87.0 all-gather.2

commit v12 on v10

--- a/solution.py
+++ b/solution.py
@@ -94,8 +94,22 @@
     order = (aux_index - jnp.arange(aux_count)) % aux_count
     slab_rows = jnp.take(jnp.stack(shifted), order, axis=0)
     partner = lax.all_gather(piece, ROW, axis=0)
-    result = jnp.einsum("pmi,rpki->mrk", slab_rows, partner, preferred_element_type=jnp.float32)
-    return result.astype(jnp.bfloat16).reshape(rows_local, partner.shape[0], 1, share)
+    result = jnp.einsum("pmi,rpki->rmk", slab_rows, partner, preferred_element_type=jnp.float32)
+    result = result.astype(jnp.bfloat16)
+    row_count = partner.shape[0]
+    rows_tile = 64
+
+    def relayout(in_ref, out_ref):
+        out_ref[...] = pltpu.einshape("rmk->mrk", in_ref[...])
+
+    result = pl.pallas_call(
+        relayout,
+        grid=(rows_local // rows_tile,),
+        in_specs=[pl.BlockSpec((row_count, rows_tile, share), lambda i: (0, i, 0))],
+        out_specs=pl.BlockSpec((rows_tile, row_count, share), lambda i: (i, 0, 0)),
+        out_shape=jax.ShapeDtypeStruct((rows_local, row_count, share), jnp.bfloat16),
+    )(result)
+    return result.reshape(rows_local, row_count, 1, share)
 
 
 def solution(mesh):

time: 170 us -> 173 us (1.018)
  Pallas kernels: 8.4 us -> 27.1 us
  local copies, waits for them, and re-layouts: 21.5 us -> 3.59 us
  matrix products: 24.2 us -> 26.5 us
    pallas_call x0 -> x1, Pallas kernels: none -> 18.7 us  [per_device(): pl.pallas_call(relayout, grid=(rows_local // rows_tile,), in_specs=[pl.Bl...]
    reshape x1 -> x0, local copies, waits for them, and re-layouts: 17.9 us -> none  [per_device(): result.astype(jnp.bfloat16).reshape(rows_local, partner.shape[0], 1, share)]
    dot_general x1, matrix products: 24.2 us -> 26.5 us  [per_device(): jnp.einsum('pmi,rpki->rmk', slab_rows, partner, preferred_element_type=jn...]
where the time goes in v12:
time: 173 us
  waiting for transfers between devices  77 us (45%)
  Pallas kernels  27.1 us (16%)
  matrix products  26.5 us (15%)
  between operations  13.4 us (8%)
  starting transfers between devices  11.1 us (6%)
  blocking collectives  11.1 us (6%)
  local copies, waits for them, and re-layouts  3.59 us (2%)
  other arithmetic  2.78 us (2%)
    all_gather x1, waiting for transfers between devices, per_device(): partner = lax.all_gather(piece, ROW, axis=0)  51 us
    dot_general x1, matrix products, per_device(): jnp.einsum('pmi,rpki->rmk', slab_rows, partner, preferred_element_type=jn...  26.5 us
    pallas_call x1, Pallas kernels, per_device(): pl.pallas_call(relayout, grid=(rows_local // rows_tile,), in_specs=[pl.Bl...  18.7 us
    ppermute x3, waiting for transfers between devices, per_device(): shifted.append(lax.ppermute(own, 'aux', pairs))  18.4 us
    all_to_all x1, blocking collectives, per_device(): lax.all_to_all(own.reshape(aux_count, share, orbitals), 'aux', 0, 0, tile...  11.1 us
    pallas_call x1, Pallas kernels, per_device(): pl.pallas_call(kernel, grid_spec=pltpu.PrefetchScalarGridSpec(num_scalar_...  8.4 us
    ppermute x3, starting transfers between devices, per_device(): shifted.append(lax.ppermute(own, 'aux', pairs))  4.62 us
    ppermute x1, starting transfers between devices, halo_pieces(): lax.ppermute(lax.slice_in_dim(block, block.shape[0] - width, None, axis=0...  4.58 us
  transfers between devices with their start and end apart: 6, of which 6 were waited for; matrix products, arithmetic and copies ran while one was open for 3% of the time, Pallas kernels for 0%

profile of v12, /device:TPU:1, one launch (start us, length us, event | category | flops | bytes accessed | tf_op | source)
XLA Modules:
  0.0 172.6 jit_solution(15153175001688737996)
XLA Ops:
  6.5 0.0 all-gather.3.cloned.1.call-start
  6.5 4.6 %collective-permute-start = (bf16[1024,256]{1,0:T(8,128)(2,1)}, bf16[1024,256]{1,0:T(8,128)(2,1)S(1)}, u32[]{:S(2)}, u32[]{:S(2)}) collective-permute-start(bf16[1024,256]{1,0:T(8,128)(2,1)} %refs_5_.1), channel_id=1, source_target_pairs={{0,1},{1,2},{2,3},{3,4},{4,5},{5,6},{6,7},{7,8},{8,9},{9,10},{10,1... | collective-permute-start | bytes 1572872 | tf_op jit(solution)/shard_map/ppermute | solution.py:13
  11.1 1.9 %collective-permute-start.1 = (bf16[1024,256]{1,0:T(8,128)(2,1)}, bf16[1024,256]{1,0:T(8,128)(2,1)S(1)}, u32[]{:S(2)}, u32[]{:S(2)}) collective-permute-start(bf16[1024,256]{1,0:T(8,128)(2,1)} %refs_5_.1), channel_id=1, source_target_pairs={{1,0},{2,1},{3,2},{4,3},{5,4},{6,5},{7,6},{8,7},{9,8},{10,9},{11,1... | collective-permute-start | bytes 1572872 | tf_op jit(solution)/shard_map/ppermute | solution.py:14
  13.1 1.3 subtract_clamp_fusion.index_ref
  14.4 3.2 %collective-permute-done.refs_4_ = bf16[1024,256]{1,0:T(8,128)(2,1)S(1)} collective-permute-done((bf16[1024,256]{1,0:T(8,128)(2,1)}, bf16[1024,256]{1,0:T(8,128)(2,1)S(1)}, u32[]{:S(2)}, u32[]{:S(2)}) %collective-permute-start) | collective-permute-done | bytes 524320 | tf_op jit(solution)/shard_map/ppermute | solution.py:13
  17.6 0.0 copy-start
  17.6 4.3 %collective-permute-done.1.refs_6_ = bf16[1024,256]{1,0:T(8,128)(2,1)S(1)} collective-permute-done((bf16[1024,256]{1,0:T(8,128)(2,1)}, bf16[1024,256]{1,0:T(8,128)(2,1)S(1)}, u32[]{:S(2)}, u32[]{:S(2)}) %collective-permute-start.1) | collective-permute-done | bytes 524320 | tf_op jit(solution)/shard_map/ppermute | solution.py:14
  21.8 0.0 copy-start.1
  21.8 0.0 copy-done
  21.8 0.8 copy-done.1
  22.6 8.4 %shard_map.46 = bf16[1024,256]{1,0:T(8,128)(2,1)} custom-call(s32[8,16]{1,0:T(8,128)} %subtract_clamp_fusion.index_ref, s32[8,16]{1,0:T(8,128)} %mask_ref.1, bf16[1024,2048]{1,0:T(8,128)(2,1)} %bitcast.22, bf16[1024,2048]{1,0:T(8,128)(2,1)} %bitcast.23, bf16[1024,2048]{1,0:T(8,128)(2,1)} %bitcast.24, bf16[1024,2048]{1,0:T(8,128)(2,1)} %bitcast.25, ...), custom_call_target="tpu_custom_call" | custom-call | tf_op jit(solution)/shard_map/pallas_call | solution.py:60
  31.0 11.1 %all_to_all.5 = bf16[4,256,256]{2,1,0:T(8,128)(2,1)} all-to-all(bf16[4,256,256]{2,1,0:T(8,128)(2,1)} %bitcast.26), channel_id=1, replica_groups=mesh['aux'=4,'rzy'=16,'core'=2] {'aux'}, dimensions={0} | all-to-all | bytes 1048576 | tf_op jit(solution)/shard_map/all_to_all | solution.py:91
  42.2 0.0 all-gather.3.cloned.1.call-update
  42.2 1.8 %collective-permute-start.4 = (bf16[1024,256]{1,0:T(8,128)(2,1)}, bf16[1024,256]{1,0:T(8,128)(2,1)S(1)}, u32[]{:S(2)}, u32[]{:S(2)}) collective-permute-start(bf16[1024,256]{1,0:T(8,128)(2,1)} %shard_map.46), channel_id=1, source_target_pairs={{0,96},{32,0},{64,32},{96,64},{1,97},{33,1},{65,33},{97,65},{2,98}... | collective-permute-start | bytes 1572872 | tf_op jit(solution)/shard_map/ppermute | solution.py:90
  44.0 2.8 %collective-permute-start.3 = (bf16[1024,256]{1,0:T(8,128)(2,1)}, bf16[1024,256]{1,0:T(8,128)(2,1)S(1)}, u32[]{:S(2)}, u32[]{:S(2)}) collective-permute-start(bf16[1024,256]{1,0:T(8,128)(2,1)} %shard_map.46), channel_id=1, source_target_pairs={{0,64},{32,96},{64,0},{96,32},{1,65},{33,97},{65,1},{97,33},{2,66}... | collective-permute-start | bytes 1572872 | tf_op jit(solution)/shard_map/ppermute | solution.py:90
  46.8 0.0 collective-permute-start.2
  46.9 10.8 %collective-permute-done.4 = bf16[1024,256]{1,0:T(8,128)(2,1)S(1)} collective-permute-done((bf16[1024,256]{1,0:T(8,128)(2,1)}, bf16[1024,256]{1,0:T(8,128)(2,1)S(1)}, u32[]{:S(2)}, u32[]{:S(2)}) %collective-permute-start.4) | collective-permute-done | bytes 524320 | tf_op jit(solution)/shard_map/ppermute | solution.py:90
  57.7 1.7 %collective-permute-done.3 = bf16[1024,256]{1,0:T(8,128)(2,1)S(1)} collective-permute-done((bf16[1024,256]{1,0:T(8,128)(2,1)}, bf16[1024,256]{1,0:T(8,128)(2,1)S(1)}, u32[]{:S(2)}, u32[]{:S(2)}) %collective-permute-start.3) | collective-permute-done | bytes 524320 | tf_op jit(solution)/shard_map/ppermute | solution.py:90
  59.4 5.9 %collective-permute-done.2 = bf16[1024,256]{1,0:T(8,128)(2,1)S(1)} collective-permute-done((bf16[1024,256]{1,0:T(8,128)(2,1)}, bf16[1024,256]{1,0:T(8,128)(2,1)S(1)}, u32[]{:S(2)}, u32[]{:S(2)}) %collective-permute-start.2) | collective-permute-done | bytes 524320 | tf_op jit(solution)/shard_map/ppermute | solution.py:90
  65.3 0.0 copy-start.2
  65.3 0.8 copy-done.2
  66.1 1.5 pad_maximum_fusion
  67.5 2.0 %gather_fusion = bf16[4,1024,256]{2,1,0:T(8,128)(2,1)} fusion(bf16[4,1024,256]{2,1,0:T(8,128)(2,1)S(1)} %pad_maximum_fusion, s32[1024]{0:T(1024)S(1)} %pad_clamp_fusion), kind=kCustom, calls=%fused_computation | custom fusion | bytes 4194320 | tf_op jit(solution)/shard_map/jit(_take)/gather | solution.py:95
  69.5 51.0 %all-gather.3.cloned.1.call-done = bf16[128,256,256]{2,1,0:T(8,128)(2,1)} async-done(((bf16[4,256,256]{2,1,0:T(8,128)(2,1)}), bf16[128,256,256]{2,1,0:T(8,128)(2,1)}) %all-gather.3.cloned.1.call-update) | async-done | bytes 16777232 | tf_op jit(solution)/shard_map/all_gather | solution.py:96
  120.6 26.5 %fusion.in_ref = bf16[32,1024,256]{2,1,0:T(8,128)(2,1)} fusion(bf16[32,4,256,256]{3,2,1,0:T(8,128)(2,1)} %bitcast.31, bf16[4,1024,256]{2,1,0:T(8,128)(2,1)} %gather_fusion, pred[4]{0:T(512)(128)(4,1)S(1)} %compare_and_fusion), kind=kOutput, calls=%fused_computation.2 | convolution fusion | flops 17189306368 | bytes 35651588 | tf_op jit(solution)/shard_map/pmi,rpki->rmk/dot_general | solution.py:97
  147.1 18.7 %shard_map.47 = bf16[1024,32,256]{2,1,0:T(8,128)(2,1)} custom-call(bf16[32,1024,256]{2,1,0:T(8,128)(2,1)} %fusion.in_ref), custom_call_target="tpu_custom_call" | custom-call | tf_op jit(solution)/shard_map/pallas_call | solution.py:105
  (3 shorter events, 0.0 us)
Async XLA Ops:
  6.5 114.0 %all-gather.3.cloned.1.call-start = ((), (), s32[]{:S(2)}) async-start(), calls=%async_computation.1 | async-start | bytes 17301504 | tf_op jit(solution)/shard_map/all_gather | solution.py:96
  6.5 11.0 %collective-permute-start = (bf16[1024,256]{1,0:T(8,128)(2,1)}, bf16[1024,256]{1,0:T(8,128)(2,1)S(1)}, u32[]{:S(2)}, u32[]{:S(2)}) collective-permute-start(bf16[1024,256]{1,0:T(8,128)(2,1)} %refs_5_.1), channel_id=1, source_target_pairs={{0,1},{1,2},{2,3},{3,4},{4,5},{5,6},{6,7},{7,8},{8,9},{9,10},{10,1... | collective-permute-start | bytes 1572872 | tf_op jit(solution)/shard_map/ppermute | solution.py:13
  11.1 10.7 %collective-permute-start.1 = (bf16[1024,256]{1,0:T(8,128)(2,1)}, bf16[1024,256]{1,0:T(8,128)(2,1)S(1)}, u32[]{:S(2)}, u32[]{:S(2)}) collective-permute-start(bf16[1024,256]{1,0:T(8,128)(2,1)} %refs_5_.1), channel_id=1, source_target_pairs={{1,0},{2,1},{3,2},{4,3},{5,4},{6,5},{7,6},{8,7},{9,8},{10,9},{11,1... | collective-permute-start | bytes 1572872 | tf_op jit(solution)/shard_map/ppermute | solution.py:14
  17.6 4.3 %copy-start = (bf16[1024,256]{1,0:T(8,128)(2,1)}, bf16[1024,256]{1,0:T(8,128)(2,1)S(1)}, u32[]{:S(2)}) copy-start(bf16[1024,256]{1,0:T(8,128)(2,1)S(1)} %collective-permute-done.refs_4_) | copy-start | bytes 1572868
  21.8 0.8 copy-start.1
  42.2 15.5 %collective-permute-start.4 = (bf16[1024,256]{1,0:T(8,128)(2,1)}, bf16[1024,256]{1,0:T(8,128)(2,1)S(1)}, u32[]{:S(2)}, u32[]{:S(2)}) collective-permute-start(bf16[1024,256]{1,0:T(8,128)(2,1)} %shard_map.46), channel_id=1, source_target_pairs={{0,96},{32,0},{64,32},{96,64},{1,97},{33,1},{65,33},{97,65},{2,98}... | collective-permute-start | bytes 1572872 | tf_op jit(solution)/shard_map/ppermute | solution.py:90
  44.0 15.4 %collective-permute-start.3 = (bf16[1024,256]{1,0:T(8,128)(2,1)}, bf16[1024,256]{1,0:T(8,128)(2,1)S(1)}, u32[]{:S(2)}, u32[]{:S(2)}) collective-permute-start(bf16[1024,256]{1,0:T(8,128)(2,1)} %shard_map.46), channel_id=1, source_target_pairs={{0,64},{32,96},{64,0},{96,32},{1,65},{33,97},{65,1},{97,33},{2,66}... | collective-permute-start | bytes 1572872 | tf_op jit(solution)/shard_map/ppermute | solution.py:90
  46.8 18.5 %collective-permute-start.2 = (bf16[1024,256]{1,0:T(8,128)(2,1)}, bf16[1024,256]{1,0:T(8,128)(2,1)S(1)}, u32[]{:S(2)}, u32[]{:S(2)}) collective-permute-start(bf16[1024,256]{1,0:T(8,128)(2,1)} %shard_map.46), channel_id=1, source_target_pairs={{0,32},{32,64},{64,96},{96,0},{1,33},{33,65},{65,97},{97,1},{2,34}... | collective-permute-start | bytes 1572872 | tf_op jit(solution)/shard_map/ppermute | solution.py:90
  65.3 0.8 copy-start.2
Sparse Core Ops, SparseCore 0:
  42.3 78.2 all-gather.2

commit v13 on v12

--- a/solution.py
+++ b/solution.py
@@ -97,7 +97,7 @@
     result = jnp.einsum("pmi,rpki->rmk", slab_rows, partner, preferred_element_type=jnp.float32)
     result = result.astype(jnp.bfloat16)
     row_count = partner.shape[0]
-    rows_tile = 64
+    rows_tile = 128
 
     def relayout(in_ref, out_ref):
         out_ref[...] = pltpu.einshape("rmk->mrk", in_ref[...])

time: 173 us -> 169 us (0.977)
  Pallas kernels: 27.1 us -> 23.5 us
    pallas_call x1, Pallas kernels: 18.7 us -> 15.1 us  [per_device(): pl.pallas_call(relayout, grid=(rows_local // rows_tile,), in_specs=[pl.Bl...]
where the time goes in v13:
time: 169 us
  waiting for transfers between devices  77 us (46%)
  matrix products  26.5 us (16%)
  Pallas kernels  23.5 us (14%)
  between operations  13.4 us (8%)
  starting transfers between devices  11.1 us (7%)
  blocking collectives  11.1 us (7%)
  local copies, waits for them, and re-layouts  3.59 us (2%)
  other arithmetic  2.78 us (2%)
    all_gather x1, waiting for transfers between devices, per_device(): partner = lax.all_gather(piece, ROW, axis=0)  51 us
    dot_general x1, matrix products, per_device(): jnp.einsum('pmi,rpki->rmk', slab_rows, partner, preferred_element_type=jn...  26.5 us
    ppermute x3, waiting for transfers between devices, per_device(): shifted.append(lax.ppermute(own, 'aux', pairs))  18.4 us
    pallas_call x1, Pallas kernels, per_device(): pl.pallas_call(relayout, grid=(rows_local // rows_tile,), in_specs=[pl.Bl...  15.1 us
    all_to_all x1, blocking collectives, per_device(): lax.all_to_all(own.reshape(aux_count, share, orbitals), 'aux', 0, 0, tile...  11.1 us
    pallas_call x1, Pallas kernels, per_device(): pl.pallas_call(kernel, grid_spec=pltpu.PrefetchScalarGridSpec(num_scalar_...  8.4 us
    ppermute x3, starting transfers between devices, per_device(): shifted.append(lax.ppermute(own, 'aux', pairs))  4.62 us
    ppermute x1, starting transfers between devices, halo_pieces(): lax.ppermute(lax.slice_in_dim(block, block.shape[0] - width, None, axis=0...  4.58 us
  transfers between devices with their start and end apart: 6, of which 6 were waited for; matrix products, arithmetic and copies ran while one was open for 3% of the time, Pallas kernels for 0%

profile of v13, /device:TPU:1, one launch (start us, length us, event | category | flops | bytes accessed | tf_op | source)
XLA Modules:
  0.0 169.0 jit_solution(11914117344569926607)
XLA Ops:
  6.5 0.0 all-gather.3.cloned.1.call-start
  6.5 4.6 %collective-permute-start = (bf16[1024,256]{1,0:T(8,128)(2,1)}, bf16[1024,256]{1,0:T(8,128)(2,1)S(1)}, u32[]{:S(2)}, u32[]{:S(2)}) collective-permute-start(bf16[1024,256]{1,0:T(8,128)(2,1)} %refs_5_.1), channel_id=1, source_target_pairs={{0,1},{1,2},{2,3},{3,4},{4,5},{5,6},{6,7},{7,8},{8,9},{9,10},{10,1... | collective-permute-start | bytes 1572872 | tf_op jit(solution)/shard_map/ppermute | solution.py:13
  11.1 1.9 %collective-permute-start.1 = (bf16[1024,256]{1,0:T(8,128)(2,1)}, bf16[1024,256]{1,0:T(8,128)(2,1)S(1)}, u32[]{:S(2)}, u32[]{:S(2)}) collective-permute-start(bf16[1024,256]{1,0:T(8,128)(2,1)} %refs_5_.1), channel_id=1, source_target_pairs={{1,0},{2,1},{3,2},{4,3},{5,4},{6,5},{7,6},{8,7},{9,8},{10,9},{11,1... | collective-permute-start | bytes 1572872 | tf_op jit(solution)/shard_map/ppermute | solution.py:14
  13.1 1.3 subtract_clamp_fusion.index_ref
  14.4 3.2 %collective-permute-done.refs_4_ = bf16[1024,256]{1,0:T(8,128)(2,1)S(1)} collective-permute-done((bf16[1024,256]{1,0:T(8,128)(2,1)}, bf16[1024,256]{1,0:T(8,128)(2,1)S(1)}, u32[]{:S(2)}, u32[]{:S(2)}) %collective-permute-start) | collective-permute-done | bytes 524320 | tf_op jit(solution)/shard_map/ppermute | solution.py:13
  17.6 0.0 copy-start
  17.6 4.3 %collective-permute-done.1.refs_6_ = bf16[1024,256]{1,0:T(8,128)(2,1)S(1)} collective-permute-done((bf16[1024,256]{1,0:T(8,128)(2,1)}, bf16[1024,256]{1,0:T(8,128)(2,1)S(1)}, u32[]{:S(2)}, u32[]{:S(2)}) %collective-permute-start.1) | collective-permute-done | bytes 524320 | tf_op jit(solution)/shard_map/ppermute | solution.py:14
  21.8 0.0 copy-start.1
  21.8 0.0 copy-done
  21.8 0.8 copy-done.1
  22.6 8.4 %shard_map.46 = bf16[1024,256]{1,0:T(8,128)(2,1)} custom-call(s32[8,16]{1,0:T(8,128)} %subtract_clamp_fusion.index_ref, s32[8,16]{1,0:T(8,128)} %mask_ref.1, bf16[1024,2048]{1,0:T(8,128)(2,1)} %bitcast.22, bf16[1024,2048]{1,0:T(8,128)(2,1)} %bitcast.23, bf16[1024,2048]{1,0:T(8,128)(2,1)} %bitcast.24, bf16[1024,2048]{1,0:T(8,128)(2,1)} %bitcast.25, ...), custom_call_target="tpu_custom_call" | custom-call | tf_op jit(solution)/shard_map/pallas_call | solution.py:60
  31.0 11.1 %all_to_all.5 = bf16[4,256,256]{2,1,0:T(8,128)(2,1)} all-to-all(bf16[4,256,256]{2,1,0:T(8,128)(2,1)} %bitcast.26), channel_id=1, replica_groups=mesh['aux'=4,'rzy'=16,'core'=2] {'aux'}, dimensions={0} | all-to-all | bytes 1048576 | tf_op jit(solution)/shard_map/all_to_all | solution.py:91
  42.2 0.0 all-gather.3.cloned.1.call-update
  42.2 1.8 %collective-permute-start.4 = (bf16[1024,256]{1,0:T(8,128)(2,1)}, bf16[1024,256]{1,0:T(8,128)(2,1)S(1)}, u32[]{:S(2)}, u32[]{:S(2)}) collective-permute-start(bf16[1024,256]{1,0:T(8,128)(2,1)} %shard_map.46), channel_id=1, source_target_pairs={{0,96},{32,0},{64,32},{96,64},{1,97},{33,1},{65,33},{97,65},{2,98}... | collective-permute-start | bytes 1572872 | tf_op jit(solution)/shard_map/ppermute | solution.py:90
  44.0 2.8 %collective-permute-start.3 = (bf16[1024,256]{1,0:T(8,128)(2,1)}, bf16[1024,256]{1,0:T(8,128)(2,1)S(1)}, u32[]{:S(2)}, u32[]{:S(2)}) collective-permute-start(bf16[1024,256]{1,0:T(8,128)(2,1)} %shard_map.46), channel_id=1, source_target_pairs={{0,64},{32,96},{64,0},{96,32},{1,65},{33,97},{65,1},{97,33},{2,66}... | collective-permute-start | bytes 1572872 | tf_op jit(solution)/shard_map/ppermute | solution.py:90
  46.8 0.0 collective-permute-start.2
  46.9 10.8 %collective-permute-done.4 = bf16[1024,256]{1,0:T(8,128)(2,1)S(1)} collective-permute-done((bf16[1024,256]{1,0:T(8,128)(2,1)}, bf16[1024,256]{1,0:T(8,128)(2,1)S(1)}, u32[]{:S(2)}, u32[]{:S(2)}) %collective-permute-start.4) | collective-permute-done | bytes 524320 | tf_op jit(solution)/shard_map/ppermute | solution.py:90
  57.7 1.7 %collective-permute-done.3 = bf16[1024,256]{1,0:T(8,128)(2,1)S(1)} collective-permute-done((bf16[1024,256]{1,0:T(8,128)(2,1)}, bf16[1024,256]{1,0:T(8,128)(2,1)S(1)}, u32[]{:S(2)}, u32[]{:S(2)}) %collective-permute-start.3) | collective-permute-done | bytes 524320 | tf_op jit(solution)/shard_map/ppermute | solution.py:90
  59.4 5.9 %collective-permute-done.2 = bf16[1024,256]{1,0:T(8,128)(2,1)S(1)} collective-permute-done((bf16[1024,256]{1,0:T(8,128)(2,1)}, bf16[1024,256]{1,0:T(8,128)(2,1)S(1)}, u32[]{:S(2)}, u32[]{:S(2)}) %collective-permute-start.2) | collective-permute-done | bytes 524320 | tf_op jit(solution)/shard_map/ppermute | solution.py:90
  65.3 0.0 copy-start.2
  65.3 0.8 copy-done.2
  66.1 1.5 pad_maximum_fusion
  67.5 2.0 %gather_fusion = bf16[4,1024,256]{2,1,0:T(8,128)(2,1)} fusion(bf16[4,1024,256]{2,1,0:T(8,128)(2,1)S(1)} %pad_maximum_fusion, s32[1024]{0:T(1024)S(1)} %pad_clamp_fusion), kind=kCustom, calls=%fused_computation | custom fusion | bytes 4194320 | tf_op jit(solution)/shard_map/jit(_take)/gather | solution.py:95
  69.5 51.0 %all-gather.3.cloned.1.call-done = bf16[128,256,256]{2,1,0:T(8,128)(2,1)} async-done(((bf16[4,256,256]{2,1,0:T(8,128)(2,1)}), bf16[128,256,256]{2,1,0:T(8,128)(2,1)}) %all-gather.3.cloned.1.call-update) | async-done | bytes 16777232 | tf_op jit(solution)/shard_map/all_gather | solution.py:96
  120.6 26.5 %fusion.in_ref = bf16[32,1024,256]{2,1,0:T(8,128)(2,1)} fusion(bf16[32,4,256,256]{3,2,1,0:T(8,128)(2,1)} %bitcast.31, bf16[4,1024,256]{2,1,0:T(8,128)(2,1)} %gather_fusion, pred[4]{0:T(512)(128)(4,1)S(1)} %compare_and_fusion), kind=kOutput, calls=%fused_computation.2 | convolution fusion | flops 17189306368 | bytes 35651588 | tf_op jit(solution)/shard_map/pmi,rpki->rmk/dot_general | solution.py:97
  147.1 15.1 %shard_map.47 = bf16[1024,32,256]{2,1,0:T(8,128)(2,1)} custom-call(bf16[32,1024,256]{2,1,0:T(8,128)(2,1)} %fusion.in_ref), custom_call_target="tpu_custom_call" | custom-call | tf_op jit(solution)/shard_map/pallas_call | solution.py:105
  (3 shorter events, 0.0 us)
Async XLA Ops:
  6.5 114.0 %all-gather.3.cloned.1.call-start = ((), (), s32[]{:S(2)}) async-start(), calls=%async_computation.1 | async-start | bytes 17301504 | tf_op jit(solution)/shard_map/all_gather | solution.py:96
  6.5 11.0 %collective-permute-start = (bf16[1024,256]{1,0:T(8,128)(2,1)}, bf16[1024,256]{1,0:T(8,128)(2,1)S(1)}, u32[]{:S(2)}, u32[]{:S(2)}) collective-permute-start(bf16[1024,256]{1,0:T(8,128)(2,1)} %refs_5_.1), channel_id=1, source_target_pairs={{0,1},{1,2},{2,3},{3,4},{4,5},{5,6},{6,7},{7,8},{8,9},{9,10},{10,1... | collective-permute-start | bytes 1572872 | tf_op jit(solution)/shard_map/ppermute | solution.py:13
  11.1 10.7 %collective-permute-start.1 = (bf16[1024,256]{1,0:T(8,128)(2,1)}, bf16[1024,256]{1,0:T(8,128)(2,1)S(1)}, u32[]{:S(2)}, u32[]{:S(2)}) collective-permute-start(bf16[1024,256]{1,0:T(8,128)(2,1)} %refs_5_.1), channel_id=1, source_target_pairs={{1,0},{2,1},{3,2},{4,3},{5,4},{6,5},{7,6},{8,7},{9,8},{10,9},{11,1... | collective-permute-start | bytes 1572872 | tf_op jit(solution)/shard_map/ppermute | solution.py:14
  17.6 4.3 %copy-start = (bf16[1024,256]{1,0:T(8,128)(2,1)}, bf16[1024,256]{1,0:T(8,128)(2,1)S(1)}, u32[]{:S(2)}) copy-start(bf16[1024,256]{1,0:T(8,128)(2,1)S(1)} %collective-permute-done.refs_4_) | copy-start | bytes 1572868
  21.8 0.8 copy-start.1
  42.2 15.5 %collective-permute-start.4 = (bf16[1024,256]{1,0:T(8,128)(2,1)}, bf16[1024,256]{1,0:T(8,128)(2,1)S(1)}, u32[]{:S(2)}, u32[]{:S(2)}) collective-permute-start(bf16[1024,256]{1,0:T(8,128)(2,1)} %shard_map.46), channel_id=1, source_target_pairs={{0,96},{32,0},{64,32},{96,64},{1,97},{33,1},{65,33},{97,65},{2,98}... | collective-permute-start | bytes 1572872 | tf_op jit(solution)/shard_map/ppermute | solution.py:90
  44.0 15.4 %collective-permute-start.3 = (bf16[1024,256]{1,0:T(8,128)(2,1)}, bf16[1024,256]{1,0:T(8,128)(2,1)S(1)}, u32[]{:S(2)}, u32[]{:S(2)}) collective-permute-start(bf16[1024,256]{1,0:T(8,128)(2,1)} %shard_map.46), channel_id=1, source_target_pairs={{0,64},{32,96},{64,0},{96,32},{1,65},{33,97},{65,1},{97,33},{2,66}... | collective-permute-start | bytes 1572872 | tf_op jit(solution)/shard_map/ppermute | solution.py:90
  46.8 18.5 %collective-permute-start.2 = (bf16[1024,256]{1,0:T(8,128)(2,1)}, bf16[1024,256]{1,0:T(8,128)(2,1)S(1)}, u32[]{:S(2)}, u32[]{:S(2)}) collective-permute-start(bf16[1024,256]{1,0:T(8,128)(2,1)} %shard_map.46), channel_id=1, source_target_pairs={{0,32},{32,64},{64,96},{96,0},{1,33},{33,65},{65,97},{97,1},{2,34}... | collective-permute-start | bytes 1572872 | tf_op jit(solution)/shard_map/ppermute | solution.py:90
  65.3 0.8 copy-start.2
Sparse Core Ops, SparseCore 0:
  42.3 78.2 all-gather.2

commit v14 on v13

--- a/solution.py
+++ b/solution.py
@@ -94,10 +94,10 @@
     order = (aux_index - jnp.arange(aux_count)) % aux_count
     slab_rows = jnp.take(jnp.stack(shifted), order, axis=0)
     partner = lax.all_gather(piece, ROW, axis=0)
-    result = jnp.einsum("pmi,rpki->rmk", slab_rows, partner, preferred_element_type=jnp.float32)
-    result = result.astype(jnp.bfloat16)
+    result = jnp.einsum("pmi,rpki->mrk", slab_rows, partner, preferred_element_type=jnp.float32)
+    result = jnp.transpose(result.astype(jnp.bfloat16), (1, 0, 2))
     row_count = partner.shape[0]
-    rows_tile = 128
+    rows_tile = 256
 
     def relayout(in_ref, out_ref):
         out_ref[...] = pltpu.einshape("rmk->mrk", in_ref[...])

time: 169 us -> 165 us (0.976)
  Pallas kernels: 23.5 us -> 21.1 us
  matrix products: 26.5 us -> 24.2 us
    dot_general x1, matrix products: 26.5 us -> 24.2 us  [per_device(): jnp.einsum('pmi,rpki->mrk', slab_rows, partner, preferred_element_type=jn...]
    pallas_call x1, Pallas kernels: 15.1 us -> 12.7 us  [per_device(): pl.pallas_call(relayout, grid=(rows_local // rows_tile,), in_specs=[pl.Bl...]
where the time goes in v14:
time: 165 us; the launch traced here: 164 us
  waiting for transfers between devices  77 us (47%)
  matrix products  24.2 us (15%)
  Pallas kernels  21.1 us (13%)
  between operations  13.4 us (8%)
  starting transfers between devices  11.1 us (7%)
  blocking collectives  11.1 us (7%)
  local copies, waits for them, and re-layouts  3.59 us (2%)
  other arithmetic  2.78 us (2%)
    all_gather x1, waiting for transfers between devices, per_device(): partner = lax.all_gather(piece, ROW, axis=0)  51 us
    dot_general x1, matrix products, per_device(): jnp.einsum('pmi,rpki->mrk', slab_rows, partner, preferred_element_type=jn...  24.2 us
    ppermute x3, waiting for transfers between devices, per_device(): shifted.append(lax.ppermute(own, 'aux', pairs))  18.4 us
    pallas_call x1, Pallas kernels, per_device(): pl.pallas_call(relayout, grid=(rows_local // rows_tile,), in_specs=[pl.Bl...  12.7 us
    all_to_all x1, blocking collectives, per_device(): lax.all_to_all(own.reshape(aux_count, share, orbitals), 'aux', 0, 0, tile...  11.1 us
    pallas_call x1, Pallas kernels, per_device(): pl.pallas_call(kernel, grid_spec=pltpu.PrefetchScalarGridSpec(num_scalar_...  8.4 us
    ppermute x3, starting transfers between devices, per_device(): shifted.append(lax.ppermute(own, 'aux', pairs))  4.62 us
    ppermute x1, starting transfers between devices, halo_pieces(): lax.ppermute(lax.slice_in_dim(block, block.shape[0] - width, None, axis=0...  4.58 us
  transfers between devices with their start and end apart: 6, of which 6 were waited for; matrix products, arithmetic and copies ran while one was open for 3% of the time, Pallas kernels for 0%

profile of v14, /device:TPU:1, one launch (start us, length us, event | category | flops | bytes accessed | tf_op | source)
XLA Modules:
  0.0 164.3 jit_solution(3783747809785028512)
XLA Ops:
  6.5 0.0 all-gather.3.cloned.1.call-start
  6.5 4.6 %collective-permute-start = (bf16[1024,256]{1,0:T(8,128)(2,1)}, bf16[1024,256]{1,0:T(8,128)(2,1)S(1)}, u32[]{:S(2)}, u32[]{:S(2)}) collective-permute-start(bf16[1024,256]{1,0:T(8,128)(2,1)} %refs_5_.1), channel_id=1, source_target_pairs={{0,1},{1,2},{2,3},{3,4},{4,5},{5,6},{6,7},{7,8},{8,9},{9,10},{10,1... | collective-permute-start | bytes 1572872 | tf_op jit(solution)/shard_map/ppermute | solution.py:13
  11.1 1.9 %collective-permute-start.1 = (bf16[1024,256]{1,0:T(8,128)(2,1)}, bf16[1024,256]{1,0:T(8,128)(2,1)S(1)}, u32[]{:S(2)}, u32[]{:S(2)}) collective-permute-start(bf16[1024,256]{1,0:T(8,128)(2,1)} %refs_5_.1), channel_id=1, source_target_pairs={{1,0},{2,1},{3,2},{4,3},{5,4},{6,5},{7,6},{8,7},{9,8},{10,9},{11,1... | collective-permute-start | bytes 1572872 | tf_op jit(solution)/shard_map/ppermute | solution.py:14
  13.1 1.3 subtract_clamp_fusion.index_ref
  14.4 3.2 %collective-permute-done.refs_4_ = bf16[1024,256]{1,0:T(8,128)(2,1)S(1)} collective-permute-done((bf16[1024,256]{1,0:T(8,128)(2,1)}, bf16[1024,256]{1,0:T(8,128)(2,1)S(1)}, u32[]{:S(2)}, u32[]{:S(2)}) %collective-permute-start) | collective-permute-done | bytes 524320 | tf_op jit(solution)/shard_map/ppermute | solution.py:13
  17.6 0.0 copy-start
  17.6 4.3 %collective-permute-done.1.refs_6_ = bf16[1024,256]{1,0:T(8,128)(2,1)S(1)} collective-permute-done((bf16[1024,256]{1,0:T(8,128)(2,1)}, bf16[1024,256]{1,0:T(8,128)(2,1)S(1)}, u32[]{:S(2)}, u32[]{:S(2)}) %collective-permute-start.1) | collective-permute-done | bytes 524320 | tf_op jit(solution)/shard_map/ppermute | solution.py:14
  21.8 0.0 copy-start.1
  21.8 0.0 copy-done
  21.8 0.8 copy-done.1
  22.6 8.4 %shard_map.46 = bf16[1024,256]{1,0:T(8,128)(2,1)} custom-call(s32[8,16]{1,0:T(8,128)} %subtract_clamp_fusion.index_ref, s32[8,16]{1,0:T(8,128)} %mask_ref.1, bf16[1024,2048]{1,0:T(8,128)(2,1)} %bitcast.23, bf16[1024,2048]{1,0:T(8,128)(2,1)} %bitcast.24, bf16[1024,2048]{1,0:T(8,128)(2,1)} %bitcast.25, bf16[1024,2048]{1,0:T(8,128)(2,1)} %bitcast.26, ...), custom_call_target="tpu_custom_call" | custom-call | tf_op jit(solution)/shard_map/pallas_call | solution.py:60
  31.0 11.1 %all_to_all.5 = bf16[4,256,256]{2,1,0:T(8,128)(2,1)} all-to-all(bf16[4,256,256]{2,1,0:T(8,128)(2,1)} %bitcast.27), channel_id=1, replica_groups=mesh['aux'=4,'rzy'=16,'core'=2] {'aux'}, dimensions={0} | all-to-all | bytes 1048576 | tf_op jit(solution)/shard_map/all_to_all | solution.py:91
  42.2 0.0 all-gather.3.cloned.1.call-update
  42.2 1.8 %collective-permute-start.4 = (bf16[1024,256]{1,0:T(8,128)(2,1)}, bf16[1024,256]{1,0:T(8,128)(2,1)S(1)}, u32[]{:S(2)}, u32[]{:S(2)}) collective-permute-start(bf16[1024,256]{1,0:T(8,128)(2,1)} %shard_map.46), channel_id=1, source_target_pairs={{0,96},{32,0},{64,32},{96,64},{1,97},{33,1},{65,33},{97,65},{2,98}... | collective-permute-start | bytes 1572872 | tf_op jit(solution)/shard_map/ppermute | solution.py:90
  44.0 2.8 %collective-permute-start.3 = (bf16[1024,256]{1,0:T(8,128)(2,1)}, bf16[1024,256]{1,0:T(8,128)(2,1)S(1)}, u32[]{:S(2)}, u32[]{:S(2)}) collective-permute-start(bf16[1024,256]{1,0:T(8,128)(2,1)} %shard_map.46), channel_id=1, source_target_pairs={{0,64},{32,96},{64,0},{96,32},{1,65},{33,97},{65,1},{97,33},{2,66}... | collective-permute-start | bytes 1572872 | tf_op jit(solution)/shard_map/ppermute | solution.py:90
  46.8 0.0 collective-permute-start.2
  46.9 10.8 %collective-permute-done.4 = bf16[1024,256]{1,0:T(8,128)(2,1)S(1)} collective-permute-done((bf16[1024,256]{1,0:T(8,128)(2,1)}, bf16[1024,256]{1,0:T(8,128)(2,1)S(1)}, u32[]{:S(2)}, u32[]{:S(2)}) %collective-permute-start.4) | collective-permute-done | bytes 524320 | tf_op jit(solution)/shard_map/ppermute | solution.py:90
  57.7 1.7 %collective-permute-done.3 = bf16[1024,256]{1,0:T(8,128)(2,1)S(1)} collective-permute-done((bf16[1024,256]{1,0:T(8,128)(2,1)}, bf16[1024,256]{1,0:T(8,128)(2,1)S(1)}, u32[]{:S(2)}, u32[]{:S(2)}) %collective-permute-start.3) | collective-permute-done | bytes 524320 | tf_op jit(solution)/shard_map/ppermute | solution.py:90
  59.4 5.9 %collective-permute-done.2 = bf16[1024,256]{1,0:T(8,128)(2,1)S(1)} collective-permute-done((bf16[1024,256]{1,0:T(8,128)(2,1)}, bf16[1024,256]{1,0:T(8,128)(2,1)S(1)}, u32[]{:S(2)}, u32[]{:S(2)}) %collective-permute-start.2) | collective-permute-done | bytes 524320 | tf_op jit(solution)/shard_map/ppermute | solution.py:90
  65.3 0.0 copy-start.2
  65.3 0.8 copy-done.2
  66.1 1.5 pad_maximum_fusion
  67.5 2.0 %gather_fusion = bf16[4,1024,256]{2,1,0:T(8,128)(2,1)} fusion(bf16[4,1024,256]{2,1,0:T(8,128)(2,1)S(1)} %pad_maximum_fusion, s32[1024]{0:T(1024)S(1)} %pad_clamp_fusion), kind=kCustom, calls=%fused_computation | custom fusion | bytes 4194320 | tf_op jit(solution)/shard_map/jit(_take)/gather | solution.py:95
  69.5 51.0 %all-gather.3.cloned.1.call-done = bf16[128,256,256]{2,1,0:T(8,128)(2,1)} async-done(((bf16[4,256,256]{2,1,0:T(8,128)(2,1)}), bf16[128,256,256]{2,1,0:T(8,128)(2,1)}) %all-gather.3.cloned.1.call-update) | async-done | bytes 16777232 | tf_op jit(solution)/shard_map/all_gather | solution.py:96
  120.6 24.2 %fusion.in_ref = bf16[32,1024,256]{2,1,0:T(8,128)(2,1)} fusion(bf16[32,4,256,256]{3,2,1,0:T(8,128)(2,1)} %bitcast.32, bf16[4,1024,256]{2,1,0:T(8,128)(2,1)} %gather_fusion, pred[4]{0:T(512)(128)(4,1)S(1)} %compare_and_fusion), kind=kOutput, calls=%fused_computation.2 | convolution fusion | flops 17189306368 | bytes 35651588 | tf_op jit(solution)/shard_map/pmi,rpki->mrk/dot_general | solution.py:97
  144.7 12.7 %shard_map.47 = bf16[1024,32,256]{2,1,0:T(8,128)(2,1)} custom-call(bf16[32,1024,256]{2,1,0:T(8,128)(2,1)} %fusion.in_ref), custom_call_target="tpu_custom_call" | custom-call | tf_op jit(solution)/shard_map/pallas_call | solution.py:105
  (3 shorter events, 0.0 us)
Async XLA Ops:
  6.5 114.0 %all-gather.3.cloned.1.call-start = ((), (), s32[]{:S(2)}) async-start(), calls=%async_computation.1 | async-start | bytes 17301504 | tf_op jit(solution)/shard_map/all_gather | solution.py:96
  6.5 11.0 %collective-permute-start = (bf16[1024,256]{1,0:T(8,128)(2,1)}, bf16[1024,256]{1,0:T(8,128)(2,1)S(1)}, u32[]{:S(2)}, u32[]{:S(2)}) collective-permute-start(bf16[1024,256]{1,0:T(8,128)(2,1)} %refs_5_.1), channel_id=1, source_target_pairs={{0,1},{1,2},{2,3},{3,4},{4,5},{5,6},{6,7},{7,8},{8,9},{9,10},{10,1... | collective-permute-start | bytes 1572872 | tf_op jit(solution)/shard_map/ppermute | solution.py:13
  11.1 10.7 %collective-permute-start.1 = (bf16[1024,256]{1,0:T(8,128)(2,1)}, bf16[1024,256]{1,0:T(8,128)(2,1)S(1)}, u32[]{:S(2)}, u32[]{:S(2)}) collective-permute-start(bf16[1024,256]{1,0:T(8,128)(2,1)} %refs_5_.1), channel_id=1, source_target_pairs={{1,0},{2,1},{3,2},{4,3},{5,4},{6,5},{7,6},{8,7},{9,8},{10,9},{11,1... | collective-permute-start | bytes 1572872 | tf_op jit(solution)/shard_map/ppermute | solution.py:14
  17.6 4.3 %copy-start = (bf16[1024,256]{1,0:T(8,128)(2,1)}, bf16[1024,256]{1,0:T(8,128)(2,1)S(1)}, u32[]{:S(2)}) copy-start(bf16[1024,256]{1,0:T(8,128)(2,1)S(1)} %collective-permute-done.refs_4_) | copy-start | bytes 1572868
  21.8 0.8 copy-start.1
  42.2 15.5 %collective-permute-start.4 = (bf16[1024,256]{1,0:T(8,128)(2,1)}, bf16[1024,256]{1,0:T(8,128)(2,1)S(1)}, u32[]{:S(2)}, u32[]{:S(2)}) collective-permute-start(bf16[1024,256]{1,0:T(8,128)(2,1)} %shard_map.46), channel_id=1, source_target_pairs={{0,96},{32,0},{64,32},{96,64},{1,97},{33,1},{65,33},{97,65},{2,98}... | collective-permute-start | bytes 1572872 | tf_op jit(solution)/shard_map/ppermute | solution.py:90
  44.0 15.4 %collective-permute-start.3 = (bf16[1024,256]{1,0:T(8,128)(2,1)}, bf16[1024,256]{1,0:T(8,128)(2,1)S(1)}, u32[]{:S(2)}, u32[]{:S(2)}) collective-permute-start(bf16[1024,256]{1,0:T(8,128)(2,1)} %shard_map.46), channel_id=1, source_target_pairs={{0,64},{32,96},{64,0},{96,32},{1,65},{33,97},{65,1},{97,33},{2,66}... | collective-permute-start | bytes 1572872 | tf_op jit(solution)/shard_map/ppermute | solution.py:90
  46.8 18.5 %collective-permute-start.2 = (bf16[1024,256]{1,0:T(8,128)(2,1)}, bf16[1024,256]{1,0:T(8,128)(2,1)S(1)}, u32[]{:S(2)}, u32[]{:S(2)}) collective-permute-start(bf16[1024,256]{1,0:T(8,128)(2,1)} %shard_map.46), channel_id=1, source_target_pairs={{0,32},{32,64},{64,96},{96,0},{1,33},{33,65},{65,97},{97,1},{2,34}... | collective-permute-start | bytes 1572872 | tf_op jit(solution)/shard_map/ppermute | solution.py:90
  65.3 0.8 copy-start.2
Sparse Core Ops, SparseCore 0:
  42.3 78.2 all-gather.2
